TPU v7x, 32 devices: a whole 2x2x4 slice. The times are simulated.
32 devices in a mesh: dp: 4 (over y, core), freq: 8 (over z, x).
Axes of the slice: x: 2, y: 2, z: 4, core: 2. Of those that a mesh axis runs over, the one named last changes fastest.
Arguments:
- grad_parts: float32 [4, 27, 4, 65536], P('dp', None, None, 'freq'), may hold values from -12 to 12
- kernel: float32 [27, 262144], P(None, ('dp', 'freq')), may hold values from -4 to 4
Outputs:
- clipped: float32 [27, 262144], P(None, ('dp', 'freq'))
All inputs are finite; a program needn't handle non-finite values.
Results may differ from a plain program's by a relative error of at most 0.0005.
The roundings to bfloat16 on the way count: a program that leaves them out, or rounds other values in their place, can miss the bound.
Values may be sent and summed in bfloat16 or wider, within the bound.
No kernel may reach another device: no remote copies, remote signals or barrier semaphores. Data moves between devices by JAX's collectives and lax.ppermute only.
A program may use at most 64 MiB of HBM per device.

v0:
```python
import math

import jax
import jax.numpy as jnp
from jax import lax
from jax.sharding import PartitionSpec as P

C = 512
TAPS = 27
GT = 8
GH = 32
GW = 32
KD = 2


CLIP = 0.25
HIGH = lax.Precision.HIGHEST


def tap_phases(freq_ids, stride):
    flat_index = freq_ids * stride
    freq_time = flat_index // (GH * GW)
    freq_row = flat_index // GW % GH
    freq_col = flat_index % GW
    taps = jnp.arange(TAPS, dtype=jnp.int32)
    off_time = taps // 9 - 1
    off_row = taps // 3 % 3 - 1
    off_col = taps % 3 - 1
    period = GT * GH * GW
    turns = (
        freq_time[:, None] * off_time[None, :] * (GH * GW)
        + freq_row[:, None] * off_row[None, :] * (GT * GW)
        + freq_col[:, None] * off_col[None, :] * (GT * GH)
    ) % period
    angle = turns.astype(jnp.float32) * (2.0 * math.pi / period)
    return (jnp.cos(angle), jnp.sin(angle))


def clip_factor(local_square):
    summed = lax.psum(local_square, ("dp", "freq"))
    return jnp.minimum(1.0, CLIP * math.sqrt(TAPS * C * C) / jnp.sqrt(summed + 1e-06))


def spectrum(field, cosine, sine_rows):
    real_spec = jnp.dot(cosine, field, precision=HIGH)
    imag_spec = -jnp.dot(sine_rows, field, precision=HIGH)
    return jnp.stack([real_spec, imag_spec], axis=1)


def taps_back(polar_part, cosine, sine_rows):
    values = polar_part.astype(jnp.float32)
    summed = jnp.dot(cosine.T, values[:, 0], precision=HIGH)
    return summed - jnp.dot(sine_rows.T, values[:, 1], precision=HIGH)


def polar_step(spectra):
    width = spectra.shape[-1]
    mean_square = jnp.mean(jnp.square(spectra.astype(jnp.float32)), axis=(1, 2, 3), keepdims=True)
    spread = math.sqrt(8.0 * width)
    scaled = (
        spectra.astype(jnp.float32) * (0.75 / (spread * jnp.sqrt(mean_square + 1e-06)))
    ).astype(jnp.bfloat16)
    real_part = scaled[:, 0]
    imag_part = scaled[:, 1]
    stacked = jnp.concatenate([real_part, imag_part], axis=1)
    turned = jnp.concatenate([imag_part, -real_part], axis=1)
    gram = jnp.einsum(
        "nri,nrj->nij",
        stacked,
        jnp.concatenate([stacked, turned], axis=2),
        preferred_element_type=jnp.float32,
    ).astype(jnp.bfloat16)
    gram_real = gram[:, :, :width]
    gram_imag = gram[:, :, width:]
    blocked = jnp.concatenate([gram, jnp.concatenate([-gram_imag, gram_real], axis=2)], axis=1)
    side = jnp.concatenate([real_part, imag_part], axis=2)
    product = jnp.einsum("nij,njk->nik", side, blocked, preferred_element_type=jnp.float32)
    result = (1.5 * side.astype(jnp.float32) - 0.5 * product).astype(jnp.bfloat16)
    return jnp.stack([result[:, :, :width], result[:, :, width:]], axis=1)


def on_device(grad_parts, kernel):
    devices_dp = lax.axis_size("dp")
    devices_freq = lax.axis_size("freq")
    total_freq = KD * devices_dp * devices_freq
    stride = GT * GH * GW // total_freq
    scale_out = math.sqrt(C / total_freq)
    own_width = kernel.shape[1]
    gradient = lax.psum_scatter(grad_parts[0], "dp", scatter_dimension=1, tiled=True).reshape(
        TAPS, own_width
    )
    local_square = jnp.sum(gradient * gradient)
    kernel_all, gradient_all = (kernel, gradient)
    freq_ids = jnp.arange(total_freq, dtype=jnp.int32)
    cosine, sine_rows = tap_phases(freq_ids, stride)
    factor = clip_factor(local_square)
    spectra = spectrum(kernel_all - factor * gradient_all, cosine, sine_rows)
    spectra = spectra.astype(jnp.bfloat16)
    count, row_width = (spectra.shape[0], spectra.shape[2])
    whole = lax.all_to_all(
        lax.all_to_all(
            spectra.reshape(count, 2, 1, 1, row_width),
            "dp",
            split_axis=0,
            concat_axis=2,
            tiled=True,
        ),
        "freq",
        split_axis=0,
        concat_axis=3,
        tiled=True,
    )
    polar_part = polar_step(whole.reshape(KD, 2, C, C))
    returned = lax.all_to_all(
        lax.all_to_all(
            polar_part.reshape(KD, 2, devices_dp, devices_freq, row_width),
            "dp",
            split_axis=2,
            concat_axis=0,
            tiled=True,
        ),
        "freq",
        split_axis=3,
        concat_axis=0,
        tiled=True,
    )
    position = jnp.arange(total_freq, dtype=jnp.int32)
    source_freq = position // (devices_dp * KD)
    source_dp = position // KD % devices_dp
    member = position % KD
    back_ids = source_dp * (devices_freq * KD) + source_freq * KD + member
    back_cos, back_sin = tap_phases(back_ids, stride)
    return taps_back(returned.reshape(count, 2, row_width), back_cos, back_sin) * scale_out


def solution(mesh):
    return jax.shard_map(
        on_device,
        mesh=mesh,
        in_specs=(P("dp", None, None, "freq"), P(None, ("dp", "freq"))),
        out_specs=P(None, ("dp", "freq")),
        check_vma=False,
    )
```

profile of v0, /device:TPU:0, one launch (start us, length us, event | category | flops | bytes accessed | tf_op | source)
XLA Modules:
  0.0 307.9 jit_solution(1594015570563499403)
XLA Ops:
  6.5 0.0 reduce-scatter.2.cloned.1.call-start
  6.5 6.0 %copy.47 = f32[1,27,4,8192]{3,1,2,0:T(8,128)} copy(f32[1,27,4,8192]{3,2,1,0:T(4,128)} %param.2) | data formatting | bytes 7077888 | tf_op args[0]
  12.5 0.0 copy-start.1
  12.5 0.0 reduce-scatter.2.cloned.1.call-update
  12.6 47.3 %reduce-scatter.2.cloned.1.call-done = f32[27,1,8192]{2,0,1:T(8,128)} async-done(((f32[27,4,8192]{2,0,1:T(8,128)}), f32[27,1,8192]{2,0,1:T(8,128)}) %reduce-scatter.2.cloned.1.call-update) | async-done | bytes 884752 | tf_op jit(solution)/shard_map/reduce_scatter | solution.py:89
  59.9 0.0 copy-start
  59.9 2.2 multiply_reduce_fusion.1
  62.1 39.5 %psum.7 = f32[]{:T(128)} all-reduce(f32[]{:T(128)} %multiply_reduce_fusion.1), channel_id=1, replica_groups=mesh['dp'=4,'freq'=8] {'dp','freq'}, use_global_device_ids=true, to_apply=%region_2.3 | all-reduce | flops 1 | bytes 8 | tf_op jit(solution)/shard_map/psum | solution.py:40
  102.3 0.0 copy-done.1
  102.3 3.2 %fusion.2 = bf16[64,1,1,1,8192]{4,0,3,2,1:T(8,128)(2,1)S(1)} fusion(f32[27,8192]{1,0:T(8,128)S(1)} %copy-done.1, f32[27,1,8192]{2,0,1:T(8,128)} %reduce-scatter.2.cloned.1.call-done, f32[]{:T(128)S(6)} %min_shard_map.3, s32[64]{0:T(128)S(1)} %get-tuple-element.11, s32[64]{0:T(128)S(1)} %get-tuple-element.12, s32[64]{0:T(128)S(1)} %and_select_fusion.3, ...), kind=kOutput, calls=%fused_computation.4 | convolution fusion | flops 171396544 | bytes 2819144 | tf_op jit(solution)/shard_map/dot_general | solution.py:46
  105.6 0.0 copy-done
  105.6 2.0 fusion.1
  107.6 0.2 pad_maximum_fusion
  107.8 2.2 copy.32
  110.0 29.2 %all_to_all.60 = bf16[64,2,1,1,8192]{4,1,3,2,0:T(2,128)(2,1)S(1)} all-to-all(bf16[64,2,1,1,8192]{4,1,3,2,0:T(2,128)(2,1)S(1)} %copy.32), channel_id=1, replica_groups=mesh['dp'=4,'freq'=8] {'dp'}, dimensions={0} | all-to-all | bytes 4194304 | tf_op jit(solution)/shard_map/all_to_all | solution.py:101
  139.2 1.2 copy.33
  140.4 1.6 copy.34
  142.0 52.3 %all_to_all.61 = bf16[16,2,4,1,8192]{4,2,1,3,0:T(4,128)(2,1)S(1)} all-to-all(bf16[16,2,4,1,8192]{4,2,1,3,0:T(4,128)(2,1)S(1)} %copy.34), channel_id=1, replica_groups=mesh['dp'=4,'freq'=8] {'freq'}, dimensions={0} | all-to-all | bytes 4194304 | tf_op jit(solution)/shard_map/all_to_all | solution.py:100
  194.3 1.2 multiply_reduce_fusion
  195.6 0.1 reduce_sum.27
  195.7 3.2 %copy.46 = f32[8,2,2,4,1,8192]{5,0,3,1,2,4:T(8,128)} copy(bf16[8,2,2,4,1,8192]{5,3,2,1,0,4:T(4,128)(2,1)S(1)} %bitcast.49) | data formatting | bytes 6291456 | tf_op jit(solution)/shard_map/convert_element_type | solution.py:61
  198.8 5.0 %reshape.259 = f32[2,2,512,512]{3,2,0,1:T(8,128)} reshape(f32[2,2,4,8,1,8192]{5,3,2,0,1,4:T(8,128)} %bitcast.50) | data formatting | bytes 8388608 | tf_op jit(solution)/shard_map/convert_element_type | solution.py:61
  203.8 2.8 multiply_convert_fusion
  206.6 0.1 fusion.83
  206.7 0.1 slice_bitcast_fusion.5
  206.9 2.6 fusion.23
  209.5 0.1 slice_negate_fusion
  209.6 2.6 subtract_convert_fusion
  212.2 0.2 fusion.84
  212.4 0.5 stack.21
  212.9 0.5 stack.22
  213.5 0.2 pad_maximum_fusion.2
  213.7 0.2 copy.42
  213.9 28.2 %all_to_all.62 = bf16[2,2,4,8,8192]{4,3,1,0,2:T(8,128)(2,1)S(1)} all-to-all(bf16[2,2,4,8,8192]{4,3,1,0,2:T(8,128)(2,1)S(1)} %copy.42), channel_id=1, replica_groups=mesh['dp'=4,'freq'=8] {'dp'}, dimensions={2} | all-to-all | bytes 4194304 | tf_op jit(solution)/shard_map/all_to_all | solution.py:115
  242.0 3.5 %copy.39 = bf16[8,2,1,8,8192]{4,1,0,2,3:T(2,128)(2,1)} copy(bf16[8,2,1,8,8192]{4,3,1,0,2:T(8,128)(2,1)S(1)} %bitcast.55) | data formatting | bytes 4194304 | tf_op jit(solution)/shard_map/all_to_all | solution.py:115
  245.6 3.6 %all-to-all-start.3 = ((bf16[8,2,1,8,8192]{4,1,0,2,3:T(2,128)(2,1)}), bf16[8,2,1,8,8192]{4,1,0,2,3:T(2,128)(2,1)S(1)}, u32[]{:S(2)}, u32[]{:S(2)}) async-start(bf16[8,2,1,8,8192]{4,1,0,2,3:T(2,128)(2,1)} %copy.39), calls=%async_computation.4 | async-start | bytes 4194304 | tf_op jit(solution)/shard_map/all_to_all | solution.py:114
  249.2 48.0 %all-to-all-done.3 = bf16[8,2,1,8,8192]{4,1,0,2,3:T(2,128)(2,1)S(1)} async-done(((bf16[8,2,1,8,8192]{4,1,0,2,3:T(2,128)(2,1)}), bf16[8,2,1,8,8192]{4,1,0,2,3:T(2,128)(2,1)S(1)}, u32[]{:S(2)}, u32[]{:S(2)}) %all-to-all-start.3) | async-done | bytes 2097184 | tf_op jit(solution)/shard_map/all_to_all | solution.py:114
  297.2 1.2 copy.48
  298.4 0.8 fusion.28
  299.2 1.8 fusion.3
  (8 shorter events, 0.1 us)
Async XLA Ops:
  6.5 53.4 %reduce-scatter.2.cloned.1.call-start = ((), (), s32[]{:S(2)}) async-start(), calls=%async_computation.5 | async-start | bytes 5242880 | tf_op jit(solution)/shard_map/reduce_scatter | solution.py:89
  12.5 89.8 %copy-start.1 = (f32[27,8192]{1,0:T(8,128)S(1)}, f32[27,8192]{1,0:T(8,128)}, u32[]{:S(2)}) copy-start(f32[27,8192]{1,0:T(8,128)} %param.3) | copy-start | bytes 2654212
  59.9 45.7 %copy-start = (f32[27,1,8192]{2,0,1:T(8,128)S(1)}, f32[27,1,8192]{2,0,1:T(8,128)}, u32[]{:S(2)}) copy-start(f32[27,1,8192]{2,0,1:T(8,128)} %reduce-scatter.2.cloned.1.call-done) | copy-start | bytes 2654212
  245.6 51.7 %all-to-all-start.3 = ((bf16[8,2,1,8,8192]{4,1,0,2,3:T(2,128)(2,1)}), bf16[8,2,1,8,8192]{4,1,0,2,3:T(2,128)(2,1)S(1)}, u32[]{:S(2)}, u32[]{:S(2)}) async-start(bf16[8,2,1,8,8192]{4,1,0,2,3:T(2,128)(2,1)} %copy.39), calls=%async_computation.4 | async-start | bytes 4194304 | tf_op jit(solution)/shard_map/all_to_all | solution.py:114
Sparse Core Ops, SparseCore 0:
  12.7 47.2 reduce-scatter.1
where the time goes:
time: 308 us
  blocking collectives  149 us (48%)
  waiting for transfers between devices  95.4 us (31%)
  local copies, waits for them, and re-layouts  25.4 us (8%)
  between operations  14.3 us (5%)
  matrix products  13 us (4%)
  other arithmetic  6.98 us (2%)
  starting transfers between devices  3.6 us (1%)
    all_to_all x1, blocking collectives, on_device(): lax.all_to_all(lax.all_to_all(spectra.reshape(count, 2, 1, 1, row_width),...  52.3 us
    all_to_all x1, waiting for transfers between devices, on_device(): lax.all_to_all(lax.all_to_all(polar_part.reshape(KD, 2, devices_dp, devic...  48 us
    reduce_scatter x1, waiting for transfers between devices, on_device(): lax.psum_scatter(grad_parts[0], 'dp', scatter_dimension=1, tiled=True)  47.3 us
    psum x1, blocking collectives, clip_factor(): summed = lax.psum(local_square, ('dp', 'freq'))  39.5 us
    all_to_all x1, blocking collectives, on_device(): lax.all_to_all(spectra.reshape(count, 2, 1, 1, row_width), 'dp', split_ax...  29.2 us
    all_to_all x1, blocking collectives, on_device(): lax.all_to_all(polar_part.reshape(KD, 2, devices_dp, devices_freq, row_wi...  28.2 us
    convert_element_type x2, local copies, waits for them, and re-layouts, polar_step(): spectra.astype(jnp.float32)  8.14 us
  transfers between devices with their start and end apart: 2, of which 2 were waited for; matrix products, arithmetic and copies ran while one was open for 0% of the time, Pallas kernels for 0%

commit v1 on v0

v1 whole, which is shorter than its diff:
```python
import math

import numpy as np

import jax
import jax.numpy as jnp
from jax import lax
from jax.sharding import PartitionSpec as P

C = 512
TAPS = 27
GT = 8
GH = 32
GW = 32
KD = 2

CLIP = 0.25
HIGH = lax.Precision.HIGHEST
AXES = ("dp", "freq")


def grid_point(freq_ids, stride):
    flat_index = freq_ids * stride
    return flat_index // (GH * GW), flat_index // GW % GH, flat_index % GW


def turns_of(freq_ids, stride):
    freq_time, freq_row, freq_col = grid_point(freq_ids, stride)
    taps = np.arange(TAPS)
    off_time = taps // 9 - 1
    off_row = taps // 3 % 3 - 1
    off_col = taps % 3 - 1
    period = GT * GH * GW
    return (
        freq_time[:, None] * off_time[None, :] * (GH * GW)
        + freq_row[:, None] * off_row[None, :] * (GT * GW)
        + freq_col[:, None] * off_col[None, :] * (GT * GH)
    ) % period


def slot_plan(total_freq, stride):
    ids = np.arange(total_freq)
    freq_time, freq_row, freq_col = grid_point(ids, stride)
    key = {(int(a), int(b), int(c)): j for j, (a, b, c) in enumerate(zip(freq_time, freq_row, freq_col))}
    pairs, selfs, seen = [], [], set()
    for j in range(total_freq):
        if j in seen:
            continue
        mate = key[(int(-freq_time[j] % GT), int(-freq_row[j] % GH), int(-freq_col[j] % GW))]
        seen.update((j, mate))
        if mate == j:
            selfs.append(j)
        else:
            pairs.append(j)
    assert len(selfs) % 2 == 0
    period = GT * GH * GW
    angle = turns_of(ids, stride).astype(np.float64) * (2.0 * math.pi / period)
    cosine, sine = np.cos(angle), np.sin(angle)
    forward, backward, kinds = [], [], []
    for j in pairs:
        forward += [cosine[j], -sine[j]]
        backward += [2.0 * cosine[j], -2.0 * sine[j]]
        kinds.append(1)
    for k in range(0, len(selfs), 2):
        a, b = selfs[k], selfs[k + 1]
        forward += [np.round(cosine[a]), np.round(cosine[b])]
        backward += [np.round(cosine[a]), np.round(cosine[b])]
        kinds.append(0)
    forward = np.stack(forward).astype(np.float32)
    backward = np.stack(backward).T.astype(np.float32)
    return forward, backward, np.array(kinds, np.int32)


def polar_complex(values):
    width = values.shape[-1]
    vals = values.astype(jnp.float32)
    mean_square = jnp.sum(vals * vals) / (2 * width * width)
    scale = 0.75 / (math.sqrt(8.0 * width) * jnp.sqrt(mean_square + 1e-06))
    scaled = (vals * scale).astype(jnp.bfloat16)
    real_part, imag_part = scaled[0], scaled[1]
    stacked = jnp.concatenate([real_part, imag_part], axis=0)
    turned = jnp.concatenate([imag_part, -real_part], axis=0)
    gram = jnp.dot(
        stacked.T, jnp.concatenate([stacked, turned], axis=1), preferred_element_type=jnp.float32
    ).astype(jnp.bfloat16)
    gram_real = gram[:, :width]
    gram_imag = gram[:, width:]
    blocked = jnp.concatenate([gram, jnp.concatenate([-gram_imag, gram_real], axis=1)], axis=0)
    side = jnp.concatenate([real_part, imag_part], axis=1)
    product = jnp.dot(side, blocked, preferred_element_type=jnp.float32)
    result = (1.5 * side.astype(jnp.float32) - 0.5 * product).astype(jnp.bfloat16)
    return jnp.stack([result[:, :width], result[:, width:]], axis=0)


def polar_real(values):
    width = values.shape[-1]
    vals = values.astype(jnp.float32)
    mean_square = jnp.sum(vals * vals, axis=(1, 2), keepdims=True) / (2 * width * width)
    scale = 0.75 / (math.sqrt(8.0 * width) * jnp.sqrt(mean_square + 1e-06))
    scaled = (vals * scale).astype(jnp.bfloat16)
    gram = jnp.einsum("nri,nrj->nij", scaled, scaled, preferred_element_type=jnp.float32).astype(
        jnp.bfloat16
    )
    product = jnp.einsum("nij,njk->nik", scaled, gram, preferred_element_type=jnp.float32)
    return (1.5 * scaled.astype(jnp.float32) - 0.5 * product).astype(jnp.bfloat16)


def on_device(grad_parts, kernel):
    devices_dp = lax.axis_size("dp")
    devices_freq = lax.axis_size("freq")
    devices = devices_dp * devices_freq
    total_freq = KD * devices
    stride = GT * GH * GW // total_freq
    scale_out = math.sqrt(C / total_freq)
    own_width = kernel.shape[1]
    forward, backward, kinds = slot_plan(total_freq, stride)

    gradient = lax.psum_scatter(grad_parts[0], "dp", scatter_dimension=1, tiled=True).reshape(
        TAPS, own_width
    )
    local_square = jnp.sum(gradient * gradient)
    summed = lax.psum(lax.psum(local_square, "freq"), "dp")
    factor = jnp.minimum(1.0, CLIP * math.sqrt(TAPS * C * C) / jnp.sqrt(summed + 1e-06))
    updated = kernel - factor * gradient

    spectra = jnp.dot(jnp.asarray(forward), updated, precision=HIGH).astype(jnp.bfloat16)
    sent = spectra.reshape(devices, 2, own_width)
    whole = lax.all_to_all(sent, AXES, 0, 0, tiled=True)
    matrix = whole.transpose(1, 0, 2).reshape(2, C, C)

    me = lax.axis_index(AXES)
    is_pair = jnp.asarray(kinds)[me] == 1
    polar_part = lax.cond(is_pair, polar_complex, polar_real, matrix)

    back = polar_part.reshape(2, devices, own_width).transpose(1, 0, 2)
    returned = lax.all_to_all(back, AXES, 0, 0, tiled=True)
    planes = returned.reshape(2 * devices, own_width).astype(jnp.float32)
    return jnp.dot(jnp.asarray(backward), planes, precision=HIGH) * scale_out


def solution(mesh):
    return jax.shard_map(
        on_device,
        mesh=mesh,
        in_specs=(P("dp", None, None, "freq"), P(None, ("dp", "freq"))),
        out_specs=P(None, ("dp", "freq")),
        check_vma=False,
    )
```

time: 308 us -> 173 us (0.56)
  blocking collectives: 149 us -> 58.1 us
  waiting for transfers between devices: 95.4 us -> 73.6 us
  local copies, waits for them, and re-layouts: 25.4 us -> 11.4 us
  matrix products: 13 us -> 7.14 us
  other arithmetic: 6.98 us -> 3.64 us
    all_to_all x3 -> x1, blocking collectives: 110 us -> 29.6 us  [on_device(): returned = lax.all_to_all(back, AXES, 0, 0, tiled=True)]
    all_to_all x1, waiting for transfers between devices: 48 us -> 26.2 us  [on_device(): whole = lax.all_to_all(sent, AXES, 0, 0, tiled=True)]
    psum x1 -> x2, blocking collectives: 39.5 us -> 28.5 us  [on_device(): summed = lax.psum(lax.psum(local_square, 'freq'), 'dp')]
    convert_element_type x2 -> x0, local copies, waits for them, and re-layouts: 8.14 us -> none  [polar_step(): spectra.astype(jnp.float32)]
    all_to_all x4 -> x0, local copies, waits for them, and re-layouts: 7.47 us -> none  [the longest x1 3.53 us: on_device(): lax.all_to_all(polar_part.reshape(KD, 2, devices_dp, devices_freq, row_wi...]
    dot_general x6 -> x4, matrix products: 13 us -> 7.14 us  [the longest x1 3.05 us: on_device(): jnp.dot(jnp.asarray(forward), updated, precision=HIGH).astype(jnp.bfloat16)]
    reshape x0 -> x5, local copies, waits for them, and re-layouts: none -> 4.05 us  [the longest x2 1.61 us: on_device(): back = polar_part.reshape(2, devices, own_width).transpose(1, 0, 2)]
    another operation x4 -> x1, local copies, waits for them, and re-layouts: 3.42 us -> 0.07 us  [polar_complex(): return jnp.stack([result[:, :width], result[:, width:]], axis=0)]
where the time goes in v1:
time: 173 us; the launch traced here: 172 us
  waiting for transfers between devices  73.6 us (43%)
  blocking collectives  58.1 us (34%)
  between operations  14.9 us (9%)
  local copies, waits for them, and re-layouts  11.4 us (7%)
  matrix products  7.14 us (4%)
  other arithmetic  3.64 us (2%)
  starting transfers between devices  2.65 us (2%)
    reduce_scatter x1, waiting for transfers between devices, on_device(): lax.psum_scatter(grad_parts[0], 'dp', scatter_dimension=1, tiled=True)  47.4 us
    all_to_all x1, blocking collectives, on_device(): returned = lax.all_to_all(back, AXES, 0, 0, tiled=True)  29.6 us
    psum x2, blocking collectives, on_device(): summed = lax.psum(lax.psum(local_square, 'freq'), 'dp')  28.5 us
    all_to_all x1, waiting for transfers between devices, on_device(): whole = lax.all_to_all(sent, AXES, 0, 0, tiled=True)  26.2 us
    unnamed x9, local copies, waits for them, and re-layouts  6 us
  transfers between devices with their start and end apart: 2, of which 2 were waited for; matrix products, arithmetic and copies ran while one was open for 0% of the time, Pallas kernels for 0%

profile of v1, /device:TPU:0, one launch (start us, length us, event | category | flops | bytes accessed | tf_op | source)
XLA Modules:
  0.0 172.5 jit_solution(1577073857258737760)
XLA Ops:
  6.5 0.0 reduce-scatter.2.cloned.1.call-start
  6.5 6.0 %copy.13 = f32[1,27,4,8192]{3,1,2,0:T(8,128)} copy(f32[1,27,4,8192]{3,2,1,0:T(4,128)} %param.7) | data formatting | bytes 7077888 | tf_op args[0]
  12.5 0.0 copy-start
  12.5 0.0 copy-start.1
  12.5 0.0 reduce-scatter.2.cloned.1.call-update
  12.5 47.4 %reduce-scatter.2.cloned.1.call-done = f32[27,1,8192]{2,0,1:T(8,128)} async-done(((f32[27,4,8192]{2,0,1:T(8,128)}), f32[27,1,8192]{2,0,1:T(8,128)}) %reduce-scatter.2.cloned.1.call-update) | async-done | bytes 884752 | tf_op jit(solution)/shard_map/reduce_scatter | solution.py:118
  59.9 2.1 %multiply_reduce_fusion = f32[]{:T(128)} fusion(f32[27,1,8192]{2,0,1:T(8,128)} %reduce-scatter.2.cloned.1.call-done), kind=kLoop, calls=%fused_computation.51 | loop fusion | flops 442367 | bytes 884740 | tf_op jit(solution)/shard_map/reduce_sum | solution.py:121
  62.0 21.9 %psum.14 = f32[]{:T(128)} all-reduce(f32[]{:T(128)} %multiply_reduce_fusion), channel_id=1, replica_groups=mesh['dp'=4,'freq'=8] {'freq'}, use_global_device_ids=true, to_apply=%region_2.0 | all-reduce | flops 1 | bytes 8 | tf_op jit(solution)/shard_map/psum | solution.py:122
  84.0 6.6 %psum.15 = f32[]{:T(128)} all-reduce(f32[]{:T(128)} %psum.14), channel_id=1, replica_groups=mesh['dp'=4,'freq'=8] {'dp'}, use_global_device_ids=true, to_apply=%region_3.0 | all-reduce | flops 1 | bytes 8 | tf_op jit(solution)/shard_map/psum | solution.py:122
  91.2 0.0 copy-done
  91.2 0.0 copy-done.1
  91.3 3.0 %fusion.36 = bf16[64,8192]{1,0:T(8,128)(2,1)S(1)} fusion(f32[64,27]{1,0:T(8,128)S(1)} %copy-done.1, f32[27,8192]{1,0:T(8,128)S(1)} %copy-done, f32[27,1,8192]{2,0,1:T(8,128)} %reduce-scatter.2.cloned.1.call-done, f32[]{:T(128)S(6)} %min_shard_map.3), kind=kOutput, calls=%fused_computation.44 | convolution fusion | flops 170835968 | bytes 2824964 | tf_op jit(solution)/shard_map/dot_general | solution.py:126
  94.3 0.0 copy-start.3
  94.3 1.5 reshape.38
  95.8 2.6 %all-to-all-start = ((bf16[32,2,8192]{2,1,0:T(2,128)(2,1)}), bf16[32,2,8192]{2,1,0:T(2,128)(2,1)S(1)}, u32[]{:S(2)}, u32[]{:S(2)}) async-start(bf16[32,2,8192]{2,1,0:T(2,128)(2,1)} %reshape.38), calls=%async_computation.1 | async-start | bytes 2097152 | tf_op jit(solution)/shard_map/all_to_all | solution.py:128
  98.5 0.0 copy-done.3
  98.5 0.7 dynamic_slice.3
  99.9 26.2 %all-to-all-done = bf16[32,2,8192]{2,1,0:T(2,128)(2,1)S(1)} async-done(((bf16[32,2,8192]{2,1,0:T(2,128)(2,1)}), bf16[32,2,8192]{2,1,0:T(2,128)(2,1)S(1)}, u32[]{:S(2)}, u32[]{:S(2)}) %all-to-all-start) | async-done | bytes 1048608 | tf_op jit(solution)/shard_map/all_to_all | solution.py:128
  126.1 0.6 copy.9
  126.6 0.5 reshape.39
  127.2 5.2 %conditional.1 = (bf16[2,512,512]{2,1,0:T(8,128)(2,1)S(1)}) conditional(s32[]{:T(128)} %bitcast.4, bf16[2,512,512]{2,1,0:T(8,128)(2,1)S(1)} %reshape.39, bf16[2,512,512]{2,1,0:T(8,128)(2,1)S(1)} %reshape.39), branch_computations={%region_4.0_spmd, %region_6.0_spmd} | conditional | flops 2175270912 | bytes 19398728 | solution.py:133
  127.2 1.1 fusion.6
  129.1 0.2 fusion.7
  129.3 0.1 slice_bitcast_fusion.3
  129.4 1.3 fusion.24
  130.7 0.1 slice_negate_fusion
  130.8 1.3 subtract_convert_fusion.1
  132.0 0.1 slice_bitcast_fusion.1
  132.1 0.1 pad_maximum_fusion
  132.4 0.5 reshape.40
  133.0 1.1 copy.14
  134.0 0.0 copy-start.2
  134.1 29.6 %all_to_all.10 = bf16[32,2,8192]{2,1,0:T(2,128)(2,1)S(1)} all-to-all(bf16[32,2,8192]{2,1,0:T(2,128)(2,1)S(1)} %bitcast.30), channel_id=1, replica_groups=mesh['dp'=4,'freq'=8] {'dp','freq'}, dimensions={0} | all-to-all | bytes 2097152 | tf_op jit(solution)/shard_map/all_to_all | solution.py:136
  163.7 0.4 reshape.41
  164.1 0.0 copy-done.2
  164.1 1.5 fusion.37
  (1 shorter events, 0.0 us)
Async XLA Ops:
  6.5 53.4 %reduce-scatter.2.cloned.1.call-start = ((), (), s32[]{:S(2)}) async-start(), calls=%async_computation.3 | async-start | bytes 5242880 | tf_op jit(solution)/shard_map/reduce_scatter | solution.py:118
  12.5 78.7 %copy-start = (f32[27,8192]{1,0:T(8,128)S(1)}, f32[27,8192]{1,0:T(8,128)}, u32[]{:S(2)}) copy-start(f32[27,8192]{1,0:T(8,128)} %param.8) | copy-start | bytes 2654212
  12.5 78.7 %copy-start.1 = (f32[64,27]{1,0:T(8,128)S(1)}, f32[64,27]{1,0:T(8,128)}, u32[]{:S(2)}) copy-start(f32[64,27]{1,0:T(8,128)} %constant.63.clone) | copy-start | bytes 20740
  94.3 4.2 %copy-start.3 = (s32[32]{0:T(128)S(1)}, s32[32]{0:T(128)}, u32[]{:S(2)}) copy-start(s32[32]{0:T(128)} %constant.64.clone) | copy-start | bytes 388
  95.8 30.2 %all-to-all-start = ((bf16[32,2,8192]{2,1,0:T(2,128)(2,1)}), bf16[32,2,8192]{2,1,0:T(2,128)(2,1)S(1)}, u32[]{:S(2)}, u32[]{:S(2)}) async-start(bf16[32,2,8192]{2,1,0:T(2,128)(2,1)} %reshape.38), calls=%async_computation.1 | async-start | bytes 2097152 | tf_op jit(solution)/shard_map/all_to_all | solution.py:128
  134.0 30.1 %copy-start.2 = (f32[27,64]{1,0:T(8,128)S(1)}, f32[27,64]{1,0:T(8,128)}, u32[]{:S(2)}) copy-start(f32[27,64]{1,0:T(8,128)} %constant.65.clone) | copy-start | bytes 20740
Sparse Core Ops, SparseCore 0:
  12.7 47.2 reduce-scatter.1

commit v2 on v1

--- a/solution.py
+++ b/solution.py
@@ -36,6 +36,25 @@
         + freq_row[:, None] * off_row[None, :] * (GT * GW)
         + freq_col[:, None] * off_col[None, :] * (GT * GH)
     ) % period
+
+
+def tap_phases(freq_ids, stride):
+    flat_index = freq_ids * stride
+    freq_time = flat_index // (GH * GW)
+    freq_row = flat_index // GW % GH
+    freq_col = flat_index % GW
+    taps = jnp.arange(TAPS, dtype=jnp.int32)
+    off_time = taps // 9 - 1
+    off_row = taps // 3 % 3 - 1
+    off_col = taps % 3 - 1
+    period = GT * GH * GW
+    turns = (
+        freq_time[:, None] * off_time[None, :] * (GH * GW)
+        + freq_row[:, None] * off_row[None, :] * (GT * GW)
+        + freq_col[:, None] * off_col[None, :] * (GT * GH)
+    ) % period
+    angle = turns.astype(jnp.float32) * (2.0 * math.pi / period)
+    return (jnp.cos(angle), jnp.sin(angle))
 
 
 def slot_plan(total_freq, stride):
@@ -58,15 +77,15 @@
     cosine, sine = np.cos(angle), np.sin(angle)
     forward, backward, kinds = [], [], []
     for j in pairs:
-        forward += [cosine[j], -sine[j]]
+        forward += [(j, 0), (j, 1)]
         backward += [2.0 * cosine[j], -2.0 * sine[j]]
         kinds.append(1)
     for k in range(0, len(selfs), 2):
         a, b = selfs[k], selfs[k + 1]
-        forward += [np.round(cosine[a]), np.round(cosine[b])]
+        forward += [(a, 0), (b, 0)]
         backward += [np.round(cosine[a]), np.round(cosine[b])]
         kinds.append(0)
-    forward = np.stack(forward).astype(np.float32)
+    forward = np.array(forward, np.int32)
     backward = np.stack(backward).T.astype(np.float32)
     return forward, backward, np.array(kinds, np.int32)
 
@@ -105,6 +124,45 @@
     return (1.5 * scaled.astype(jnp.float32) - 0.5 * product).astype(jnp.bfloat16)
 
 
+def reduce_over_dp(grad_parts, own_width):
+    devices_dp = lax.axis_size("dp")
+    if devices_dp % 2:
+        return lax.psum_scatter(grad_parts[0], "dp", scatter_dimension=1, tiled=True).reshape(
+            TAPS, own_width
+        )
+    d = lax.axis_index("dp")
+    core = d % 2
+    chips = devices_dp // 2
+    parts = grad_parts[0].reshape(TAPS, chips, 2, own_width)
+    send = lax.dynamic_index_in_dim(parts, 1 - core, axis=2, keepdims=False)
+    keep = lax.dynamic_index_in_dim(parts, core, axis=2, keepdims=False)
+    pair = [(i, i ^ 1) for i in range(devices_dp)]
+    halves = keep + lax.ppermute(send, "dp", pair)
+    if chips == 1:
+        return halves.reshape(TAPS, own_width)
+    chip = d // 2
+    blocks = halves
+    width = chips
+    level = 1
+    while width > 1:
+        width //= 2
+        bit = (chip // width) % 2
+        split = blocks.reshape(TAPS, 2, width, own_width)
+        mine = lax.dynamic_index_in_dim(split, bit, axis=1, keepdims=False)
+        other = lax.dynamic_index_in_dim(split, 1 - bit, axis=1, keepdims=False)
+        stride = 2 * width
+        partner = [(i, i ^ stride) for i in range(devices_dp)]
+        blocks = mine + lax.ppermute(other, "dp", partner)
+        level += 1
+    return blocks.reshape(TAPS, own_width)
+
+
+def total_over_devices(value, devices):
+    spread = jnp.broadcast_to(value, (devices, 1))
+    gathered = lax.all_to_all(spread, AXES, 0, 0, tiled=True)
+    return jnp.sum(gathered)
+
+
 def on_device(grad_parts, kernel):
     devices_dp = lax.axis_size("dp")
     devices_freq = lax.axis_size("freq")
@@ -113,17 +171,17 @@
     stride = GT * GH * GW // total_freq
     scale_out = math.sqrt(C / total_freq)
     own_width = kernel.shape[1]
-    forward, backward, kinds = slot_plan(total_freq, stride)
-
-    gradient = lax.psum_scatter(grad_parts[0], "dp", scatter_dimension=1, tiled=True).reshape(
-        TAPS, own_width
-    )
+    rows, backward, kinds = slot_plan(total_freq, stride)
+
+    gradient = reduce_over_dp(grad_parts, own_width)
     local_square = jnp.sum(gradient * gradient)
-    summed = lax.psum(lax.psum(local_square, "freq"), "dp")
+    summed = total_over_devices(local_square, devices)
     factor = jnp.minimum(1.0, CLIP * math.sqrt(TAPS * C * C) / jnp.sqrt(summed + 1e-06))
     updated = kernel - factor * gradient
 
-    spectra = jnp.dot(jnp.asarray(forward), updated, precision=HIGH).astype(jnp.bfloat16)
+    cosine, sine = tap_phases(jnp.asarray(rows[:, 0]), stride)
+    forward = jnp.where(jnp.asarray(rows[:, 1] == 0)[:, None], cosine, -sine)
+    spectra = jnp.dot(forward, updated, precision=HIGH).astype(jnp.bfloat16)
     sent = spectra.reshape(devices, 2, own_width)
     whole = lax.all_to_all(sent, AXES, 0, 0, tiled=True)
     matrix = whole.transpose(1, 0, 2).reshape(2, C, C)

time: 173 us -> 135 us (0.78)
  blocking collectives: 58.1 us -> 29.6 us
  waiting for transfers between devices: 73.6 us -> 56.8 us
  between operations: 14.9 us -> 1.45 us
  starting transfers between devices: 2.65 us -> 12.2 us
  local copies, waits for them, and re-layouts: 11.4 us -> 18.4 us
  other arithmetic: 3.64 us -> 9.06 us
    reduce_scatter x1 -> x0, waiting for transfers between devices: 47.4 us -> none  [on_device(): lax.psum_scatter(grad_parts[0], 'dp', scatter_dimension=1, tiled=True)]
    psum x2 -> x0, blocking collectives: 28.5 us -> none  [on_device(): summed = lax.psum(lax.psum(local_square, 'freq'), 'dp')]
    ppermute x0 -> x2, waiting for transfers between devices: none -> 23.4 us  [the longest x1 19.9 us: reduce_over_dp(): blocks = mine + lax.ppermute(other, 'dp', partner)]
    all_to_all x0 -> x1, waiting for transfers between devices: none -> 7.02 us  [total_over_devices(): gathered = lax.all_to_all(spread, AXES, 0, 0, tiled=True)]
    all_to_all x0 -> x1, starting transfers between devices: none -> 6.07 us  [total_over_devices(): gathered = lax.all_to_all(spread, AXES, 0, 0, tiled=True)]
    dynamic_slice x0 -> x1, local copies, waits for them, and re-layouts: none -> 4.94 us  [reduce_over_dp(): keep = lax.dynamic_index_in_dim(parts, core, axis=2, keepdims=False)]
    unnamed x9 -> x15, local copies, waits for them, and re-layouts: 6 us -> 1.47 us
    another operation x0 -> x1, local copies, waits for them, and re-layouts: none -> 4.49 us  [reduce_over_dp(): parts = grad_parts[0].reshape(TAPS, chips, 2, own_width)]
  transfers between devices with their start and end apart: 2 -> 4, of which waited for: 2 -> 4; matrix products, arithmetic and copies ran while one was open for 0% -> 0% of each run, Pallas kernels for 0% -> 0%
where the time goes in v2:
time: 135 us
  waiting for transfers between devices  56.8 us (42%)
  blocking collectives  29.6 us (22%)
  local copies, waits for them, and re-layouts  18.4 us (14%)
  starting transfers between devices  12.2 us (9%)
  other arithmetic  9.06 us (7%)
  matrix products  6.54 us (5%)
  between operations  1.45 us (1%)
    all_to_all x1, blocking collectives, on_device(): returned = lax.all_to_all(back, AXES, 0, 0, tiled=True)  29.6 us
    all_to_all x1, waiting for transfers between devices, on_device(): whole = lax.all_to_all(sent, AXES, 0, 0, tiled=True)  26.4 us
    ppermute x1, waiting for transfers between devices, reduce_over_dp(): blocks = mine + lax.ppermute(other, 'dp', partner)  19.9 us
    all_to_all x1, waiting for transfers between devices, total_over_devices(): gathered = lax.all_to_all(spread, AXES, 0, 0, tiled=True)  7.02 us
    all_to_all x1, starting transfers between devices, total_over_devices(): gathered = lax.all_to_all(spread, AXES, 0, 0, tiled=True)  6.07 us
    dynamic_slice x1, local copies, waits for them, and re-layouts, reduce_over_dp(): keep = lax.dynamic_index_in_dim(parts, core, axis=2, keepdims=False)  4.94 us
    another operation x1, local copies, waits for them, and re-layouts, reduce_over_dp(): parts = grad_parts[0].reshape(TAPS, chips, 2, own_width)  4.49 us
    ppermute x1, waiting for transfers between devices, reduce_over_dp(): halves = keep + lax.ppermute(send, 'dp', pair)  3.45 us
  transfers between devices with their start and end apart: 4, of which 4 were waited for; matrix products, arithmetic and copies ran while one was open for 0% of the time, Pallas kernels for 0%

profile of v2, /device:TPU:0, one launch (start us, length us, event | category | flops | bytes accessed | tf_op | source)
XLA Modules:
  0.0 134.9 jit_solution(16284759115566230394)
XLA Ops:
  0.0 4.5 %reshape_squeeze.3 = f32[27,2,2,8192]{3,2,1,0:T(2,128)S(1)} reshape(f32[1,27,4,8192]{3,2,1,0:T(4,128)} %param.8) | data formatting | bytes 7077888 | tf_op jit(solution)/shard_map/reshape;squeeze | solution.py:136
  4.5 4.9 %constant_dynamic-slice_fusion.1 = (f32[27,2,1,8192]{3,2,1,0:T(1,128)}, f32[27,2,1,8192]{3,2,1,0:T(1,128)S(1)}) fusion(f32[27,2,2,8192]{3,2,1,0:T(2,128)S(1)} %reshape_squeeze.3, s32[]{:T(128)S(6)} %select_n.107, s32[]{:T(128)S(6)} %select_n.108), kind=kLoop, calls=%fused_computation.86 | loop fusion | bytes 7077896 | tf_op jit(solution)/shard_map/jit(dynamic_index_in_dim)/dynamic_slice | solution.py:138
  9.4 0.0 copy-start
  9.4 1.4 %copy.44 = f32[27,2,1,8192]{3,1,0,2:T(2,128)S(1)} copy(f32[27,2,1,8192]{3,2,1,0:T(1,128)S(1)} %get-tuple-element.17) | data formatting | bytes 3538944
  10.8 0.5 collective-permute-start
  11.4 3.4 %collective-permute-done = f32[27,2,8192]{2,1,0:T(2,128)} collective-permute-done((f32[27,2,8192]{2,1,0:T(2,128)S(1)}, f32[27,2,8192]{2,1,0:T(2,128)}, u32[]{:S(2)}, u32[]{:S(2)}) %collective-permute-start) | collective-permute-done | bytes 1769504 | tf_op jit(solution)/shard_map/ppermute | solution.py:140
  14.8 0.0 copy-done
  14.8 3.3 %fusion.37 = f32[27,2,8192]{2,1,0:T(2,128)S(1)} fusion(f32[27,2,8192]{2,1,0:T(2,128)} %collective-permute-done, f32[27,2,1,8192]{3,2,1,0:T(1,128)S(1)} %copy-done), kind=kLoop, calls=%fused_computation.48 | loop fusion | flops 442368 | bytes 5308416 | tf_op jit(solution)/shard_map/add | solution.py:140
  18.1 1.0 constant_dynamic-slice_fusion.2
  19.1 3.0 %collective-permute-start.1 = (f32[27,1,8192]{2,1,0:T(1,128)S(1)}, f32[27,1,8192]{2,1,0:T(1,128)S(1)}, u32[]{:S(2)}, u32[]{:S(2)}) collective-permute-start(f32[27,1,8192]{2,1,0:T(1,128)S(1)} %constant_dynamic-slice_fusion.2), channel_id=1, source_target_pairs={{0,16},{8,24},{16,0},{24,8},{1,17},{9,25},{17,1},{25,9},{2,18},{10... | collective-permute-start | bytes 2654216 | tf_op jit(solution)/shard_map/ppermute | solution.py:155
  22.1 0.0 copy-start.3
  22.1 0.0 copy-start.4
  22.1 0.0 copy-start.5
  22.1 19.9 %collective-permute-done.1 = f32[27,1,8192]{2,1,0:T(1,128)S(1)} collective-permute-done((f32[27,1,8192]{2,1,0:T(1,128)S(1)}, f32[27,1,8192]{2,1,0:T(1,128)S(1)}, u32[]{:S(2)}, u32[]{:S(2)}) %collective-permute-start.1) | collective-permute-done | bytes 884768 | tf_op jit(solution)/shard_map/ppermute | solution.py:155
  42.0 2.4 %multiply_reduce_fusion = f32[]{:T(128)} fusion(f32[27,1,8192]{2,1,0:T(1,128)S(1)} %collective-permute-done.1, f32[27,2,8192]{2,1,0:T(2,128)S(1)} %fusion.37, s32[]{:T(128)S(6)} %select_n.111), kind=kLoop, calls=%fused_computation.52 | loop fusion | flops 663551 | bytes 1769480 | tf_op jit(solution)/shard_map/reduce_sum | solution.py:177
  44.4 1.2 broadcast_in_dim.8
  45.6 6.1 %all-to-all-start = ((f32[32,1,1]{2,1,0:T(1,128)}), f32[32,1,1]{2,1,0:T(1,128)S(1)}, u32[]{:S(2)}, u32[]{:S(2)}) async-start(f32[32,1,1]{2,1,0:T(1,128)} %broadcast_in_dim.8), calls=%async_computation | async-start | bytes 32768 | tf_op jit(solution)/shard_map/all_to_all | solution.py:162
  51.7 7.0 %all-to-all-done = f32[32,1,1]{2,1,0:T(1,128)S(1)} async-done(((f32[32,1,1]{2,1,0:T(1,128)}), f32[32,1,1]{2,1,0:T(1,128)S(1)}, u32[]{:S(2)}, u32[]{:S(2)}) %all-to-all-start) | async-done | bytes 160 | tf_op jit(solution)/shard_map/all_to_all | solution.py:162
  58.7 0.6 reduce_sum.37
  60.0 0.0 copy-start.1
  60.0 1.1 broadcast_multiply_fusion
  61.2 0.0 copy-done.3
  61.2 0.0 copy-done.4
  61.2 0.0 copy-done.5
  61.2 0.1 copy-done.1
  61.3 2.4 %convolution_convert_fusion.1 = bf16[64,8192]{1,0:T(8,128)(2,1)S(1)} fusion(f32[27,8192]{1,0:T(8,128)S(1)} %copy-done.1, f32[27,1,8192]{2,1,0:T(1,128)S(1)} %broadcast_multiply_fusion, s32[27]{0:T(128)S(1)} %get-tuple-element.18, s32[64]{0:T(128)S(1)} %copy-done.3, s32[27]{0:T(128)S(1)} %get-tuple-element.19, s32[64]{0:T(128)S(1)} %copy-done.4, ...), kind=kOutput, calls=%fused_computation.43 | convolution fusion | flops 170649344 | bytes 2818840 | tf_op jit(solution)/shard_map/dot_general | solution.py:184
  63.7 0.0 copy-start.6
  63.7 1.5 %reshape.89 = bf16[32,2,8192]{2,1,0:T(2,128)(2,1)} reshape(bf16[64,8192]{1,0:T(8,128)(2,1)S(1)} %convolution_convert_fusion.1) | data formatting | bytes 2097152 | tf_op jit(solution)/shard_map/reshape | solution.py:185
  65.2 2.6 %all-to-all-start.1 = ((bf16[32,2,8192]{2,1,0:T(2,128)(2,1)}), bf16[32,2,8192]{2,1,0:T(2,128)(2,1)S(1)}, u32[]{:S(2)}, u32[]{:S(2)}) async-start(bf16[32,2,8192]{2,1,0:T(2,128)(2,1)} %reshape.89), calls=%async_computation.1 | async-start | bytes 2097152 | tf_op jit(solution)/shard_map/all_to_all | solution.py:186
  67.9 0.0 copy-done.6
  67.9 0.6 dynamic_slice.13
  69.0 26.4 %all-to-all-done.1 = bf16[32,2,8192]{2,1,0:T(2,128)(2,1)S(1)} async-done(((bf16[32,2,8192]{2,1,0:T(2,128)(2,1)}), bf16[32,2,8192]{2,1,0:T(2,128)(2,1)S(1)}, u32[]{:S(2)}, u32[]{:S(2)}) %all-to-all-start.1) | async-done | bytes 1048608 | tf_op jit(solution)/shard_map/all_to_all | solution.py:186
  95.5 0.6 copy.28
  96.1 0.5 reshape.90
  96.6 5.0 %conditional.1 = (bf16[2,512,512]{2,1,0:T(8,128)(2,1)S(1)}) conditional(s32[]{:T(128)} %bitcast.4, bf16[2,512,512]{2,1,0:T(8,128)(2,1)S(1)} %reshape.90, bf16[2,512,512]{2,1,0:T(8,128)(2,1)S(1)} %reshape.90), branch_computations={%region_2.4_spmd, %region_4.6_spmd} | conditional | flops 2175270912 | bytes 19398728 | solution.py:191
  96.6 1.1 fusion.6
  98.5 0.2 fusion.7
  98.7 0.1 slice_bitcast_fusion.3
  98.8 1.3 fusion.24
  100.1 0.1 slice_negate_fusion
  100.2 1.3 subtract_convert_fusion.1
  101.5 0.1 slice_bitcast_fusion.1
  101.5 0.1 pad_maximum_fusion
  101.6 0.5 reshape.91
  102.2 1.1 copy.45
  103.3 0.0 copy-start.2
  103.3 29.6 %all_to_all.16 = bf16[32,2,8192]{2,1,0:T(2,128)(2,1)S(1)} all-to-all(bf16[32,2,8192]{2,1,0:T(2,128)(2,1)S(1)} %bitcast.30), channel_id=1, replica_groups=mesh['dp'=4,'freq'=8] {'dp','freq'}, dimensions={0} | all-to-all | bytes 2097152 | tf_op jit(solution)/shard_map/all_to_all | solution.py:194
  132.9 0.4 reshape.92
  133.3 0.0 copy-done.2
  133.3 1.5 %fusion.36 = f32[27,8192]{1,0:T(8,128)} fusion(bf16[64,8192]{1,0:T(8,128)(2,1)S(1)} %reshape.92, f32[27,64]{1,0:T(8,128)S(1)} %copy-done.2), kind=kOutput, calls=%fused_computation.45 | convolution fusion | flops 170090496 | bytes 1940224 | tf_op jit(solution)/shard_map/dot_general | solution.py:196
  (2 shorter events, 0.1 us)
Async XLA Ops:
  9.4 5.4 %copy-start = (f32[27,2,1,8192]{3,2,1,0:T(1,128)S(1)}, f32[27,2,1,8192]{3,2,1,0:T(1,128)}, u32[]{:S(2)}) copy-start(f32[27,2,1,8192]{3,2,1,0:T(1,128)} %get-tuple-element.16) | copy-start | bytes 5308420
  10.8 4.0 %collective-permute-start = (f32[27,2,8192]{2,1,0:T(2,128)S(1)}, f32[27,2,8192]{2,1,0:T(2,128)}, u32[]{:S(2)}, u32[]{:S(2)}) collective-permute-start(f32[27,2,8192]{2,1,0:T(2,128)S(1)} %bitcast.31), channel_id=1, source_target_pairs={{0,8},{8,0},{16,24},{24,16},{1,9},{9,1},{17,25},{25,17},{2,10},{10... | collective-permute-start | bytes 5308424 | tf_op jit(solution)/shard_map/ppermute | solution.py:140
  19.1 22.9 %collective-permute-start.1 = (f32[27,1,8192]{2,1,0:T(1,128)S(1)}, f32[27,1,8192]{2,1,0:T(1,128)S(1)}, u32[]{:S(2)}, u32[]{:S(2)}) collective-permute-start(f32[27,1,8192]{2,1,0:T(1,128)S(1)} %constant_dynamic-slice_fusion.2), channel_id=1, source_target_pairs={{0,16},{8,24},{16,0},{24,8},{1,17},{9,25},{17,1},{25,9},{2,18},{10... | collective-permute-start | bytes 2654216 | tf_op jit(solution)/shard_map/ppermute | solution.py:155
  22.1 39.1 %copy-start.3 = (s32[64]{0:T(128)S(1)}, s32[64]{0:T(128)}, u32[]{:S(2)}) copy-start(s32[64]{0:T(128)} %constant.246) | copy-start | bytes 772
  22.1 39.1 %copy-start.4 = (s32[64]{0:T(128)S(1)}, s32[64]{0:T(128)}, u32[]{:S(2)}) copy-start(s32[64]{0:T(128)} %constant.225) | copy-start | bytes 772
  22.1 39.1 %copy-start.5 = (pred[64]{0:T(512)(128)(4,1)S(1)}, pred[64]{0:T(512)(128)(4,1)}, u32[]{:S(2)}) copy-start(pred[64]{0:T(512)(128)(4,1)} %constant.206.clone) | copy-start | bytes 196
  45.6 13.1 %all-to-all-start = ((f32[32,1,1]{2,1,0:T(1,128)}), f32[32,1,1]{2,1,0:T(1,128)S(1)}, u32[]{:S(2)}, u32[]{:S(2)}) async-start(f32[32,1,1]{2,1,0:T(1,128)} %broadcast_in_dim.8), calls=%async_computation | async-start | bytes 32768 | tf_op jit(solution)/shard_map/all_to_all | solution.py:162
  60.0 1.2 copy-start.1
  63.7 4.2 %copy-start.6 = (s32[32]{0:T(128)S(1)}, s32[32]{0:T(128)}, u32[]{:S(2)}) copy-start(s32[32]{0:T(128)} %constant.207.clone) | copy-start | bytes 388
  65.2 30.2 %all-to-all-start.1 = ((bf16[32,2,8192]{2,1,0:T(2,128)(2,1)}), bf16[32,2,8192]{2,1,0:T(2,128)(2,1)S(1)}, u32[]{:S(2)}, u32[]{:S(2)}) async-start(bf16[32,2,8192]{2,1,0:T(2,128)(2,1)} %reshape.89), calls=%async_computation.1 | async-start | bytes 2097152 | tf_op jit(solution)/shard_map/all_to_all | solution.py:186
  103.3 30.1 %copy-start.2 = (f32[27,64]{1,0:T(8,128)S(1)}, f32[27,64]{1,0:T(8,128)}, u32[]{:S(2)}) copy-start(f32[27,64]{1,0:T(8,128)} %constant.208.clone) | copy-start | bytes 20740

commit v3 on v2

--- a/solution.py
+++ b/solution.py
@@ -124,37 +124,40 @@
     return (1.5 * scaled.astype(jnp.float32) - 0.5 * product).astype(jnp.bfloat16)
 
 
-def reduce_over_dp(grad_parts, own_width):
+def reduce_over_dp(grad_parts, own_width, pieces=2):
     devices_dp = lax.axis_size("dp")
-    if devices_dp % 2:
+    if devices_dp % 2 or own_width % (128 * pieces):
         return lax.psum_scatter(grad_parts[0], "dp", scatter_dimension=1, tiled=True).reshape(
             TAPS, own_width
         )
     d = lax.axis_index("dp")
     core = d % 2
+    chip = d // 2
     chips = devices_dp // 2
-    parts = grad_parts[0].reshape(TAPS, chips, 2, own_width)
-    send = lax.dynamic_index_in_dim(parts, 1 - core, axis=2, keepdims=False)
-    keep = lax.dynamic_index_in_dim(parts, core, axis=2, keepdims=False)
+    parts = grad_parts[0]
+    piece = own_width // pieces
     pair = [(i, i ^ 1) for i in range(devices_dp)]
-    halves = keep + lax.ppermute(send, "dp", pair)
-    if chips == 1:
-        return halves.reshape(TAPS, own_width)
-    chip = d // 2
-    blocks = halves
-    width = chips
-    level = 1
-    while width > 1:
-        width //= 2
-        bit = (chip // width) % 2
-        split = blocks.reshape(TAPS, 2, width, own_width)
-        mine = lax.dynamic_index_in_dim(split, bit, axis=1, keepdims=False)
-        other = lax.dynamic_index_in_dim(split, 1 - bit, axis=1, keepdims=False)
-        stride = 2 * width
-        partner = [(i, i ^ stride) for i in range(devices_dp)]
-        blocks = mine + lax.ppermute(other, "dp", partner)
-        level += 1
-    return blocks.reshape(TAPS, own_width)
+    outs = []
+    for p in range(pieces):
+        cols = parts[:, :, p * piece:(p + 1) * piece]
+
+        def gather(c):
+            return jnp.stack(
+                [lax.dynamic_index_in_dim(cols, 2 * k + c, axis=1, keepdims=False) for k in range(chips)]
+            )
+
+        blocks = gather(core) + lax.ppermute(gather(1 - core), "dp", pair)
+        width = chips
+        while width > 1:
+            width //= 2
+            bit = (chip // width) % 2
+            split = blocks.reshape(2, width, TAPS, piece)
+            mine = lax.dynamic_index_in_dim(split, bit, axis=0, keepdims=False)
+            other = lax.dynamic_index_in_dim(split, 1 - bit, axis=0, keepdims=False)
+            partner = [(i, i ^ (2 * width)) for i in range(devices_dp)]
+            blocks = mine + lax.ppermute(other, "dp", partner)
+        outs.append(blocks.reshape(TAPS, piece))
+    return jnp.concatenate(outs, axis=1)
 
 
 def total_over_devices(value, devices):

time: 135 us -> 129 us (0.956)
  waiting for transfers between devices: 56.8 us -> 53 us
  local copies, waits for them, and re-layouts: 18.4 us -> 15 us
    dynamic_slice x1 -> x0, local copies, waits for them, and re-layouts: 4.94 us -> none  [reduce_over_dp(): keep = lax.dynamic_index_in_dim(parts, core, axis=2, keepdims=False)]
    another operation x0 -> x2, other arithmetic: none -> 2.59 us  [gather(): jnp.stack([lax.dynamic_index_in_dim(cols, 2 * k + c, axis=1, keepdims=Fal...]
    ppermute x1 -> x2, waiting for transfers between devices: 3.45 us -> 0.86 us  [reduce_over_dp(): blocks = gather(core) + lax.ppermute(gather(1 - core), 'dp', pair)]
    slice x0 -> x1, local copies, waits for them, and re-layouts: none -> 2.24 us  [reduce_over_dp(): cols = parts[:, :, p * piece:(p + 1) * piece]]
    reduce_sum x1, other arithmetic: 2.42 us -> 0.87 us  [on_device(): local_square = jnp.sum(gradient * gradient)]
    add x1 -> x3, other arithmetic: 3.32 us -> 4.44 us  [the longest x2 3.83 us: reduce_over_dp(): blocks = gather(core) + lax.ppermute(gather(1 - core), 'dp', pair)]
    ppermute x1 -> x2, waiting for transfers between devices: 19.9 us -> 18.9 us  [reduce_over_dp(): blocks = mine + lax.ppermute(other, 'dp', partner)]
    another operation x1 -> x3, local copies, waits for them, and re-layouts: 4.49 us -> 5.43 us  [gather(): jnp.stack([lax.dynamic_index_in_dim(cols, 2 * k + c, axis=1, keepdims=Fal...]
  transfers between devices with their start and end apart: 4 -> 6, of which waited for: 4 -> 5; matrix products, arithmetic and copies ran while one was open for 0% -> 6% of each run, Pallas kernels for 0% -> 0%
where the time goes in v3:
time: 129 us
  waiting for transfers between devices  53 us (41%)
  blocking collectives  29.6 us (23%)
  local copies, waits for them, and re-layouts  15 us (12%)
  starting transfers between devices  12.5 us (10%)
  other arithmetic  10.2 us (8%)
  matrix products  6.09 us (5%)
  between operations  1.53 us (1%)
    all_to_all x1, blocking collectives, on_device(): returned = lax.all_to_all(back, AXES, 0, 0, tiled=True)  29.6 us
    all_to_all x1, waiting for transfers between devices, on_device(): whole = lax.all_to_all(sent, AXES, 0, 0, tiled=True)  26.4 us
    ppermute x2, waiting for transfers between devices, reduce_over_dp(): blocks = mine + lax.ppermute(other, 'dp', partner)  18.9 us
    all_to_all x1, waiting for transfers between devices, total_over_devices(): gathered = lax.all_to_all(spread, AXES, 0, 0, tiled=True)  6.84 us
    all_to_all x1, starting transfers between devices, total_over_devices(): gathered = lax.all_to_all(spread, AXES, 0, 0, tiled=True)  6.25 us
    another operation x3, local copies, waits for them, and re-layouts, gather(): jnp.stack([lax.dynamic_index_in_dim(cols, 2 * k + c, axis=1, keepdims=Fal...  5.43 us
    add x2, other arithmetic, reduce_over_dp(): blocks = gather(core) + lax.ppermute(gather(1 - core), 'dp', pair)  3.83 us
    ppermute x2, starting transfers between devices, reduce_over_dp(): blocks = mine + lax.ppermute(other, 'dp', partner)  3.04 us
  transfers between devices with their start and end apart: 6, of which 5 were waited for; matrix products, arithmetic and copies ran while one was open for 6% of the time, Pallas kernels for 0%

profile of v3, /device:TPU:0, one launch (start us, length us, event | category | flops | bytes accessed | tf_op | source)
XLA Modules:
  0.0 128.8 jit_solution(45753300968682159)
XLA Ops:
  0.0 2.2 %fusion.72 = (f32[27,4,4096]{2,1,0:T(4,128)S(1)}, f32[27,4,4096]{2,1,0:T(4,128)S(1)}) fusion(f32[27,4,8192]{2,1,0:T(4,128)} %bitcast.45), kind=kLoop, calls=%fused_computation.111 | loop fusion | bytes 7077888 | tf_op jit(solution)/shard_map/slice | solution.py:142
  2.3 4.9 %dynamic-slice_bitcast_fusion.1 = (f32[1,27,4096]{2,0,1:T(1,128)S(1)}, f32[1,27,4096]{2,0,1:T(1,128)S(1)}, f32[1,27,4096]{2,0,1:T(1,128)}, f32[1,27,4096]{2,0,1:...) fusion(f32[27,4,4096]{2,1,0:T(4,128)S(1)} %get-tuple-element.17, ...), kind=kLoop, calls=%fused_computation.59 | loop fusion | bytes 7077904 | tf_op jit(solution)/shard_map/stack | solution.py:145
  7.2 0.0 copy-start.1
  7.2 0.0 copy-start
  7.2 1.8 %pad_maximum_fusion.2 = f32[2,27,4096]{2,0,1:T(2,128)} fusion(f32[1,27,4096]{2,0,1:T(1,128)S(1)} %get-tuple-element.30, f32[1,27,4096]{2,0,1:T(1,128)S(1)} %get-tuple-element.29), kind=kLoop, calls=%fused_computation.53 | loop fusion | flops 221184 | bytes 1769472 | tf_op jit(solution)/shard_map/stack | solution.py:145
  8.9 0.5 collective-permute-start
  9.4 0.8 pad_maximum_fusion.3
  10.2 0.1 collective-permute-start.2
  10.3 0.0 copy-done.1
  10.3 0.3 copy.28
  10.6 0.0 copy-done
  10.6 0.3 copy.27
  10.9 0.9 collective-permute-done
  11.8 0.0 copy-done.2
  11.8 0.0 copy-done.3
  11.8 2.1 %maximum_add_fusion.1 = f32[2,27,4096]{2,0,1:T(2,128)S(1)} fusion(f32[2,27,4096]{2,0,1:T(2,128)} %collective-permute-done, f32[1,27,4096]{2,0,1:T(1,128)S(1)} %copy-done.2, f32[1,27,4096]{2,0,1:T(1,128)S(1)} %copy-done.3), kind=kLoop, calls=%fused_computation.52 | loop fusion | flops 442368 | bytes 2654208 | tf_op jit(solution)/shard_map/add | solution.py:149
  13.9 0.5 constant_dynamic-slice_fusion
  14.4 3.0 %collective-permute-start.1 = (f32[1,27,4096]{2,0,1:T(1,128)S(1)}, f32[1,27,4096]{2,0,1:T(1,128)S(1)}, u32[]{:S(2)}, u32[]{:S(2)}) collective-permute-start(f32[1,27,4096]{2,0,1:T(1,128)S(1)} %constant_dynamic-slice_fusion), channel_id=1, source_target_pairs={{0,16},{8,24},{16,0},{24,8},{1,17},{9,25},{17,1},{25,9},{2,18},{10... | collective-permute-start | bytes 1327112 | tf_op jit(solution)/shard_map/ppermute | solution.py:158
  17.3 0.0 collective-permute-done.2
  17.3 1.7 %maximum_add_fusion = f32[2,27,4096]{2,1,0:T(8,128)S(1)} fusion(f32[1,27,4096]{2,1,0:T(8,128)S(1)} %copy.28, f32[1,27,4096]{2,1,0:T(8,128)S(1)} %copy.27, f32[2,27,4096]{2,0,1:T(2,128)} %collective-permute-done.2), kind=kLoop, calls=%fused_computation.46 | loop fusion | flops 442368 | bytes 2654208 | tf_op jit(solution)/shard_map/add | solution.py:149
  19.1 0.1 collective-permute-start.3
  19.2 9.1 %collective-permute-done.1 = f32[1,27,4096]{2,0,1:T(1,128)S(1)} collective-permute-done((f32[1,27,4096]{2,0,1:T(1,128)S(1)}, f32[1,27,4096]{2,0,1:T(1,128)S(1)}, u32[]{:S(2)}, u32[]{:S(2)}) %collective-permute-start.1) | collective-permute-done | bytes 442400 | tf_op jit(solution)/shard_map/ppermute | solution.py:158
  28.3 0.6 dynamic-slice_add_fusion
  28.9 0.0 copy-start.4
  28.9 0.0 copy-start.6
  28.9 0.0 copy-start.7
  28.9 0.0 copy-start.8
  28.9 0.3 copy.40
  29.2 9.8 %collective-permute-done.3 = f32[1,27,4096]{2,1,0:T(8,128)S(1)} collective-permute-done((f32[1,27,4096]{2,1,0:T(8,128)S(1)}, f32[1,27,4096]{2,1,0:T(8,128)S(1)}, u32[]{:S(2)}, u32[]{:S(2)}) %collective-permute-start.3) | collective-permute-done | bytes 442400 | tf_op jit(solution)/shard_map/ppermute | solution.py:158
  39.0 0.1 add_bitcast_fusion
  39.1 0.9 multiply_reduce_fusion
  40.0 1.2 broadcast_in_dim.8
  41.2 6.3 %all-to-all-start = ((f32[32,1,1]{2,1,0:T(1,128)}), f32[32,1,1]{2,1,0:T(1,128)S(1)}, u32[]{:S(2)}, u32[]{:S(2)}) async-start(f32[32,1,1]{2,1,0:T(1,128)} %broadcast_in_dim.8), calls=%async_computation | async-start | bytes 32768 | tf_op jit(solution)/shard_map/all_to_all | solution.py:165
  47.4 6.8 %all-to-all-done = f32[32,1,1]{2,1,0:T(1,128)S(1)} async-done(((f32[32,1,1]{2,1,0:T(1,128)}), f32[32,1,1]{2,1,0:T(1,128)S(1)}, u32[]{:S(2)}, u32[]{:S(2)}) %all-to-all-start) | async-done | bytes 160 | tf_op jit(solution)/shard_map/all_to_all | solution.py:165
  54.3 0.6 reduce_sum.37
  55.6 0.0 copy-done.4
  55.6 0.0 copy-done.6
  55.6 0.0 copy-done.7
  55.6 0.0 copy-done.8
  55.6 2.0 %convolution_convert_fusion.1 = bf16[64,8192]{1,0:T(8,128)(2,1)S(1)} fusion(f32[27,8192]{1,0:T(8,128)S(1)} %copy-done.4, f32[27,4096]{1,0:T(8,128)S(1)} %add_bitcast_fusion, f32[27,4096]{1,0:T(8,128)S(1)} %bitcast.42, f32[]{:T(128)S(6)} %min_shard_map.3, s32[27]{0:T(128)S(1)} %get-tuple-element.26, s32[64]{0:T(128)S(1)} %copy-done.6, ...), kind=kOutput, calls=%fused_computation.43 | convolution fusion | flops 171091712 | bytes 2818844 | tf_op jit(solution)/shard_map/dot_general | solution.py:187
  57.6 0.0 copy-start.9
  57.7 1.5 %reshape.106 = bf16[32,2,8192]{2,1,0:T(2,128)(2,1)} reshape(bf16[64,8192]{1,0:T(8,128)(2,1)S(1)} %convolution_convert_fusion.1) | data formatting | bytes 2097152 | tf_op jit(solution)/shard_map/reshape | solution.py:188
  59.2 2.6 %all-to-all-start.1 = ((bf16[32,2,8192]{2,1,0:T(2,128)(2,1)}), bf16[32,2,8192]{2,1,0:T(2,128)(2,1)S(1)}, u32[]{:S(2)}, u32[]{:S(2)}) async-start(bf16[32,2,8192]{2,1,0:T(2,128)(2,1)} %reshape.106), calls=%async_computation.1 | async-start | bytes 2097152 | tf_op jit(solution)/shard_map/all_to_all | solution.py:189
  61.8 0.0 copy-done.9
  61.8 0.6 dynamic_slice.33
  63.0 26.4 %all-to-all-done.1 = bf16[32,2,8192]{2,1,0:T(2,128)(2,1)S(1)} async-done(((bf16[32,2,8192]{2,1,0:T(2,128)(2,1)}), bf16[32,2,8192]{2,1,0:T(2,128)(2,1)S(1)}, u32[]{:S(2)}, u32[]{:S(2)}) %all-to-all-start.1) | async-done | bytes 1048608 | tf_op jit(solution)/shard_map/all_to_all | solution.py:189
  89.4 0.6 copy.31
  90.0 0.5 reshape.107
  90.5 5.0 %conditional.1 = (bf16[2,512,512]{2,1,0:T(8,128)(2,1)S(1)}) conditional(s32[]{:T(128)} %bitcast.4, bf16[2,512,512]{2,1,0:T(8,128)(2,1)S(1)} %reshape.107, bf16[2,512,512]{2,1,0:T(8,128)(2,1)S(1)} %reshape.107), branch_computations={%region_2.4_spmd, %region_4.6_spmd} | conditional | flops 2175270912 | bytes 19398728 | solution.py:194
  90.5 1.1 fusion.6
  92.4 0.2 fusion.7
  92.7 0.1 slice_bitcast_fusion.3
  92.7 1.3 fusion.24
  94.0 0.1 slice_negate_fusion
  94.1 1.3 subtract_convert_fusion.1
  95.4 0.1 slice_bitcast_fusion.1
  95.5 0.1 pad_maximum_fusion
  95.6 0.5 reshape.108
  96.1 1.1 copy.39
  97.2 0.0 copy-start.5
  97.2 29.6 %all_to_all.16 = bf16[32,2,8192]{2,1,0:T(2,128)(2,1)S(1)} all-to-all(bf16[32,2,8192]{2,1,0:T(2,128)(2,1)S(1)} %bitcast.44), channel_id=1, replica_groups=mesh['dp'=4,'freq'=8] {'dp','freq'}, dimensions={0} | all-to-all | bytes 2097152 | tf_op jit(solution)/shard_map/all_to_all | solution.py:197
  126.8 0.4 reshape.109
  127.3 0.0 copy-done.5
  127.3 1.5 %fusion.36 = f32[27,8192]{1,0:T(8,128)} fusion(bf16[64,8192]{1,0:T(8,128)(2,1)S(1)} %reshape.109, f32[27,64]{1,0:T(8,128)S(1)} %copy-done.5), kind=kOutput, calls=%fused_computation.45 | convolution fusion | flops 170090496 | bytes 1940224 | tf_op jit(solution)/shard_map/dot_general | solution.py:199
  (5 shorter events, 0.1 us)
Async XLA Ops:
  7.2 3.2 %copy-start.1 = (f32[1,27,4096]{2,0,1:T(1,128)S(1)}, f32[1,27,4096]{2,0,1:T(1,128)}, u32[]{:S(2)}) copy-start(f32[1,27,4096]{2,0,1:T(1,128)} %get-tuple-element.24) | copy-start | bytes 1327108
  7.2 3.5 %copy-start = (f32[1,27,4096]{2,0,1:T(1,128)S(1)}, f32[1,27,4096]{2,0,1:T(1,128)}, u32[]{:S(2)}) copy-start(f32[1,27,4096]{2,0,1:T(1,128)} %get-tuple-element.25) | copy-start | bytes 1327108
  8.9 2.9 %copy-start.2 = (f32[1,27,4096]{2,0,1:T(1,128)S(1)}, f32[1,27,4096]{2,0,1:T(1,128)}, u32[]{:S(2)}) copy-start(f32[1,27,4096]{2,0,1:T(1,128)} %get-tuple-element.28) | copy-start | bytes 1327108
  8.9 2.9 %copy-start.3 = (f32[1,27,4096]{2,0,1:T(1,128)S(1)}, f32[1,27,4096]{2,0,1:T(1,128)}, u32[]{:S(2)}) copy-start(f32[1,27,4096]{2,0,1:T(1,128)} %get-tuple-element.31) | copy-start | bytes 1327108
  8.9 2.8 %collective-permute-start = (f32[2,27,4096]{2,0,1:T(2,128)}, f32[2,27,4096]{2,0,1:T(2,128)}, u32[]{:S(2)}, u32[]{:S(2)}) collective-permute-start(f32[2,27,4096]{2,0,1:T(2,128)} %pad_maximum_fusion.2), channel_id=1, source_target_pairs={{0,8},{8,0},{16,24},{24,16},{1,9},{9,1},{17,25},{25,17},{2,10},{10... | collective-permute-start | bytes 2654216 | tf_op jit(solution)/shard_map/ppermute | solution.py:149
  10.2 7.1 %collective-permute-start.2 = (f32[2,27,4096]{2,0,1:T(2,128)S(1)}, f32[2,27,4096]{2,0,1:T(2,128)}, u32[]{:S(2)}, u32[]{:S(2)}) collective-permute-start(f32[2,27,4096]{2,0,1:T(2,128)S(1)} %pad_maximum_fusion.3), channel_id=1, source_target_pairs={{0,8},{8,0},{16,24},{24,16},{1,9},{9,1},{17,25},{25,17},{2,10},{10... | collective-permute-start | bytes 2654216 | tf_op jit(solution)/shard_map/ppermute | solution.py:149
  14.4 13.9 %collective-permute-start.1 = (f32[1,27,4096]{2,0,1:T(1,128)S(1)}, f32[1,27,4096]{2,0,1:T(1,128)S(1)}, u32[]{:S(2)}, u32[]{:S(2)}) collective-permute-start(f32[1,27,4096]{2,0,1:T(1,128)S(1)} %constant_dynamic-slice_fusion), channel_id=1, source_target_pairs={{0,16},{8,24},{16,0},{24,8},{1,17},{9,25},{17,1},{25,9},{2,18},{10... | collective-permute-start | bytes 1327112 | tf_op jit(solution)/shard_map/ppermute | solution.py:158
  19.1 19.9 %collective-permute-start.3 = (f32[1,27,4096]{2,1,0:T(8,128)S(1)}, f32[1,27,4096]{2,1,0:T(8,128)S(1)}, u32[]{:S(2)}, u32[]{:S(2)}) collective-permute-start(f32[1,27,4096]{2,1,0:T(8,128)S(1)} %constant_dynamic-slice_fusion.1), channel_id=1, source_target_pairs={{0,16},{8,24},{16,0},{24,8},{1,17},{9,25},{17,1},{25,9},{2,18},{10... | collective-permute-start | bytes 1327112 | tf_op jit(solution)/shard_map/ppermute | solution.py:158
  28.9 26.7 %copy-start.4 = (f32[27,8192]{1,0:T(8,128)S(1)}, f32[27,8192]{1,0:T(8,128)}, u32[]{:S(2)}) copy-start(f32[27,8192]{1,0:T(8,128)} %param.9) | copy-start | bytes 2654212
  28.9 26.7 %copy-start.6 = (s32[64]{0:T(128)S(1)}, s32[64]{0:T(128)}, u32[]{:S(2)}) copy-start(s32[64]{0:T(128)} %constant.272) | copy-start | bytes 772
  28.9 26.7 %copy-start.7 = (s32[64]{0:T(128)S(1)}, s32[64]{0:T(128)}, u32[]{:S(2)}) copy-start(s32[64]{0:T(128)} %constant.251) | copy-start | bytes 772
  28.9 26.7 %copy-start.8 = (pred[64]{0:T(512)(128)(4,1)S(1)}, pred[64]{0:T(512)(128)(4,1)}, u32[]{:S(2)}) copy-start(pred[64]{0:T(512)(128)(4,1)} %constant.232.clone) | copy-start | bytes 196
  41.2 13.1 %all-to-all-start = ((f32[32,1,1]{2,1,0:T(1,128)}), f32[32,1,1]{2,1,0:T(1,128)S(1)}, u32[]{:S(2)}, u32[]{:S(2)}) async-start(f32[32,1,1]{2,1,0:T(1,128)} %broadcast_in_dim.8), calls=%async_computation | async-start | bytes 32768 | tf_op jit(solution)/shard_map/all_to_all | solution.py:165
  57.6 4.2 %copy-start.9 = (s32[32]{0:T(128)S(1)}, s32[32]{0:T(128)}, u32[]{:S(2)}) copy-start(s32[32]{0:T(128)} %constant.233.clone) | copy-start | bytes 388
  59.2 30.2 %all-to-all-start.1 = ((bf16[32,2,8192]{2,1,0:T(2,128)(2,1)}), bf16[32,2,8192]{2,1,0:T(2,128)(2,1)S(1)}, u32[]{:S(2)}, u32[]{:S(2)}) async-start(bf16[32,2,8192]{2,1,0:T(2,128)(2,1)} %reshape.106), calls=%async_computation.1 | async-start | bytes 2097152 | tf_op jit(solution)/shard_map/all_to_all | solution.py:189
  97.2 30.1 %copy-start.5 = (f32[27,64]{1,0:T(8,128)S(1)}, f32[27,64]{1,0:T(8,128)}, u32[]{:S(2)}) copy-start(f32[27,64]{1,0:T(8,128)} %constant.234.clone) | copy-start | bytes 20740

commit v4 on v3

--- a/solution.py
+++ b/solution.py
@@ -166,6 +166,18 @@
     return jnp.sum(gathered)
 
 
+def tap_groups(total_freq, stride):
+    turns = turns_of(np.arange(total_freq), stride)
+    groups = {}
+    for t in range(TAPS):
+        groups.setdefault(tuple(turns[:, t]), []).append(t)
+    return list(groups.values())
+
+
+def group_sums(field, groups):
+    return jnp.stack([sum(field[t] for t in group) for group in groups])
+
+
 def on_device(grad_parts, kernel):
     devices_dp = lax.axis_size("dp")
     devices_freq = lax.axis_size("freq")
@@ -175,19 +187,43 @@
     scale_out = math.sqrt(C / total_freq)
     own_width = kernel.shape[1]
     rows, backward, kinds = slot_plan(total_freq, stride)
+    groups = tap_groups(total_freq, stride)
+    half = devices_freq // 2
+    fi = lax.axis_index("freq")
+    side = fi // half
+    across = [(i, i ^ half) for i in range(devices_freq)]
+
+    kernel_sums = group_sums(kernel, groups)
+    kernel_far = lax.ppermute(kernel_sums, "freq", across)
 
     gradient = reduce_over_dp(grad_parts, own_width)
+    gradient_sums = group_sums(gradient, groups)
+    gradient_far = lax.ppermute(gradient_sums, "freq", across)
     local_square = jnp.sum(gradient * gradient)
     summed = total_over_devices(local_square, devices)
     factor = jnp.minimum(1.0, CLIP * math.sqrt(TAPS * C * C) / jnp.sqrt(summed + 1e-06))
-    updated = kernel - factor * gradient
+
+    near = kernel_sums - factor * gradient_sums
+    far = kernel_far - factor * gradient_far
+    first = side == 0
+    fields = jnp.stack([jnp.where(first, near, far), jnp.where(first, far, near)], axis=1)
 
     cosine, sine = tap_phases(jnp.asarray(rows[:, 0]), stride)
     forward = jnp.where(jnp.asarray(rows[:, 1] == 0)[:, None], cosine, -sine)
-    spectra = jnp.dot(forward, updated, precision=HIGH).astype(jnp.bfloat16)
-    sent = spectra.reshape(devices, 2, own_width)
-    whole = lax.all_to_all(sent, AXES, 0, 0, tiled=True)
-    matrix = whole.transpose(1, 0, 2).reshape(2, C, C)
+    forward = forward[:, np.array([group[0] for group in groups])]
+    members = [
+        [d * devices_freq + h * half + q for d in range(devices_dp) for q in range(half)] for h in range(2)
+    ]
+    plane_ids = np.array([[2 * s + r for s in members[h] for r in range(2)] for h in range(2)])
+    forward_side = lax.dynamic_index_in_dim(forward[plane_ids], side, axis=0, keepdims=False)
+    spectra = jnp.dot(
+        forward_side, fields.reshape(len(groups), 2 * own_width), precision=HIGH
+    ).astype(jnp.bfloat16)
+    sent = spectra.reshape(len(members[0]), 2, 2, own_width)
+    got = lax.all_to_all(sent, AXES, 0, 0, tiled=True, axis_index_groups=members)
+    matrix = (
+        got.reshape(devices_dp, half, 2, 2, own_width).transpose(2, 0, 3, 1, 4).reshape(2, C, C)
+    )
 
     me = lax.axis_index(AXES)
     is_pair = jnp.asarray(kinds)[me] == 1

time: 129 us -> 136 us (1.054)
  local copies, waits for them, and re-layouts: 15 us -> 19.4 us
  starting transfers between devices: 12.5 us -> 16.7 us
  waiting for transfers between devices: 53 us -> 49.1 us
  other arithmetic: 10.2 us -> 12.7 us
    all_to_all x1, waiting for transfers between devices: 26.4 us -> 13.6 us  [on_device(): lax.all_to_all(sent, AXES, 0, 0, tiled=True, axis_index_groups=members)]
    all_to_all x1, waiting for transfers between devices: 6.84 us -> 17.2 us  [total_over_devices(): gathered = lax.all_to_all(spread, AXES, 0, 0, tiled=True)]
    ppermute x0 -> x2, starting transfers between devices: none -> 4.51 us  [the longest x1 4.1 us: on_device(): kernel_far = lax.ppermute(kernel_sums, 'freq', across)]
    another operation x0 -> x3, local copies, waits for them, and re-layouts: none -> 1.5 us  [the longest x2 1.05 us: group_sums(): return jnp.stack([sum((field[t] for t in group)) for group in groups])]
    reshape x2 -> x3, local copies, waits for them, and re-layouts: 2.03 us -> 3.21 us  [the longest x2 1.62 us: on_device(): got.reshape(devices_dp, half, 2, 2, own_width).transpose(2, 0, 3, 1, 4)]
  transfers between devices with their start and end apart: 6 -> 8, of which waited for: 5 -> 4; matrix products, arithmetic and copies ran while one was open for 6% -> 11% of each run, Pallas kernels for 0% -> 0%
where the time goes in v4:
time: 136 us
  waiting for transfers between devices  49.1 us (36%)
  blocking collectives  29.7 us (22%)
  local copies, waits for them, and re-layouts  19.4 us (14%)
  starting transfers between devices  16.7 us (12%)
  other arithmetic  12.7 us (9%)
  matrix products  5.87 us (4%)
  between operations  1.68 us (1%)
    all_to_all x1, blocking collectives, on_device(): returned = lax.all_to_all(back, AXES, 0, 0, tiled=True)  29.7 us
    ppermute x2, waiting for transfers between devices, reduce_over_dp(): blocks = mine + lax.ppermute(other, 'dp', partner)  18.2 us
    all_to_all x1, waiting for transfers between devices, total_over_devices(): gathered = lax.all_to_all(spread, AXES, 0, 0, tiled=True)  17.2 us
    all_to_all x1, waiting for transfers between devices, on_device(): lax.all_to_all(sent, AXES, 0, 0, tiled=True, axis_index_groups=members)  13.6 us
    all_to_all x1, starting transfers between devices, total_over_devices(): gathered = lax.all_to_all(spread, AXES, 0, 0, tiled=True)  5.84 us
    another operation x3, local copies, waits for them, and re-layouts, gather(): jnp.stack([lax.dynamic_index_in_dim(cols, 2 * k + c, axis=1, keepdims=Fal...  5.46 us
    ppermute x1, starting transfers between devices, on_device(): kernel_far = lax.ppermute(kernel_sums, 'freq', across)  4.1 us
    add x2, other arithmetic, reduce_over_dp(): blocks = gather(core) + lax.ppermute(gather(1 - core), 'dp', pair)  3.83 us
  transfers between devices with their start and end apart: 8, of which 4 were waited for; matrix products, arithmetic and copies ran while one was open for 11% of the time, Pallas kernels for 0%

profile of v4, /device:TPU:0, one launch (start us, length us, event | category | flops | bytes accessed | tf_op | source)
XLA Modules:
  0.0 136.1 jit_solution(9944012572018567033)
XLA Ops:
  0.0 2.2 %fusion.93 = (f32[27,4,4096]{2,1,0:T(4,128)S(1)}, f32[27,4,4096]{2,1,0:T(4,128)S(1)}) fusion(f32[27,4,8192]{2,1,0:T(4,128)} %bitcast.64), kind=kLoop, calls=%fused_computation.207 | loop fusion | bytes 7077888 | tf_op jit(solution)/shard_map/slice | solution.py:142
  2.3 4.9 %dynamic-slice_bitcast_fusion.1 = (f32[1,27,4096]{2,0,1:T(1,128)S(1)}, f32[1,27,4096]{2,0,1:T(1,128)S(1)}, f32[1,27,4096]{2,0,1:T(1,128)}, f32[1,27,4096]{2,0,1:...) fusion(f32[27,4,4096]{2,1,0:T(4,128)S(1)} %get-tuple-element.17, ...), kind=kLoop, calls=%fused_computation.119 | loop fusion | bytes 7077904 | tf_op jit(solution)/shard_map/stack | solution.py:145
  7.2 1.8 %pad_maximum_fusion.3 = f32[2,27,4096]{2,0,1:T(2,128)} fusion(f32[1,27,4096]{2,0,1:T(1,128)S(1)} %get-tuple-element.50, f32[1,27,4096]{2,0,1:T(1,128)S(1)} %get-tuple-element.49), kind=kLoop, calls=%fused_computation.110 | loop fusion | flops 221184 | bytes 1769472 | tf_op jit(solution)/shard_map/stack | solution.py:145
  9.0 0.5 collective-permute-start
  9.4 1.8 %pad_maximum_fusion.4 = f32[2,27,4096]{2,0,1:T(2,128)} fusion(f32[1,27,4096]{2,0,1:T(1,128)S(1)} %get-tuple-element.25, f32[1,27,4096]{2,0,1:T(1,128)S(1)} %get-tuple-element.24), kind=kLoop, calls=%fused_computation.111 | loop fusion | flops 221184 | bytes 1769472 | tf_op jit(solution)/shard_map/stack | solution.py:145
  11.2 0.1 collective-permute-start.2
  11.2 0.4 slice_add_fusion
  11.6 0.2 slice_add_fusion.1
  11.8 0.4 stack.78
  12.3 4.1 %collective-permute-start.4 = (f32[9,8192]{1,0:T(8,128)S(1)}, f32[9,8192]{1,0:T(8,128)S(1)}, u32[]{:S(2)}, u32[]{:S(2)}) collective-permute-start(f32[9,8192]{1,0:T(8,128)S(1)} %stack.78), channel_id=1, source_target_pairs={{0,4},{1,5},{2,6},{3,7},{4,0},{5,1},{6,2},{7,3},{8,12},{9,13},{10,... | collective-permute-start | bytes 884744 | tf_op jit(solution)/shard_map/ppermute | solution.py:197
  16.4 0.3 copy.39
  16.6 0.3 copy.40
  17.0 2.1 %maximum_add_fusion.1 = f32[2,27,4096]{2,0,1:T(2,128)S(1)} fusion(f32[2,27,4096]{2,0,1:T(2,128)} %collective-permute-done, f32[1,27,4096]{2,0,1:T(1,128)S(1)} %copy-done.2, f32[1,27,4096]{2,0,1:T(1,128)S(1)} %copy-done.3), kind=kLoop, calls=%fused_computation.109 | loop fusion | flops 442368 | bytes 2654208 | tf_op jit(solution)/shard_map/add | solution.py:149
  19.1 0.5 constant_dynamic-slice_fusion
  19.6 1.6 %collective-permute-start.1 = (f32[1,27,4096]{2,0,1:T(1,128)S(1)}, f32[1,27,4096]{2,0,1:T(1,128)S(1)}, u32[]{:S(2)}, u32[]{:S(2)}) collective-permute-start(f32[1,27,4096]{2,0,1:T(1,128)S(1)} %constant_dynamic-slice_fusion), channel_id=1, source_target_pairs={{0,16},{8,24},{16,0},{24,8},{1,17},{9,25},{17,1},{25,9},{2,18},{10... | collective-permute-start | bytes 1327112 | tf_op jit(solution)/shard_map/ppermute | solution.py:158
  21.2 1.7 %maximum_add_fusion = f32[2,27,4096]{2,1,0:T(8,128)S(1)} fusion(f32[1,27,4096]{2,1,0:T(8,128)S(1)} %copy.40, f32[1,27,4096]{2,1,0:T(8,128)S(1)} %copy.39, f32[2,27,4096]{2,0,1:T(2,128)} %collective-permute-done.2), kind=kLoop, calls=%fused_computation.105 | loop fusion | flops 442368 | bytes 2654208 | tf_op jit(solution)/shard_map/add | solution.py:149
  23.0 0.6 collective-permute-start.3
  23.5 9.2 %collective-permute-done.1 = f32[1,27,4096]{2,0,1:T(1,128)S(1)} collective-permute-done((f32[1,27,4096]{2,0,1:T(1,128)S(1)}, f32[1,27,4096]{2,0,1:T(1,128)S(1)}, u32[]{:S(2)}, u32[]{:S(2)}) %collective-permute-start.1) | collective-permute-done | bytes 442400 | tf_op jit(solution)/shard_map/ppermute | solution.py:158
  32.7 0.6 dynamic-slice_add_fusion
  33.4 0.3 copy.56
  33.6 0.0 copy-start.6
  33.6 0.0 copy-start.7
  33.7 0.0 copy-start.8
  33.7 9.0 %collective-permute-done.3 = f32[1,27,4096]{2,1,0:T(8,128)S(1)} collective-permute-done((f32[1,27,4096]{2,1,0:T(8,128)S(1)}, f32[1,27,4096]{2,1,0:T(8,128)S(1)}, u32[]{:S(2)}, u32[]{:S(2)}) %collective-permute-start.3) | collective-permute-done | bytes 442400 | tf_op jit(solution)/shard_map/ppermute | solution.py:158
  42.7 0.1 add_bitcast_fusion
  42.8 0.6 fusion.66
  43.4 0.6 stack.91
  44.0 0.4 collective-permute-start.5
  44.5 0.2 negate_select_fusion.2
  44.7 0.9 fusion.38
  45.5 1.2 broadcast_in_dim.28
  46.7 5.8 %all-to-all-start = ((f32[32,1,1]{2,1,0:T(1,128)}), f32[32,1,1]{2,1,0:T(1,128)S(1)}, u32[]{:S(2)}, u32[]{:S(2)}) async-start(f32[32,1,1]{2,1,0:T(1,128)} %broadcast_in_dim.28), calls=%async_computation | async-start | bytes 32768 | tf_op jit(solution)/shard_map/all_to_all | solution.py:165
  52.6 0.6 gather_fusion
  53.1 0.1 copy.38
  53.2 0.6 gather_fusion.1
  53.8 17.2 %all-to-all-done = f32[32,1,1]{2,1,0:T(1,128)S(1)} async-done(((f32[32,1,1]{2,1,0:T(1,128)}), f32[32,1,1]{2,1,0:T(1,128)S(1)}, u32[]{:S(2)}, u32[]{:S(2)}) %all-to-all-start) | async-done | bytes 160 | tf_op jit(solution)/shard_map/all_to_all | solution.py:165
  71.0 0.6 reduce_sum.37
  72.4 0.1 select_bitcast_fusion.1
  72.5 0.1 pad_maximum_fusion.2
  72.6 0.5 copy.43
  73.1 0.3 pad.27
  73.4 0.6 copy.49
  74.0 1.8 %convolution_convert_fusion.1 = bf16[32,16384]{1,0:T(8,128)(2,1)S(1)} fusion(f32[9,16384]{1,0:T(8,128)S(1)} %bitcast.59, f32[2,32,9]{2,1,0:T(8,128)S(1)} %bitcast.66, s32[]{:T(128)S(6)} %select_n.149), kind=kOutput, calls=%fused_computation.45 | convolution fusion | flops 57147392 | bytes 2113540 | tf_op jit(solution)/shard_map/dot_general | solution.py:219
  75.8 0.0 copy-start.10
  75.8 1.6 %reshape.113 = bf16[16,2,2,8192]{3,2,1,0:T(2,128)(2,1)} reshape(bf16[32,16384]{1,0:T(8,128)(2,1)S(1)} %convolution_convert_fusion.1) | data formatting | bytes 2097152 | tf_op jit(solution)/shard_map/reshape | solution.py:222
  77.4 3.7 %all-to-all-start.1 = ((bf16[16,2,2,8192]{3,2,1,0:T(2,128)(2,1)}), bf16[16,2,2,8192]{3,2,1,0:T(2,128)(2,1)S(1)}, u32[]{:S(2)}, u32[]{:S(2)}) async-start(bf16[16,2,2,8192]{3,2,1,0:T(2,128)(2,1)} %reshape.113), calls=%async_computation.1 | async-start | bytes 2097152 | tf_op jit(solution)/shard_map/all_to_all | solution.py:223
  81.1 0.6 dynamic_slice.37
  82.2 13.6 %all-to-all-done.1 = bf16[16,2,2,8192]{3,2,1,0:T(2,128)(2,1)S(1)} async-done(((bf16[16,2,2,8192]{3,2,1,0:T(2,128)(2,1)}), bf16[16,2,2,8192]{3,2,1,0:T(2,128)(2,1)S(1)}, u32[]{:S(2)}, u32[]{:S(2)}) %all-to-all-start.1) | async-done | bytes 1048608 | tf_op jit(solution)/shard_map/all_to_all | solution.py:223
  95.8 0.8 copy.55
  96.7 0.8 reshape.115
  97.5 5.3 %conditional.1 = (bf16[2,512,512]{2,1,0:T(8,128)(2,1)S(1)}) conditional(s32[]{:T(128)} %bitcast.4, bf16[2,512,512]{2,1,0:T(8,128)(2,1)S(1)} %reshape.115, bf16[2,512,512]{2,1,0:T(8,128)(2,1)S(1)} %reshape.115), branch_computations={%region_2.4_spmd, %region_4.6_spmd} | conditional | flops 2175270912 | bytes 19398728 | solution.py:230
  97.5 1.1 fusion.6
  99.4 0.2 fusion.7
  99.6 0.1 slice_bitcast_fusion.3
  99.7 1.3 fusion.24
  101.0 0.1 slice_negate_fusion
  101.0 1.3 subtract_convert_fusion.1
  102.3 0.1 slice_bitcast_fusion.1
  102.4 0.1 pad_maximum_fusion
  102.7 0.5 reshape.116
  103.3 1.1 copy.54
  104.4 29.7 %all_to_all.16 = bf16[32,2,8192]{2,1,0:T(2,128)(2,1)S(1)} all-to-all(bf16[32,2,8192]{2,1,0:T(2,128)(2,1)S(1)} %bitcast.63), channel_id=1, replica_groups=mesh['dp'=4,'freq'=8] {'dp','freq'}, dimensions={0} | all-to-all | bytes 2097152 | tf_op jit(solution)/shard_map/all_to_all | solution.py:233
  134.1 0.4 reshape.117
  134.5 1.5 %fusion.36 = f32[27,8192]{1,0:T(8,128)} fusion(bf16[64,8192]{1,0:T(8,128)(2,1)S(1)} %reshape.117, f32[27,64]{1,0:T(8,128)S(1)} %copy-done.5), kind=kOutput, calls=%fused_computation.47 | convolution fusion | flops 170090496 | bytes 1940224 | tf_op jit(solution)/shard_map/dot_general | solution.py:235
  (28 shorter events, 0.2 us)
Async XLA Ops:
  7.2 4.0 %copy-start.4 = (f32[27,8192]{1,0:T(8,128)S(1)}, f32[27,8192]{1,0:T(8,128)}, u32[]{:S(2)}) copy-start(f32[27,8192]{1,0:T(8,128)} %param.13) | copy-start | bytes 2654212
  9.0 7.4 %copy-start.1 = (f32[1,27,4096]{2,0,1:T(1,128)S(1)}, f32[1,27,4096]{2,0,1:T(1,128)}, u32[]{:S(2)}) copy-start(f32[1,27,4096]{2,0,1:T(1,128)} %get-tuple-element.27) | copy-start | bytes 1327108
  9.0 8.0 %collective-permute-start = (f32[2,27,4096]{2,0,1:T(2,128)}, f32[2,27,4096]{2,0,1:T(2,128)}, u32[]{:S(2)}, u32[]{:S(2)}) collective-permute-start(f32[2,27,4096]{2,0,1:T(2,128)} %pad_maximum_fusion.3), channel_id=1, source_target_pairs={{0,8},{8,0},{16,24},{24,16},{1,9},{9,1},{17,25},{25,17},{2,10},{10... | collective-permute-start | bytes 2654216 | tf_op jit(solution)/shard_map/ppermute | solution.py:149
  9.4 7.2 %copy-start = (f32[1,27,4096]{2,0,1:T(1,128)S(1)}, f32[1,27,4096]{2,0,1:T(1,128)}, u32[]{:S(2)}) copy-start(f32[1,27,4096]{2,0,1:T(1,128)} %get-tuple-element.26) | copy-start | bytes 1327108
  11.2 5.8 %copy-start.9 = (s32[64]{0:T(128)S(1)}, s32[64]{0:T(128)}, u32[]{:S(2)}) copy-start(s32[64]{0:T(128)} %constant.308) | copy-start | bytes 772
  11.2 5.8 %copy-start.2 = (f32[1,27,4096]{2,0,1:T(1,128)S(1)}, f32[1,27,4096]{2,0,1:T(1,128)}, u32[]{:S(2)}) copy-start(f32[1,27,4096]{2,0,1:T(1,128)} %get-tuple-element.48) | copy-start | bytes 1327108
  11.2 5.8 %copy-start.3 = (f32[1,27,4096]{2,0,1:T(1,128)S(1)}, f32[1,27,4096]{2,0,1:T(1,128)}, u32[]{:S(2)}) copy-start(f32[1,27,4096]{2,0,1:T(1,128)} %get-tuple-element.51) | copy-start | bytes 1327108
  11.2 10.0 %collective-permute-start.2 = (f32[2,27,4096]{2,0,1:T(2,128)}, f32[2,27,4096]{2,0,1:T(2,128)}, u32[]{:S(2)}, u32[]{:S(2)}) collective-permute-start(f32[2,27,4096]{2,0,1:T(2,128)} %pad_maximum_fusion.4), channel_id=1, source_target_pairs={{0,8},{8,0},{16,24},{24,16},{1,9},{9,1},{17,25},{25,17},{2,10},{10... | collective-permute-start | bytes 2654216 | tf_op jit(solution)/shard_map/ppermute | solution.py:149
  12.3 60.1 %collective-permute-start.4 = (f32[9,8192]{1,0:T(8,128)S(1)}, f32[9,8192]{1,0:T(8,128)S(1)}, u32[]{:S(2)}, u32[]{:S(2)}) collective-permute-start(f32[9,8192]{1,0:T(8,128)S(1)} %stack.78), channel_id=1, source_target_pairs={{0,4},{1,5},{2,6},{3,7},{4,0},{5,1},{6,2},{7,3},{8,12},{9,13},{10,... | collective-permute-start | bytes 884744 | tf_op jit(solution)/shard_map/ppermute | solution.py:197
  19.6 13.1 %collective-permute-start.1 = (f32[1,27,4096]{2,0,1:T(1,128)S(1)}, f32[1,27,4096]{2,0,1:T(1,128)S(1)}, u32[]{:S(2)}, u32[]{:S(2)}) collective-permute-start(f32[1,27,4096]{2,0,1:T(1,128)S(1)} %constant_dynamic-slice_fusion), channel_id=1, source_target_pairs={{0,16},{8,24},{16,0},{24,8},{1,17},{9,25},{17,1},{25,9},{2,18},{10... | collective-permute-start | bytes 1327112 | tf_op jit(solution)/shard_map/ppermute | solution.py:158
  23.0 19.8 %collective-permute-start.3 = (f32[1,27,4096]{2,1,0:T(8,128)S(1)}, f32[1,27,4096]{2,1,0:T(8,128)S(1)}, u32[]{:S(2)}, u32[]{:S(2)}) collective-permute-start(f32[1,27,4096]{2,1,0:T(8,128)S(1)} %constant_dynamic-slice_fusion.1), channel_id=1, source_target_pairs={{0,16},{8,24},{16,0},{24,8},{1,17},{9,25},{17,1},{25,9},{2,18},{10... | collective-permute-start | bytes 1327112 | tf_op jit(solution)/shard_map/ppermute | solution.py:158
  33.6 10.8 %copy-start.6 = (pred[64]{0:T(512)(128)(4,1)S(1)}, pred[64]{0:T(512)(128)(4,1)}, u32[]{:S(2)}) copy-start(pred[64]{0:T(512)(128)(4,1)} %constant.258.clone) | copy-start | bytes 196
  33.6 10.8 %copy-start.7 = (s32[64]{0:T(128)S(1)}, s32[64]{0:T(128)}, u32[]{:S(2)}) copy-start(s32[64]{0:T(128)} %constant.280) | copy-start | bytes 772
  33.7 10.8 %copy-start.8 = (s32[64]{0:T(128)S(1)}, s32[64]{0:T(128)}, u32[]{:S(2)}) copy-start(s32[64]{0:T(128)} %constant.301) | copy-start | bytes 772
  44.0 28.4 %collective-permute-start.5 = (f32[9,8192]{1,0:T(8,128)S(1)}, f32[9,8192]{1,0:T(8,128)S(1)}, u32[]{:S(2)}, u32[]{:S(2)}) collective-permute-start(f32[9,8192]{1,0:T(8,128)S(1)} %stack.91), channel_id=1, source_target_pairs={{0,4},{1,5},{2,6},{3,7},{4,0},{5,1},{6,2},{7,3},{8,12},{9,13},{10,... | collective-permute-start | bytes 884744 | tf_op jit(solution)/shard_map/ppermute | solution.py:201
  46.7 24.3 %all-to-all-start = ((f32[32,1,1]{2,1,0:T(1,128)}), f32[32,1,1]{2,1,0:T(1,128)S(1)}, u32[]{:S(2)}, u32[]{:S(2)}) async-start(f32[32,1,1]{2,1,0:T(1,128)} %broadcast_in_dim.28), calls=%async_computation | async-start | bytes 32768 | tf_op jit(solution)/shard_map/all_to_all | solution.py:165
  75.8 5.3 %copy-start.10 = (s32[32]{0:T(128)S(1)}, s32[32]{0:T(128)}, u32[]{:S(2)}) copy-start(s32[32]{0:T(128)} %constant.262.clone) | copy-start | bytes 388
  77.4 18.4 %all-to-all-start.1 = ((bf16[16,2,2,8192]{3,2,1,0:T(2,128)(2,1)}), bf16[16,2,2,8192]{3,2,1,0:T(2,128)(2,1)S(1)}, u32[]{:S(2)}, u32[]{:S(2)}) async-start(bf16[16,2,2,8192]{3,2,1,0:T(2,128)(2,1)} %reshape.113), calls=%async_computation.1 | async-start | bytes 2097152 | tf_op jit(solution)/shard_map/all_to_all | solution.py:223
  104.4 30.1 %copy-start.5 = (f32[27,64]{1,0:T(8,128)S(1)}, f32[27,64]{1,0:T(8,128)}, u32[]{:S(2)}) copy-start(f32[27,64]{1,0:T(8,128)} %constant.263.clone) | copy-start | bytes 20740

commit v5 on v4

--- a/solution.py
+++ b/solution.py
@@ -127,9 +127,11 @@
 def reduce_over_dp(grad_parts, own_width, pieces=2):
     devices_dp = lax.axis_size("dp")
     if devices_dp % 2 or own_width % (128 * pieces):
-        return lax.psum_scatter(grad_parts[0], "dp", scatter_dimension=1, tiled=True).reshape(
-            TAPS, own_width
-        )
+        return [
+            lax.psum_scatter(grad_parts[0], "dp", scatter_dimension=1, tiled=True).reshape(
+                TAPS, own_width
+            )
+        ]
     d = lax.axis_index("dp")
     core = d % 2
     chip = d // 2
@@ -157,7 +159,7 @@
             partner = [(i, i ^ (2 * width)) for i in range(devices_dp)]
             blocks = mine + lax.ppermute(other, "dp", partner)
         outs.append(blocks.reshape(TAPS, piece))
-    return jnp.concatenate(outs, axis=1)
+    return outs
 
 
 def total_over_devices(value, devices):
@@ -191,14 +193,26 @@
     half = devices_freq // 2
     fi = lax.axis_index("freq")
     side = fi // half
+    pairs = [
+        [d * devices_freq + q, d * devices_freq + q + half] for d in range(devices_dp) for q in range(half)
+    ]
+
+    def swap(value):
+        both = lax.all_to_all(
+            jnp.stack([value, value]), AXES, 0, 0, tiled=True, axis_index_groups=pairs
+        )
+        return lax.dynamic_index_in_dim(both, 1 - side, axis=0, keepdims=False)
+
+    kernel_sums = group_sums(kernel, groups)
+    kernel_far = swap(kernel_sums)
+
+    pieces = reduce_over_dp(grad_parts, own_width)
+    gradient = jnp.concatenate(pieces, axis=1)
+    gradient_sums = jnp.concatenate([group_sums(p, groups) for p in pieces], axis=1)
     across = [(i, i ^ half) for i in range(devices_freq)]
-
-    kernel_sums = group_sums(kernel, groups)
-    kernel_far = lax.ppermute(kernel_sums, "freq", across)
-
-    gradient = reduce_over_dp(grad_parts, own_width)
-    gradient_sums = group_sums(gradient, groups)
-    gradient_far = lax.ppermute(gradient_sums, "freq", across)
+    gradient_far = jnp.concatenate(
+        [lax.ppermute(group_sums(p, groups), "freq", across) for p in pieces], axis=1
+    )
     local_square = jnp.sum(gradient * gradient)
     summed = total_over_devices(local_square, devices)
     factor = jnp.minimum(1.0, CLIP * math.sqrt(TAPS * C * C) / jnp.sqrt(summed + 1e-06))

time: 136 us -> 138 us (1.015)
  waiting for transfers between devices: 49.1 us -> 38.5 us
  other arithmetic: 12.7 us -> 18.4 us
  starting transfers between devices: 16.7 us -> 21.7 us
    all_to_all x1, waiting for transfers between devices: 17.2 us -> 11.6 us  [total_over_devices(): gathered = lax.all_to_all(spread, AXES, 0, 0, tiled=True)]
    all_to_all x0 -> x1, starting transfers between devices: none -> 5.45 us  [swap(): lax.all_to_all(jnp.stack([value, value]), AXES, 0, 0, tiled=True, axis_in...]
    ppermute x2, waiting for transfers between devices: 18.2 us -> 13.6 us  [reduce_over_dp(): blocks = mine + lax.ppermute(other, 'dp', partner)]
    all_to_all x1, starting transfers between devices: 5.84 us -> 3.82 us  [total_over_devices(): gathered = lax.all_to_all(spread, AXES, 0, 0, tiled=True)]
    select_n x0 -> x2, other arithmetic: none -> 1.38 us  [the longest x1 1.07 us: on_device(): jnp.where(first, near, far)]
  transfers between devices with their start and end apart: 8 -> 9, of which waited for: 4 -> 4; matrix products, arithmetic and copies ran while one was open for 11% -> 14% of each run, Pallas kernels for 0% -> 0%
where the time goes in v5:
time: 138 us; the launch traced here: 137 us
  waiting for transfers between devices  38.5 us (28%)
  blocking collectives  29.7 us (22%)
  starting transfers between devices  21.7 us (16%)
  local copies, waits for them, and re-layouts  20.6 us (15%)
  other arithmetic  18.4 us (13%)
  matrix products  5.86 us (4%)
  between operations  1.76 us (1%)
    all_to_all x1, blocking collectives, on_device(): returned = lax.all_to_all(back, AXES, 0, 0, tiled=True)  29.7 us
    ppermute x2, waiting for transfers between devices, reduce_over_dp(): blocks = mine + lax.ppermute(other, 'dp', partner)  13.6 us
    all_to_all x1, waiting for transfers between devices, on_device(): lax.all_to_all(sent, AXES, 0, 0, tiled=True, axis_index_groups=members)  13.2 us
    all_to_all x1, waiting for transfers between devices, total_over_devices(): gathered = lax.all_to_all(spread, AXES, 0, 0, tiled=True)  11.6 us
    ppermute x2, starting transfers between devices, on_device(): lax.ppermute(group_sums(p, groups), 'freq', across)  5.88 us
    all_to_all x1, starting transfers between devices, swap(): lax.all_to_all(jnp.stack([value, value]), AXES, 0, 0, tiled=True, axis_in...  5.45 us
    another operation x3, local copies, waits for them, and re-layouts, gather(): jnp.stack([lax.dynamic_index_in_dim(cols, 2 * k + c, axis=1, keepdims=Fal...  5.44 us
    add x2, other arithmetic, reduce_over_dp(): blocks = gather(core) + lax.ppermute(gather(1 - core), 'dp', pair)  4.07 us
  transfers between devices with their start and end apart: 9, of which 4 were waited for; matrix products, arithmetic and copies ran while one was open for 14% of the time, Pallas kernels for 0%

profile of v5, /device:TPU:0, one launch (start us, length us, event | category | flops | bytes accessed | tf_op | source)
XLA Modules:
  0.0 137.3 jit_solution(12111130489436254455)
XLA Ops:
  0.0 2.2 %fusion.67 = (f32[27,4,4096]{2,1,0:T(4,128)S(1)}, f32[27,4,4096]{2,1,0:T(4,128)S(1)}) fusion(f32[27,4,8192]{2,1,0:T(4,128)} %bitcast.116), kind=kLoop, calls=%fused_computation.174 | loop fusion | bytes 7077888 | tf_op jit(solution)/shard_map/slice | solution.py:144
  2.3 4.9 %dynamic-slice_bitcast_fusion.1 = (f32[1,27,4096]{2,0,1:T(1,128)S(1)}, f32[1,27,4096]{2,0,1:T(1,128)S(1)}, f32[1,27,4096]{2,0,1:T(1,128)}, f32[1,27,4096]{2,0,1:...) fusion(f32[27,4,4096]{2,1,0:T(4,128)S(1)} %get-tuple-element.38, ...), kind=kLoop, calls=%fused_computation.64 | loop fusion | bytes 7077904 | tf_op jit(solution)/shard_map/stack | solution.py:147
  7.2 1.8 %pad_maximum_fusion.2 = f32[2,27,4096]{2,0,1:T(2,128)} fusion(f32[1,27,4096]{2,0,1:T(1,128)S(1)} %get-tuple-element.69, f32[1,27,4096]{2,0,1:T(1,128)S(1)} %get-tuple-element.68), kind=kLoop, calls=%fused_computation.55 | loop fusion | flops 221184 | bytes 1769472 | tf_op jit(solution)/shard_map/stack | solution.py:147
  8.9 0.5 collective-permute-start
  9.4 1.8 %pad_maximum_fusion.3 = f32[2,27,4096]{2,0,1:T(2,128)} fusion(f32[1,27,4096]{2,0,1:T(1,128)S(1)} %get-tuple-element.44, f32[1,27,4096]{2,0,1:T(1,128)S(1)} %get-tuple-element.43), kind=kLoop, calls=%fused_computation.56 | loop fusion | flops 221184 | bytes 1769472 | tf_op jit(solution)/shard_map/stack | solution.py:147
  12.0 0.7 copy-done.3
  12.7 0.4 stack.157
  13.1 1.0 pad_maximum_fusion.1
  14.2 5.4 %all-to-all-start.1 = ((f32[2,9,8192]{2,1,0:T(8,128)}), f32[2,9,8192]{2,1,0:T(8,128)S(1)}, u32[]{:S(2)}, u32[]{:S(2)}) async-start(f32[2,9,8192]{2,1,0:T(8,128)} %pad_maximum_fusion.1), calls=%async_computation.1 | async-start | bytes 2097152 | tf_op jit(solution)/shard_map/all_to_all | solution.py:201
  19.6 0.3 copy.52
  19.9 0.3 copy.53
  20.3 0.2 negate_select_fusion.2
  20.4 0.6 gather_fusion
  21.0 0.1 copy.51
  21.1 0.6 gather_fusion.1
  21.7 2.4 %maximum_add_fusion.1 = f32[2,27,4096]{2,0,1:T(2,128)S(1)} fusion(f32[2,27,4096]{2,0,1:T(2,128)} %collective-permute-done, f32[1,27,4096]{2,0,1:T(1,128)} %get-tuple-element.67, f32[1,27,4096]{2,0,1:T(1,128)} %get-tuple-element.70), kind=kLoop, calls=%fused_computation.54 | loop fusion | flops 442368 | bytes 2654208 | tf_op jit(solution)/shard_map/add | solution.py:151
  24.0 0.5 constant_dynamic-slice_fusion.1
  24.5 1.6 %collective-permute-start.1 = (f32[1,27,4096]{2,0,1:T(1,128)S(1)}, f32[1,27,4096]{2,0,1:T(1,128)S(1)}, u32[]{:S(2)}, u32[]{:S(2)}) collective-permute-start(f32[1,27,4096]{2,0,1:T(1,128)S(1)} %constant_dynamic-slice_fusion.1), channel_id=1, source_target_pairs={{0,16},{8,24},{16,0},{24,8},{1,17},{9,25},{17,1},{25,9},{2,18},{10... | collective-permute-start | bytes 1327112 | tf_op jit(solution)/shard_map/ppermute | solution.py:160
  26.1 1.7 %maximum_add_fusion = f32[2,27,4096]{2,1,0:T(8,128)S(1)} fusion(f32[1,27,4096]{2,1,0:T(8,128)S(1)} %copy.53, f32[1,27,4096]{2,1,0:T(8,128)S(1)} %copy.52, f32[2,27,4096]{2,0,1:T(2,128)} %collective-permute-done.2), kind=kLoop, calls=%fused_computation.48 | loop fusion | flops 442368 | bytes 2654208 | tf_op jit(solution)/shard_map/add | solution.py:151
  27.9 0.6 collective-permute-start.3
  28.4 9.2 %collective-permute-done.1 = f32[1,27,4096]{2,0,1:T(1,128)S(1)} collective-permute-done((f32[1,27,4096]{2,0,1:T(1,128)S(1)}, f32[1,27,4096]{2,0,1:T(1,128)S(1)}, u32[]{:S(2)}, u32[]{:S(2)}) %collective-permute-start.1) | collective-permute-done | bytes 442400 | tf_op jit(solution)/shard_map/ppermute | solution.py:160
  37.7 0.6 dynamic-slice_add_fusion.1
  38.3 0.1 fusion.51
  38.4 0.7 fusion.53
  39.1 0.3 copy.73
  39.4 1.0 stack.155
  40.3 3.0 %collective-permute-start.4 = (f32[9,4096]{1,0:T(8,128)S(1)}, f32[9,4096]{1,0:T(8,128)}, u32[]{:S(2)}, u32[]{:S(2)}) collective-permute-start(f32[9,4096]{1,0:T(8,128)S(1)} %stack.155), channel_id=1, source_target_pairs={{0,4},{1,5},{2,6},{3,7},{4,0},{5,1},{6,2},{7,3},{8,12},{9,13},{10,... | collective-permute-start | bytes 442376 | tf_op jit(solution)/shard_map/ppermute | solution.py:214
  43.3 4.4 %collective-permute-done.3 = f32[1,27,4096]{2,1,0:T(8,128)} collective-permute-done((f32[1,27,4096]{2,1,0:T(8,128)S(1)}, f32[1,27,4096]{2,1,0:T(8,128)}, u32[]{:S(2)}, u32[]{:S(2)}) %collective-permute-start.3) | collective-permute-done | bytes 442400 | tf_op jit(solution)/shard_map/ppermute | solution.py:160
  47.8 1.1 dynamic-slice_add_fusion
  48.9 0.2 fusion.42
  49.1 0.1 fusion.44
  49.2 0.2 stack.156
  49.4 2.9 %collective-permute-start.5 = (f32[9,4096]{1,0:T(8,128)S(1)}, f32[9,4096]{1,0:T(8,128)S(1)}, u32[]{:S(2)}, u32[]{:S(2)}) collective-permute-start(f32[9,4096]{1,0:T(8,128)S(1)} %stack.156), channel_id=1, source_target_pairs={{0,4},{1,5},{2,6},{3,7},{4,0},{5,1},{6,2},{7,3},{8,12},{9,13},{10,... | collective-permute-start | bytes 442376 | tf_op jit(solution)/shard_map/ppermute | solution.py:214
  52.3 0.9 fusion.37
  53.2 1.2 broadcast_in_dim.28
  54.5 3.8 %all-to-all-start = ((f32[32,1,1]{2,1,0:T(1,128)}), f32[32,1,1]{2,1,0:T(1,128)S(1)}, u32[]{:S(2)}, u32[]{:S(2)}) async-start(f32[32,1,1]{2,1,0:T(1,128)} %broadcast_in_dim.28), calls=%async_computation | async-start | bytes 32768 | tf_op jit(solution)/shard_map/all_to_all | solution.py:167
  58.3 0.1 concatenate.70
  58.5 0.2 copy.56
  58.6 11.6 %all-to-all-done = f32[32,1,1]{2,1,0:T(1,128)S(1)} async-done(((f32[32,1,1]{2,1,0:T(1,128)}), f32[32,1,1]{2,1,0:T(1,128)S(1)}, u32[]{:S(2)}, u32[]{:S(2)}) %all-to-all-start) | async-done | bytes 160 | tf_op jit(solution)/shard_map/all_to_all | solution.py:167
  70.3 0.6 reduce_sum.37
  71.6 1.0 maximum_multiply_fusion.1
  72.6 1.1 broadcast_select_fusion.1
  73.7 0.3 broadcast_select_fusion
  74.0 0.5 pad_maximum_fusion.4
  74.5 0.3 pad.33
  74.9 0.6 copy.64
  75.5 1.8 %convolution_convert_fusion.1 = bf16[32,16384]{1,0:T(8,128)(2,1)S(1)} fusion(f32[9,16384]{1,0:T(8,128)S(1)} %bitcast.111, f32[2,32,9]{2,1,0:T(8,128)S(1)} %bitcast.122, s32[]{:T(128)S(6)} %select_n.167), kind=kOutput, calls=%fused_computation.45 | convolution fusion | flops 57147392 | bytes 2113540 | tf_op jit(solution)/shard_map/dot_general | solution.py:233
  77.3 1.6 %reshape.993 = bf16[16,2,2,8192]{3,2,1,0:T(2,128)(2,1)} reshape(bf16[32,16384]{1,0:T(8,128)(2,1)S(1)} %convolution_convert_fusion.1) | data formatting | bytes 2097152 | tf_op jit(solution)/shard_map/reshape | solution.py:236
  78.9 3.9 %all-to-all-start.2 = ((bf16[16,2,2,8192]{3,2,1,0:T(2,128)(2,1)}), bf16[16,2,2,8192]{3,2,1,0:T(2,128)(2,1)S(1)}, u32[]{:S(2)}, u32[]{:S(2)}) async-start(bf16[16,2,2,8192]{3,2,1,0:T(2,128)(2,1)} %reshape.993), calls=%async_computation.2 | async-start | bytes 2097152 | tf_op jit(solution)/shard_map/all_to_all | solution.py:237
  82.8 0.7 dynamic_slice.41
  84.1 13.2 %all-to-all-done.2 = bf16[16,2,2,8192]{3,2,1,0:T(2,128)(2,1)S(1)} async-done(((bf16[16,2,2,8192]{3,2,1,0:T(2,128)(2,1)}), bf16[16,2,2,8192]{3,2,1,0:T(2,128)(2,1)S(1)}, u32[]{:S(2)}, u32[]{:S(2)}) %all-to-all-start.2) | async-done | bytes 1048608 | tf_op jit(solution)/shard_map/all_to_all | solution.py:237
  97.3 0.8 copy.72
  98.1 0.8 reshape.995
  98.9 5.0 %conditional.1 = (bf16[2,512,512]{2,1,0:T(8,128)(2,1)S(1)}) conditional(s32[]{:T(128)} %bitcast.4, bf16[2,512,512]{2,1,0:T(8,128)(2,1)S(1)} %reshape.995, bf16[2,512,512]{2,1,0:T(8,128)(2,1)S(1)} %reshape.995), branch_computations={%region_2.4_spmd, %region_4.6_spmd} | conditional | flops 2175270912 | bytes 19398728 | solution.py:244
  99.0 1.1 fusion.6
  100.8 0.2 fusion.7
  101.2 1.3 fusion.24
  102.5 1.3 subtract_convert_fusion.1
  103.9 0.1 pad_maximum_fusion
  104.0 0.5 reshape.996
  104.5 1.1 copy.71
  105.6 29.7 %all_to_all.21 = bf16[32,2,8192]{2,1,0:T(2,128)(2,1)S(1)} all-to-all(bf16[32,2,8192]{2,1,0:T(2,128)(2,1)S(1)} %bitcast.115), channel_id=1, replica_groups=mesh['dp'=4,'freq'=8] {'dp','freq'}, dimensions={0} | all-to-all | bytes 2097152 | tf_op jit(solution)/shard_map/all_to_all | solution.py:247
  135.3 0.4 reshape.997
  135.8 1.5 %fusion.36 = f32[27,8192]{1,0:T(8,128)} fusion(bf16[64,8192]{1,0:T(8,128)(2,1)S(1)} %reshape.997, f32[27,64]{1,0:T(8,128)S(1)} %copy-done.5), kind=kOutput, calls=%fused_computation.47 | convolution fusion | flops 170090496 | bytes 1940224 | tf_op jit(solution)/shard_map/dot_general | solution.py:249
  (45 shorter events, 1.2 us)
Async XLA Ops:
  7.2 4.0 %copy-start.2 = (f32[27,8192]{1,0:T(8,128)S(1)}, f32[27,8192]{1,0:T(8,128)}, u32[]{:S(2)}) copy-start(f32[27,8192]{1,0:T(8,128)} %param.13) | copy-start | bytes 2654212
  8.9 12.8 %collective-permute-start = (f32[2,27,4096]{2,0,1:T(2,128)}, f32[2,27,4096]{2,0,1:T(2,128)}, u32[]{:S(2)}, u32[]{:S(2)}) collective-permute-start(f32[2,27,4096]{2,0,1:T(2,128)} %pad_maximum_fusion.2), channel_id=1, source_target_pairs={{0,8},{8,0},{16,24},{24,16},{1,9},{9,1},{17,25},{25,17},{2,10},{10... | collective-permute-start | bytes 2654216 | tf_op jit(solution)/shard_map/ppermute | solution.py:151
  11.1 15.0 %collective-permute-start.2 = (f32[2,27,4096]{2,0,1:T(2,128)}, f32[2,27,4096]{2,0,1:T(2,128)}, u32[]{:S(2)}, u32[]{:S(2)}) collective-permute-start(f32[2,27,4096]{2,0,1:T(2,128)} %pad_maximum_fusion.3), channel_id=1, source_target_pairs={{0,8},{8,0},{16,24},{24,16},{1,9},{9,1},{17,25},{25,17},{2,10},{10... | collective-permute-start | bytes 2654216 | tf_op jit(solution)/shard_map/ppermute | solution.py:151
  12.0 0.7 copy-start.3
  12.7 6.9 %copy-start.1 = (f32[1,27,4096]{2,0,1:T(1,128)S(1)}, f32[1,27,4096]{2,0,1:T(1,128)}, u32[]{:S(2)}) copy-start(f32[1,27,4096]{2,0,1:T(1,128)} %get-tuple-element.46) | copy-start | bytes 1327108
  13.1 6.8 %copy-start = (f32[1,27,4096]{2,0,1:T(1,128)S(1)}, f32[1,27,4096]{2,0,1:T(1,128)}, u32[]{:S(2)}) copy-start(f32[1,27,4096]{2,0,1:T(1,128)} %get-tuple-element.45) | copy-start | bytes 1327108
  14.1 6.1 %copy-start.9 = (s32[64]{0:T(128)S(1)}, s32[64]{0:T(128)}, u32[]{:S(2)}) copy-start(s32[64]{0:T(128)} %constant.313) | copy-start | bytes 772
  14.2 6.1 %copy-start.6 = (pred[64]{0:T(512)(128)(4,1)S(1)}, pred[64]{0:T(512)(128)(4,1)}, u32[]{:S(2)}) copy-start(pred[64]{0:T(512)(128)(4,1)} %constant.263.clone) | copy-start | bytes 196
  14.2 6.1 %copy-start.7 = (s32[64]{0:T(128)S(1)}, s32[64]{0:T(128)}, u32[]{:S(2)}) copy-start(s32[64]{0:T(128)} %constant.285) | copy-start | bytes 772
  14.2 6.1 %copy-start.8 = (s32[64]{0:T(128)S(1)}, s32[64]{0:T(128)}, u32[]{:S(2)}) copy-start(s32[64]{0:T(128)} %constant.306) | copy-start | bytes 772
  14.2 39.1 %all-to-all-start.1 = ((f32[2,9,8192]{2,1,0:T(8,128)}), f32[2,9,8192]{2,1,0:T(8,128)S(1)}, u32[]{:S(2)}, u32[]{:S(2)}) async-start(f32[2,9,8192]{2,1,0:T(8,128)} %pad_maximum_fusion.1), calls=%async_computation.1 | async-start | bytes 2097152 | tf_op jit(solution)/shard_map/all_to_all | solution.py:201
  24.5 13.1 %collective-permute-start.1 = (f32[1,27,4096]{2,0,1:T(1,128)S(1)}, f32[1,27,4096]{2,0,1:T(1,128)S(1)}, u32[]{:S(2)}, u32[]{:S(2)}) collective-permute-start(f32[1,27,4096]{2,0,1:T(1,128)S(1)} %constant_dynamic-slice_fusion.1), channel_id=1, source_target_pairs={{0,16},{8,24},{16,0},{24,8},{1,17},{9,25},{17,1},{25,9},{2,18},{10... | collective-permute-start | bytes 1327112 | tf_op jit(solution)/shard_map/ppermute | solution.py:160
  27.9 19.9 %collective-permute-start.3 = (f32[1,27,4096]{2,1,0:T(8,128)S(1)}, f32[1,27,4096]{2,1,0:T(8,128)}, u32[]{:S(2)}, u32[]{:S(2)}) collective-permute-start(f32[1,27,4096]{2,1,0:T(8,128)S(1)} %constant_dynamic-slice_fusion), channel_id=1, source_target_pairs={{0,16},{8,24},{16,0},{24,8},{1,17},{9,25},{17,1},{25,9},{2,18},{10... | collective-permute-start | bytes 1327112 | tf_op jit(solution)/shard_map/ppermute | solution.py:160
  40.3 31.3 %collective-permute-start.4 = (f32[9,4096]{1,0:T(8,128)S(1)}, f32[9,4096]{1,0:T(8,128)}, u32[]{:S(2)}, u32[]{:S(2)}) collective-permute-start(f32[9,4096]{1,0:T(8,128)S(1)} %stack.155), channel_id=1, source_target_pairs={{0,4},{1,5},{2,6},{3,7},{4,0},{5,1},{6,2},{7,3},{8,12},{9,13},{10,... | collective-permute-start | bytes 442376 | tf_op jit(solution)/shard_map/ppermute | solution.py:214
  49.4 23.2 %copy-start.4 = (f32[9,1,8192]{2,1,0:T(1,128)S(1)}, f32[9,1,8192]{2,1,0:T(1,128)}, u32[]{:S(2)}) copy-start(f32[9,1,8192]{2,1,0:T(1,128)} %copy-done.3) | copy-start | bytes 884740
  49.4 22.2 %collective-permute-start.5 = (f32[9,4096]{1,0:T(8,128)S(1)}, f32[9,4096]{1,0:T(8,128)S(1)}, u32[]{:S(2)}, u32[]{:S(2)}) collective-permute-start(f32[9,4096]{1,0:T(8,128)S(1)} %stack.156), channel_id=1, source_target_pairs={{0,4},{1,5},{2,6},{3,7},{4,0},{5,1},{6,2},{7,3},{8,12},{9,13},{10,... | collective-permute-start | bytes 442376 | tf_op jit(solution)/shard_map/ppermute | solution.py:214
  54.5 15.8 %all-to-all-start = ((f32[32,1,1]{2,1,0:T(1,128)}), f32[32,1,1]{2,1,0:T(1,128)S(1)}, u32[]{:S(2)}, u32[]{:S(2)}) async-start(f32[32,1,1]{2,1,0:T(1,128)} %broadcast_in_dim.28), calls=%async_computation | async-start | bytes 32768 | tf_op jit(solution)/shard_map/all_to_all | solution.py:167
  77.3 5.5 %copy-start.10 = (s32[32]{0:T(128)S(1)}, s32[32]{0:T(128)}, u32[]{:S(2)}) copy-start(s32[32]{0:T(128)} %constant.267.clone) | copy-start | bytes 388
  78.9 18.4 %all-to-all-start.2 = ((bf16[16,2,2,8192]{3,2,1,0:T(2,128)(2,1)}), bf16[16,2,2,8192]{3,2,1,0:T(2,128)(2,1)S(1)}, u32[]{:S(2)}, u32[]{:S(2)}) async-start(bf16[16,2,2,8192]{3,2,1,0:T(2,128)(2,1)} %reshape.993), calls=%async_computation.2 | async-start | bytes 2097152 | tf_op jit(solution)/shard_map/all_to_all | solution.py:237
  105.6 30.1 %copy-start.5 = (f32[27,64]{1,0:T(8,128)S(1)}, f32[27,64]{1,0:T(8,128)}, u32[]{:S(2)}) copy-start(f32[27,64]{1,0:T(8,128)} %constant.268.clone) | copy-start | bytes 20740

commit v6 on v3

--- a/solution.py
+++ b/solution.py
@@ -126,7 +126,8 @@
 
 def reduce_over_dp(grad_parts, own_width, pieces=2):
     devices_dp = lax.axis_size("dp")
-    if devices_dp % 2 or own_width % (128 * pieces):
+    half = own_width // 2
+    if devices_dp % 2 or half % (128 * pieces):
         return lax.psum_scatter(grad_parts[0], "dp", scatter_dimension=1, tiled=True).reshape(
             TAPS, own_width
         )
@@ -135,29 +136,31 @@
     chip = d // 2
     chips = devices_dp // 2
     parts = grad_parts[0]
-    piece = own_width // pieces
+    piece = half // pieces
     pair = [(i, i ^ 1) for i in range(devices_dp)]
-    outs = []
+    mine, theirs = [], []
     for p in range(pieces):
-        cols = parts[:, :, p * piece:(p + 1) * piece]
-
-        def gather(c):
-            return jnp.stack(
-                [lax.dynamic_index_in_dim(cols, 2 * k + c, axis=1, keepdims=False) for k in range(chips)]
-            )
-
-        blocks = gather(core) + lax.ppermute(gather(1 - core), "dp", pair)
+        keep = lax.dynamic_slice_in_dim(parts, core * half + p * piece, piece, axis=2)
+        send = lax.dynamic_slice_in_dim(parts, (1 - core) * half + p * piece, piece, axis=2)
+        blocks = (keep + lax.ppermute(send, "dp", pair)).transpose(1, 0, 2)
+        blocks = blocks.reshape(chips, 2, TAPS, piece)
         width = chips
         while width > 1:
             width //= 2
             bit = (chip // width) % 2
-            split = blocks.reshape(2, width, TAPS, piece)
-            mine = lax.dynamic_index_in_dim(split, bit, axis=0, keepdims=False)
-            other = lax.dynamic_index_in_dim(split, 1 - bit, axis=0, keepdims=False)
+            split = blocks.reshape(2, width, 2, TAPS, piece)
+            near = lax.dynamic_index_in_dim(split, bit, axis=0, keepdims=False)
+            far = lax.dynamic_index_in_dim(split, 1 - bit, axis=0, keepdims=False)
             partner = [(i, i ^ (2 * width)) for i in range(devices_dp)]
-            blocks = mine + lax.ppermute(other, "dp", partner)
-        outs.append(blocks.reshape(TAPS, piece))
-    return jnp.concatenate(outs, axis=1)
+            blocks = near + lax.ppermute(far, "dp", partner)
+        blocks = blocks.reshape(2, TAPS, piece)
+        mine.append(lax.dynamic_index_in_dim(blocks, core, axis=0, keepdims=False))
+        theirs.append(
+            lax.ppermute(lax.dynamic_index_in_dim(blocks, 1 - core, axis=0, keepdims=False), "dp", pair)
+        )
+    own = jnp.concatenate(mine, axis=1)
+    other = jnp.concatenate(theirs, axis=1)
+    return jnp.where(core == 0, jnp.concatenate([own, other], axis=1), jnp.concatenate([other, own], axis=1))
 
 
 def total_over_devices(value, devices):

time: 129 us -> 129 us (level)
  waiting for transfers between devices: 53 us -> 57 us
  other arithmetic: 10.2 us -> 6.87 us
  local copies, waits for them, and re-layouts: 15 us -> 13.6 us
    dynamic_slice x0 -> x2, local copies, waits for them, and re-layouts: none -> 3.95 us  [the longest x1 3.03 us: reduce_over_dp(): lax.dynamic_slice_in_dim(parts, (1 - core) * half + p * piece, piece, axi...]
    add x3 -> x2, other arithmetic: 4.44 us -> 0.5 us  [reduce_over_dp(): blocks = near + lax.ppermute(far, 'dp', partner)]
    ppermute x4 -> x6, waiting for transfers between devices: 19.8 us -> 23.7 us  [the longest x2 18.8 us: reduce_over_dp(): blocks = near + lax.ppermute(far, 'dp', partner)]
    transpose x0 -> x1, other arithmetic: none -> 3.27 us  [reduce_over_dp(): blocks = (keep + lax.ppermute(send, 'dp', pair)).transpose(1, 0, 2)]
    another operation x3 -> x2, local copies, waits for them, and re-layouts: 5.43 us -> 2.61 us  [reduce_over_dp(): split = blocks.reshape(2, width, 2, TAPS, piece)]
    another operation x2 -> x0, other arithmetic: 2.59 us -> none  [gather(): jnp.stack([lax.dynamic_index_in_dim(cols, 2 * k + c, axis=1, keepdims=Fal...]
    slice x1 -> x0, local copies, waits for them, and re-layouts: 2.24 us -> none  [reduce_over_dp(): cols = parts[:, :, p * piece:(p + 1) * piece]]
    ppermute x4 -> x6, starting transfers between devices: 3.62 us -> 4.15 us  [the longest x2 3.07 us: reduce_over_dp(): blocks = near + lax.ppermute(far, 'dp', partner)]
  transfers between devices with their start and end apart: 6 -> 8, of which waited for: 5 -> 8; matrix products, arithmetic and copies ran while one was open for 6% -> 1% of each run, Pallas kernels for 0% -> 0%
where the time goes in v6:
time: 129 us
  waiting for transfers between devices  57 us (44%)
  blocking collectives  29.6 us (23%)
  local copies, waits for them, and re-layouts  13.6 us (11%)
  starting transfers between devices  12.9 us (10%)
  other arithmetic  6.87 us (5%)
  matrix products  6.1 us (5%)
  between operations  1.59 us (1%)
    all_to_all x1, blocking collectives, on_device(): returned = lax.all_to_all(back, AXES, 0, 0, tiled=True)  29.6 us
    all_to_all x1, waiting for transfers between devices, on_device(): whole = lax.all_to_all(sent, AXES, 0, 0, tiled=True)  26.3 us
    ppermute x2, waiting for transfers between devices, reduce_over_dp(): blocks = near + lax.ppermute(far, 'dp', partner)  18.8 us
    all_to_all x1, waiting for transfers between devices, total_over_devices(): gathered = lax.all_to_all(spread, AXES, 0, 0, tiled=True)  7.02 us
    all_to_all x1, starting transfers between devices, total_over_devices(): gathered = lax.all_to_all(spread, AXES, 0, 0, tiled=True)  6.07 us
    ppermute x2, waiting for transfers between devices, reduce_over_dp(): blocks = (keep + lax.ppermute(send, 'dp', pair)).transpose(1, 0, 2)  3.6 us
    transpose x1, other arithmetic, reduce_over_dp(): blocks = (keep + lax.ppermute(send, 'dp', pair)).transpose(1, 0, 2)  3.27 us
    ppermute x2, starting transfers between devices, reduce_over_dp(): blocks = near + lax.ppermute(far, 'dp', partner)  3.07 us
  transfers between devices with their start and end apart: 8, of which 8 were waited for; matrix products, arithmetic and copies ran while one was open for 1% of the time, Pallas kernels for 0%

profile of v6, /device:TPU:0, one launch (start us, length us, event | category | flops | bytes accessed | tf_op | source)
XLA Modules:
  0.0 128.7 jit_solution(6141084087803297215)
XLA Ops:
  0.0 0.0 copy-start
  0.0 3.0 %dynamic-slice_bitcast_fusion.1 = (f32[27,4,2048]{2,1,0:T(4,128)}, f32[27,4,2048]{2,1,0:T(4,128)}) fusion(f32[1,27,4,8192]{3,2,1,0:T(4,128)} %param.8, s32[]{:T(128)S(6)} %select_n.136, s32[]{:T(128)S(6)} %select_n.143), kind=kLoop, calls=%fused_computation.56 | loop fusion | bytes 3538952 | tf_op jit(solution)/shard_map/dynamic_slice | solution.py:144
  3.0 0.5 collective-permute-start
  3.5 0.1 collective-permute-start.2
  3.5 2.3 %collective-permute-done = f32[27,4,2048]{2,1,0:T(4,128)} collective-permute-done((f32[27,4,2048]{2,1,0:T(4,128)}, f32[27,4,2048]{2,1,0:T(4,128)}, u32[]{:S(2)}, u32[]{:S(2)}) %collective-permute-start) | collective-permute-done | bytes 884768 | tf_op jit(solution)/shard_map/ppermute | solution.py:145
  5.9 1.3 collective-permute-done.2
  7.1 0.0 copy-done
  7.2 3.3 %fusion.40 = (f32[4,27,2048]{2,0,1:T(4,128)}, f32[4,27,2048]{2,0,1:T(4,128)}) fusion(f32[27,4,2048]{2,1,0:T(4,128)} %collective-permute-done, f32[1,27,4,8192]{3,2,1,0:T(4,128)S(1)} %copy-done, s32[]{:T(128)S(6)} %select_n.135, f32[27,4,2048]{2,1,0:T(4,128)} %collective-permute-done.2, s32[]{:T(128)S(6)} %select_n.142), kind=kLoop, calls=%fused_computation.54 | loop fusion | flops 442368 | bytes 5308424 | tf_op jit(solution)/shard_map/transpose | solution.py:145
  10.4 1.9 %reshape_reshape.6 = f32[2,1,2,27,2048]{4,2,0,3,1:T(2,128)S(1)} reshape(f32[4,27,2048]{2,0,1:T(4,128)} %get-tuple-element.16) | data formatting | bytes 1769472 | tf_op jit(solution)/shard_map/reshape;reshape | solution.py:151
  12.4 3.0 %collective-permute-start.1 = (f32[1,2,27,2048]{3,1,2,0:T(2,128)S(1)}, f32[1,2,27,2048]{3,1,2,0:T(2,128)S(1)}, u32[]{:S(2)}, u32[]{:S(2)}) collective-permute-start(f32[1,2,27,2048]{3,1,2,0:T(2,128)S(1)} %dynamic-slice_bitcast_fusion.3), channel_id=1, source_target_pairs={{0,16},{8,24},{16,0},{24,8},{1,17},{9,25},{17,1},{25,9},{2,18},{10... | collective-permute-start | bytes 1327112 | tf_op jit(solution)/shard_map/ppermute | solution.py:155
  15.4 0.0 copy-done.1
  15.4 0.7 reshape_reshape.7
  16.1 0.1 collective-permute-start.3
  16.2 10.1 %collective-permute-done.1 = f32[1,2,27,2048]{3,1,2,0:T(2,128)S(1)} collective-permute-done((f32[1,2,27,2048]{3,1,2,0:T(2,128)S(1)}, f32[1,2,27,2048]{3,1,2,0:T(2,128)S(1)}, u32[]{:S(2)}, u32[]{:S(2)}) %collective-permute-start.1) | collective-permute-done | bytes 442400 | tf_op jit(solution)/shard_map/ppermute | solution.py:155
  26.3 0.2 bitcast_add_fusion.3
  26.6 8.7 %collective-permute-done.3 = f32[1,2,27,2048]{3,1,2,0:T(2,128)S(1)} collective-permute-done((f32[1,2,27,2048]{3,1,2,0:T(2,128)S(1)}, f32[1,2,27,2048]{3,1,2,0:T(2,128)S(1)}, u32[]{:S(2)}, u32[]{:S(2)}) %collective-permute-start.3) | collective-permute-done | bytes 442400 | tf_op jit(solution)/shard_map/ppermute | solution.py:155
  35.3 0.2 bitcast_add_fusion.2
  35.6 0.0 copy-start.3
  35.6 0.0 copy-start.5
  35.6 0.0 copy-start.6
  35.6 0.0 copy-start.7
  35.6 0.9 constant_dynamic-slice_fusion
  36.5 0.1 copy.30
  36.6 0.1 copy.29
  36.7 0.1 collective-permute-start.5
  36.8 0.5 collective-permute-start.4
  37.3 0.1 copy.32
  37.4 0.1 copy.31
  37.4 0.9 collective-permute-done.5
  38.3 0.4 collective-permute-done.4
  38.7 0.9 multiply_reduce_fusion
  39.6 1.2 broadcast_in_dim.8
  40.8 6.1 %all-to-all-start = ((f32[32,1,1]{2,1,0:T(1,128)}), f32[32,1,1]{2,1,0:T(1,128)S(1)}, u32[]{:S(2)}, u32[]{:S(2)}) async-start(f32[32,1,1]{2,1,0:T(1,128)} %broadcast_in_dim.8), calls=%async_computation | async-start | bytes 32768 | tf_op jit(solution)/shard_map/all_to_all | solution.py:168
  46.9 7.0 %all-to-all-done = f32[32,1,1]{2,1,0:T(1,128)S(1)} async-done(((f32[32,1,1]{2,1,0:T(1,128)}), f32[32,1,1]{2,1,0:T(1,128)S(1)}, u32[]{:S(2)}, u32[]{:S(2)}) %all-to-all-start) | async-done | bytes 160 | tf_op jit(solution)/shard_map/all_to_all | solution.py:168
  53.9 0.6 reduce_sum.37
  55.3 0.0 copy-done.3
  55.3 0.0 copy-done.5
  55.3 0.0 copy-done.6
  55.3 0.0 copy-done.7
  55.3 2.0 %convolution_convert_fusion.1 = bf16[64,8192]{1,0:T(8,128)(2,1)S(1)} fusion(f32[27,8192]{1,0:T(8,128)S(1)} %copy-done.3, f32[]{:T(128)S(6)} %min_shard_map.3, f32[27,2048]{1,0:T(8,128)S(1)} %collective-permute-done.5, f32[27,2048]{1,0:T(8,128)S(1)} %collective-permute-done.4, f32[27,2048]{1,0:T(8,128)S(1)} %bitcast.64, f32[27,2048]{1,0:T(8,128)S(1)} %bitcast.62, ...), kind=kOutput, calls=%fused_computation.43 | convolution fusion | flops 172418816 | bytes 2818845 | tf_op jit(solution)/shard_map/dot_general | solution.py:190
  57.3 0.0 copy-start.4
  57.4 1.5 %reshape.94 = bf16[32,2,8192]{2,1,0:T(2,128)(2,1)} reshape(bf16[64,8192]{1,0:T(8,128)(2,1)S(1)} %convolution_convert_fusion.1) | data formatting | bytes 2097152 | tf_op jit(solution)/shard_map/reshape | solution.py:191
  58.8 2.6 %all-to-all-start.1 = ((bf16[32,2,8192]{2,1,0:T(2,128)(2,1)}), bf16[32,2,8192]{2,1,0:T(2,128)(2,1)S(1)}, u32[]{:S(2)}, u32[]{:S(2)}) async-start(bf16[32,2,8192]{2,1,0:T(2,128)(2,1)} %reshape.94), calls=%async_computation.1 | async-start | bytes 2097152 | tf_op jit(solution)/shard_map/all_to_all | solution.py:192
  61.5 0.0 copy-done.4
  61.5 0.6 dynamic_slice.49
  62.8 26.3 %all-to-all-done.1 = bf16[32,2,8192]{2,1,0:T(2,128)(2,1)S(1)} async-done(((bf16[32,2,8192]{2,1,0:T(2,128)(2,1)}), bf16[32,2,8192]{2,1,0:T(2,128)(2,1)S(1)}, u32[]{:S(2)}, u32[]{:S(2)}) %all-to-all-start.1) | async-done | bytes 1048608 | tf_op jit(solution)/shard_map/all_to_all | solution.py:192
  89.1 0.6 copy.15
  89.7 0.5 reshape.95
  90.2 5.2 %conditional.1 = (bf16[2,512,512]{2,1,0:T(8,128)(2,1)S(1)}) conditional(s32[]{:T(128)} %bitcast.4, bf16[2,512,512]{2,1,0:T(8,128)(2,1)S(1)} %reshape.95, bf16[2,512,512]{2,1,0:T(8,128)(2,1)S(1)} %reshape.95), branch_computations={%region_2.4_spmd, %region_4.6_spmd} | conditional | flops 2175270912 | bytes 19398728 | solution.py:197
  90.4 1.1 fusion.6
  92.3 0.2 fusion.7
  92.5 0.1 slice_bitcast_fusion.3
  92.6 1.3 fusion.24
  93.9 0.1 slice_negate_fusion
  94.0 1.3 subtract_convert_fusion.1
  95.3 0.1 slice_bitcast_fusion.1
  95.3 0.1 pad_maximum_fusion
  95.4 0.5 reshape.96
  96.0 1.1 copy.28
  97.1 0.0 copy-start.2
  97.1 29.6 %all_to_all.16 = bf16[32,2,8192]{2,1,0:T(2,128)(2,1)S(1)} all-to-all(bf16[32,2,8192]{2,1,0:T(2,128)(2,1)S(1)} %bitcast.60), channel_id=1, replica_groups=mesh['dp'=4,'freq'=8] {'dp','freq'}, dimensions={0} | all-to-all | bytes 2097152 | tf_op jit(solution)/shard_map/all_to_all | solution.py:200
  126.7 0.4 reshape.97
  127.1 0.0 copy-done.2
  127.1 1.5 %fusion.36 = f32[27,8192]{1,0:T(8,128)} fusion(bf16[64,8192]{1,0:T(8,128)(2,1)S(1)} %reshape.97, f32[27,64]{1,0:T(8,128)S(1)} %copy-done.2), kind=kOutput, calls=%fused_computation.45 | convolution fusion | flops 170090496 | bytes 1940224 | tf_op jit(solution)/shard_map/dot_general | solution.py:202
  (5 shorter events, 0.1 us)
Async XLA Ops:
  0.0 7.2 %copy-start = (f32[1,27,4,8192]{3,2,1,0:T(4,128)S(1)}, f32[1,27,4,8192]{3,2,1,0:T(4,128)}, u32[]{:S(2)}) copy-start(f32[1,27,4,8192]{3,2,1,0:T(4,128)} %param.8) | copy-start | bytes 10616836
  3.0 2.8 %collective-permute-start = (f32[27,4,2048]{2,1,0:T(4,128)}, f32[27,4,2048]{2,1,0:T(4,128)}, u32[]{:S(2)}, u32[]{:S(2)}) collective-permute-start(f32[27,4,2048]{2,1,0:T(4,128)} %get-tuple-element.18), channel_id=1, source_target_pairs={{0,8},{8,0},{16,24},{24,16},{1,9},{9,1},{17,25},{25,17},{2,10},{10... | collective-permute-start | bytes 2654216 | tf_op jit(solution)/shard_map/ppermute | solution.py:145
  3.5 3.7 %collective-permute-start.2 = (f32[27,4,2048]{2,1,0:T(4,128)}, f32[27,4,2048]{2,1,0:T(4,128)}, u32[]{:S(2)}, u32[]{:S(2)}) collective-permute-start(f32[27,4,2048]{2,1,0:T(4,128)} %get-tuple-element.19), channel_id=1, source_target_pairs={{0,8},{8,0},{16,24},{24,16},{1,9},{9,1},{17,25},{25,17},{2,10},{10... | collective-permute-start | bytes 2654216 | tf_op jit(solution)/shard_map/ppermute | solution.py:145
  10.4 4.9 %copy-start.1 = (f32[4,27,2048]{2,0,1:T(4,128)S(1)}, f32[4,27,2048]{2,0,1:T(4,128)}, u32[]{:S(2)}) copy-start(f32[4,27,2048]{2,0,1:T(4,128)} %get-tuple-element.17) | copy-start | bytes 2654212
  12.4 13.9 %collective-permute-start.1 = (f32[1,2,27,2048]{3,1,2,0:T(2,128)S(1)}, f32[1,2,27,2048]{3,1,2,0:T(2,128)S(1)}, u32[]{:S(2)}, u32[]{:S(2)}) collective-permute-start(f32[1,2,27,2048]{3,1,2,0:T(2,128)S(1)} %dynamic-slice_bitcast_fusion.3), channel_id=1, source_target_pairs={{0,16},{8,24},{16,0},{24,8},{1,17},{9,25},{17,1},{25,9},{2,18},{10... | collective-permute-start | bytes 1327112 | tf_op jit(solution)/shard_map/ppermute | solution.py:155
  16.1 19.2 %collective-permute-start.3 = (f32[1,2,27,2048]{3,1,2,0:T(2,128)S(1)}, f32[1,2,27,2048]{3,1,2,0:T(2,128)S(1)}, u32[]{:S(2)}, u32[]{:S(2)}) collective-permute-start(f32[1,2,27,2048]{3,1,2,0:T(2,128)S(1)} %dynamic-slice_bitcast_fusion.2), channel_id=1, source_target_pairs={{0,16},{8,24},{16,0},{24,8},{1,17},{9,25},{17,1},{25,9},{2,18},{10... | collective-permute-start | bytes 1327112 | tf_op jit(solution)/shard_map/ppermute | solution.py:155
  35.6 19.7 %copy-start.3 = (f32[27,8192]{1,0:T(8,128)S(1)}, f32[27,8192]{1,0:T(8,128)}, u32[]{:S(2)}) copy-start(f32[27,8192]{1,0:T(8,128)} %param.9) | copy-start | bytes 2654212
  35.6 19.7 %copy-start.5 = (s32[64]{0:T(128)S(1)}, s32[64]{0:T(128)}, u32[]{:S(2)}) copy-start(s32[64]{0:T(128)} %constant.273) | copy-start | bytes 772
  35.6 19.7 %copy-start.6 = (s32[64]{0:T(128)S(1)}, s32[64]{0:T(128)}, u32[]{:S(2)}) copy-start(s32[64]{0:T(128)} %constant.252) | copy-start | bytes 772
  35.6 19.7 %copy-start.7 = (pred[64]{0:T(512)(128)(4,1)S(1)}, pred[64]{0:T(512)(128)(4,1)}, u32[]{:S(2)}) copy-start(pred[64]{0:T(512)(128)(4,1)} %constant.233.clone) | copy-start | bytes 196
  36.7 1.6 %collective-permute-start.5 = (f32[27,2048]{1,0:T(8,128)S(1)}, f32[27,2048]{1,0:T(8,128)S(1)}, u32[]{:S(2)}, u32[]{:S(2)}) collective-permute-start(f32[27,2048]{1,0:T(8,128)S(1)} %bitcast.66), channel_id=1, source_target_pairs={{0,8},{8,0},{16,24},{24,16},{1,9},{9,1},{17,25},{25,17},{2,10},{10... | collective-permute-start | bytes 663560 | tf_op jit(solution)/shard_map/ppermute | solution.py:159
  36.8 1.9 %collective-permute-start.4 = (f32[27,2048]{1,0:T(8,128)S(1)}, f32[27,2048]{1,0:T(8,128)S(1)}, u32[]{:S(2)}, u32[]{:S(2)}) collective-permute-start(f32[27,2048]{1,0:T(8,128)S(1)} %bitcast.65), channel_id=1, source_target_pairs={{0,8},{8,0},{16,24},{24,16},{1,9},{9,1},{17,25},{25,17},{2,10},{10... | collective-permute-start | bytes 663560 | tf_op jit(solution)/shard_map/ppermute | solution.py:159
  40.8 13.1 %all-to-all-start = ((f32[32,1,1]{2,1,0:T(1,128)}), f32[32,1,1]{2,1,0:T(1,128)S(1)}, u32[]{:S(2)}, u32[]{:S(2)}) async-start(f32[32,1,1]{2,1,0:T(1,128)} %broadcast_in_dim.8), calls=%async_computation | async-start | bytes 32768 | tf_op jit(solution)/shard_map/all_to_all | solution.py:168
  57.3 4.2 %copy-start.4 = (s32[32]{0:T(128)S(1)}, s32[32]{0:T(128)}, u32[]{:S(2)}) copy-start(s32[32]{0:T(128)} %constant.234.clone) | copy-start | bytes 388
  58.8 30.2 %all-to-all-start.1 = ((bf16[32,2,8192]{2,1,0:T(2,128)(2,1)}), bf16[32,2,8192]{2,1,0:T(2,128)(2,1)S(1)}, u32[]{:S(2)}, u32[]{:S(2)}) async-start(bf16[32,2,8192]{2,1,0:T(2,128)(2,1)} %reshape.94), calls=%async_computation.1 | async-start | bytes 2097152 | tf_op jit(solution)/shard_map/all_to_all | solution.py:192
  97.1 30.1 %copy-start.2 = (f32[27,64]{1,0:T(8,128)S(1)}, f32[27,64]{1,0:T(8,128)}, u32[]{:S(2)}) copy-start(f32[27,64]{1,0:T(8,128)} %constant.235.clone) | copy-start | bytes 20740

commit v7 on v6

--- a/solution.py
+++ b/solution.py
@@ -124,10 +124,16 @@
     return (1.5 * scaled.astype(jnp.float32) - 0.5 * product).astype(jnp.bfloat16)
 
 
-def reduce_over_dp(grad_parts, own_width, pieces=2):
+def piece_widths(width):
+    tiles = width // 128
+    first = max(1, (tiles * 3) // 8)
+    return [first * 128, width - first * 128] if tiles > 1 else [width]
+
+
+def reduce_over_dp(grad_parts, own_width):
     devices_dp = lax.axis_size("dp")
     half = own_width // 2
-    if devices_dp % 2 or half % (128 * pieces):
+    if devices_dp % 2 or half % 128:
         return lax.psum_scatter(grad_parts[0], "dp", scatter_dimension=1, tiled=True).reshape(
             TAPS, own_width
         )
@@ -136,12 +142,13 @@
     chip = d // 2
     chips = devices_dp // 2
     parts = grad_parts[0]
-    piece = half // pieces
     pair = [(i, i ^ 1) for i in range(devices_dp)]
     mine, theirs = [], []
-    for p in range(pieces):
-        keep = lax.dynamic_slice_in_dim(parts, core * half + p * piece, piece, axis=2)
-        send = lax.dynamic_slice_in_dim(parts, (1 - core) * half + p * piece, piece, axis=2)
+    offset = 0
+    for piece in piece_widths(half):
+        keep = lax.dynamic_slice_in_dim(parts, core * half + offset, piece, axis=2)
+        send = lax.dynamic_slice_in_dim(parts, (1 - core) * half + offset, piece, axis=2)
+        offset += piece
         blocks = (keep + lax.ppermute(send, "dp", pair)).transpose(1, 0, 2)
         blocks = blocks.reshape(chips, 2, TAPS, piece)
         width = chips

time: 129 us -> 122 us (0.946)
  waiting for transfers between devices: 57 us -> 50.7 us
  local copies, waits for them, and re-layouts: 13.6 us -> 12.2 us
    ppermute x2, waiting for transfers between devices: 3.6 us -> 0.29 us  [reduce_over_dp(): blocks = (keep + lax.ppermute(send, 'dp', pair)).transpose(1, 0, 2)]
    ppermute x2, waiting for transfers between devices: 18.8 us -> 16.1 us  [reduce_over_dp(): blocks = near + lax.ppermute(far, 'dp', partner)]
    dynamic_slice x1 -> x2, local copies, waits for them, and re-layouts: 3.03 us -> 2.45 us  [reduce_over_dp(): lax.dynamic_slice_in_dim(parts, (1 - core) * half + offset, piece, axis=2)]
    transpose x1 -> x2, other arithmetic: 3.27 us -> 3.13 us  [reduce_over_dp(): blocks = (keep + lax.ppermute(send, 'dp', pair)).transpose(1, 0, 2)]
  transfers between devices with their start and end apart: 8 -> 8, of which waited for: 8 -> 6; matrix products, arithmetic and copies ran while one was open for 1% -> 7% of each run, Pallas kernels for 0% -> 0%
where the time goes in v7:
time: 122 us
  waiting for transfers between devices  50.7 us (42%)
  blocking collectives  29.6 us (24%)
  starting transfers between devices  12.9 us (11%)
  local copies, waits for them, and re-layouts  12.2 us (10%)
  other arithmetic  7.76 us (6%)
  matrix products  6.11 us (5%)
  between operations  1.63 us (1%)
    all_to_all x1, blocking collectives, on_device(): returned = lax.all_to_all(back, AXES, 0, 0, tiled=True)  29.6 us
    all_to_all x1, waiting for transfers between devices, on_device(): whole = lax.all_to_all(sent, AXES, 0, 0, tiled=True)  26.3 us
    ppermute x2, waiting for transfers between devices, reduce_over_dp(): blocks = near + lax.ppermute(far, 'dp', partner)  16.1 us
    all_to_all x1, waiting for transfers between devices, total_over_devices(): gathered = lax.all_to_all(spread, AXES, 0, 0, tiled=True)  7.02 us
    all_to_all x1, starting transfers between devices, total_over_devices(): gathered = lax.all_to_all(spread, AXES, 0, 0, tiled=True)  6.06 us
    transpose x2, other arithmetic, reduce_over_dp(): blocks = (keep + lax.ppermute(send, 'dp', pair)).transpose(1, 0, 2)  3.13 us
    ppermute x2, starting transfers between devices, reduce_over_dp(): blocks = near + lax.ppermute(far, 'dp', partner)  2.96 us
    all_to_all x1, starting transfers between devices, on_device(): whole = lax.all_to_all(sent, AXES, 0, 0, tiled=True)  2.65 us
  transfers between devices with their start and end apart: 8, of which 6 were waited for; matrix products, arithmetic and copies ran while one was open for 7% of the time, Pallas kernels for 0%

profile of v7, /device:TPU:0, one launch (start us, length us, event | category | flops | bytes accessed | tf_op | source)
XLA Modules:
  0.0 122.0 jit_solution(3917128504673434260)
XLA Ops:
  0.0 1.1 dynamic-slice_bitcast_fusion.1
  1.1 0.5 collective-permute-start
  1.7 1.3 %dynamic-slice_bitcast_fusion = f32[27,4,2560]{2,1,0:T(4,128)S(1)} fusion(f32[1,27,4,8192]{3,2,1,0:T(4,128)} %param.8, s32[]{:T(128)S(6)} %select_n.145), kind=kLoop, calls=%fused_computation.48 | loop fusion | bytes 2211844 | tf_op jit(solution)/shard_map/dynamic_slice | solution.py:150
  3.0 0.1 collective-permute-start.2
  3.1 0.3 collective-permute-done
  3.4 1.3 %fusion.40 = f32[4,27,1536]{2,0,1:T(4,128)S(1)} fusion(f32[27,4,1536]{2,1,0:T(4,128)S(1)} %collective-permute-done, f32[1,27,4,8192]{3,2,1,0:T(4,128)} %param.8, s32[]{:T(128)S(6)} %select_n.137), kind=kLoop, calls=%fused_computation.55 | loop fusion | flops 165888 | bytes 1990660 | tf_op jit(solution)/shard_map/transpose | solution.py:152
  4.7 0.5 reshape_reshape.6
  5.2 0.8 dynamic-slice_bitcast_fusion.3
  5.9 2.9 %collective-permute-start.1 = (f32[1,2,27,1536]{3,1,2,0:T(2,128)}, f32[1,2,27,1536]{3,1,2,0:T(2,128)}, u32[]{:S(2)}, u32[]{:S(2)}) collective-permute-start(f32[1,2,27,1536]{3,1,2,0:T(2,128)} %dynamic-slice_bitcast_fusion.3), channel_id=1, source_target_pairs={{0,16},{8,24},{16,0},{24,8},{1,17},{9,25},{17,1},{25,9},{2,18},{10... | collective-permute-start | bytes 995336 | tf_op jit(solution)/shard_map/ppermute | solution.py:162
  8.8 0.0 collective-permute-done.2
  8.8 1.9 %fusion.37 = f32[4,27,2560]{2,0,1:T(4,128)S(1)} fusion(f32[27,4,2560]{2,1,0:T(4,128)} %collective-permute-done.2, f32[1,27,4,8192]{3,2,1,0:T(4,128)} %param.8, s32[]{:T(128)S(6)} %select_n.144), kind=kLoop, calls=%fused_computation.47 | loop fusion | flops 276480 | bytes 3317764 | tf_op jit(solution)/shard_map/transpose | solution.py:152
  10.7 0.9 reshape_reshape.7
  11.6 0.1 collective-permute-start.3
  11.7 6.0 %collective-permute-done.1 = f32[1,2,27,1536]{3,1,2,0:T(2,128)} collective-permute-done((f32[1,2,27,1536]{3,1,2,0:T(2,128)}, f32[1,2,27,1536]{3,1,2,0:T(2,128)}, u32[]{:S(2)}, u32[]{:S(2)}) %collective-permute-start.1) | collective-permute-done | bytes 331808 | tf_op jit(solution)/shard_map/ppermute | solution.py:162
  17.7 1.1 bitcast_add_fusion.3
  18.9 10.1 %collective-permute-done.3 = f32[1,2,27,2560]{3,1,2,0:T(2,128)S(1)} collective-permute-done((f32[1,2,27,2560]{3,1,2,0:T(2,128)S(1)}, f32[1,2,27,2560]{3,1,2,0:T(2,128)S(1)}, u32[]{:S(2)}, u32[]{:S(2)}) %collective-permute-start.3) | collective-permute-done | bytes 552992 | tf_op jit(solution)/shard_map/ppermute | solution.py:162
  29.0 0.4 bitcast_add_fusion.2
  29.3 0.5 constant_dynamic-slice_fusion.3
  29.8 0.0 copy-start.1
  29.8 0.0 copy-start.3
  29.9 0.0 copy-start.4
  29.9 0.0 copy-start.5
  29.9 0.1 collective-permute-start.5
  30.0 0.3 constant_dynamic-slice_fusion
  30.3 0.6 collective-permute-start.4
  30.9 1.0 collective-permute-done.4
  31.9 0.0 collective-permute-done.5
  31.9 0.9 multiply_reduce_fusion
  32.9 1.2 %broadcast_in_dim.8 = f32[32,1,1]{2,1,0:T(1,128)} broadcast(f32[]{:T(128)} %multiply_reduce_fusion), dimensions={} | broadcast | bytes 132 | tf_op jit(solution)/shard_map/broadcast_in_dim | solution.py:174
  34.1 6.1 %all-to-all-start = ((f32[32,1,1]{2,1,0:T(1,128)}), f32[32,1,1]{2,1,0:T(1,128)S(1)}, u32[]{:S(2)}, u32[]{:S(2)}) async-start(f32[32,1,1]{2,1,0:T(1,128)} %broadcast_in_dim.8), calls=%async_computation | async-start | bytes 32768 | tf_op jit(solution)/shard_map/all_to_all | solution.py:175
  40.2 7.0 %all-to-all-done = f32[32,1,1]{2,1,0:T(1,128)S(1)} async-done(((f32[32,1,1]{2,1,0:T(1,128)}), f32[32,1,1]{2,1,0:T(1,128)S(1)}, u32[]{:S(2)}, u32[]{:S(2)}) %all-to-all-start) | async-done | bytes 160 | tf_op jit(solution)/shard_map/all_to_all | solution.py:175
  47.2 0.6 reduce_sum.37
  48.5 0.0 copy-done.1
  48.6 0.0 copy-done.3
  48.6 0.0 copy-done.4
  48.6 0.0 copy-done.5
  48.6 2.0 %convolution_convert_fusion.1 = bf16[64,8192]{1,0:T(8,128)(2,1)S(1)} fusion(f32[27,8192]{1,0:T(8,128)S(1)} %copy-done.1, f32[]{:T(128)S(6)} %min_shard_map.3, f32[27,2560]{1,0:T(8,128)S(1)} %collective-permute-done.5, f32[27,1536]{1,0:T(8,128)S(1)} %collective-permute-done.4, f32[27,2560]{1,0:T(8,128)S(1)} %bitcast.62, f32[27,1536]{1,0:T(8,128)S(1)} %bitcast.64, ...), kind=kOutput, calls=%fused_computation.43 | convolution fusion | flops 172418816 | bytes 2818845 | tf_op jit(solution)/shard_map/dot_general | solution.py:197
  50.6 0.0 copy-start.2
  50.6 1.5 %reshape.94 = bf16[32,2,8192]{2,1,0:T(2,128)(2,1)} reshape(bf16[64,8192]{1,0:T(8,128)(2,1)S(1)} %convolution_convert_fusion.1) | data formatting | bytes 2097152 | tf_op jit(solution)/shard_map/reshape | solution.py:198
  52.1 2.6 %all-to-all-start.1 = ((bf16[32,2,8192]{2,1,0:T(2,128)(2,1)}), bf16[32,2,8192]{2,1,0:T(2,128)(2,1)S(1)}, u32[]{:S(2)}, u32[]{:S(2)}) async-start(bf16[32,2,8192]{2,1,0:T(2,128)(2,1)} %reshape.94), calls=%async_computation.1 | async-start | bytes 2097152 | tf_op jit(solution)/shard_map/all_to_all | solution.py:199
  54.8 0.0 copy-done.2
  54.8 0.7 dynamic_slice.51
  56.1 26.3 %all-to-all-done.1 = bf16[32,2,8192]{2,1,0:T(2,128)(2,1)S(1)} async-done(((bf16[32,2,8192]{2,1,0:T(2,128)(2,1)}), bf16[32,2,8192]{2,1,0:T(2,128)(2,1)S(1)}, u32[]{:S(2)}, u32[]{:S(2)}) %all-to-all-start.1) | async-done | bytes 1048608 | tf_op jit(solution)/shard_map/all_to_all | solution.py:199
  82.4 0.6 copy.15
  82.9 0.5 reshape.95
  83.5 5.2 %conditional.1 = (bf16[2,512,512]{2,1,0:T(8,128)(2,1)S(1)}) conditional(s32[]{:T(128)} %bitcast.4, bf16[2,512,512]{2,1,0:T(8,128)(2,1)S(1)} %reshape.95, bf16[2,512,512]{2,1,0:T(8,128)(2,1)S(1)} %reshape.95), branch_computations={%region_2.4_spmd, %region_4.6_spmd} | conditional | flops 2175270912 | bytes 19398728 | solution.py:204
  83.7 1.1 fusion.6
  85.6 0.2 fusion.7
  85.8 0.1 slice_bitcast_fusion.3
  85.9 1.3 %fusion.24 = bf16[512,1024]{1,0:T(8,128)(2,1)S(1)} fusion(bf16[512,512]{1,0:T(8,128)(2,1)S(1)} %fusion.35, bf16[512,512]{1,0:T(8,128)(2,1)S(1)} %get-tuple-element.15, bf16[512,512]{1,0:T(8,128)(2,1)S(1)} %get-tuple-element.14), kind=kOutput, calls=%fused_computation.27 | convolution fusion | flops 1084751872 | bytes 2621440 | tf_op jit(solution)/shard_map/cond/branch_1_fun/dot_general | solution.py:102
  87.2 0.1 slice_negate_fusion
  87.2 1.3 %subtract_convert_fusion.1 = bf16[512,1024]{1,0:T(8,128)(2,1)S(1)} fusion(bf16[512,512]{1,0:T(8,128)(2,1)S(1)} %get-tuple-element.13, bf16[512,512]{1,0:T(8,128)(2,1)S(1)} %get-tuple-element.12, bf16[512,1024]{1,0:T(8,128)(2,1)S(1)} %fusion.24, bf16[512,512]{1,0:T(8,128)(2,1)S(1)} %get-tuple-element.15, bf16[512,512]{1,0:T(8,128)(2,1)S(1)} %get-tuple-element.14), kind=kOutput, calls=%fused_computation.26 | convolution fusion | flops 1086324736 | bytes 4194304 | tf_op jit(solution)/shard_map/cond/branch_1_fun/dot_general | solution.py:109
  88.5 0.1 slice_bitcast_fusion.1
  88.6 0.1 pad_maximum_fusion
  88.7 0.5 reshape.96
  89.3 1.1 copy.28
  90.3 0.0 copy-start
  90.4 29.6 %all_to_all.16 = bf16[32,2,8192]{2,1,0:T(2,128)(2,1)S(1)} all-to-all(bf16[32,2,8192]{2,1,0:T(2,128)(2,1)S(1)} %bitcast.60), channel_id=1, replica_groups=mesh['dp'=4,'freq'=8] {'dp','freq'}, dimensions={0} | all-to-all | bytes 2097152 | tf_op jit(solution)/shard_map/all_to_all | solution.py:207
  120.0 0.4 reshape.97
  120.4 0.0 copy-done
  120.4 1.5 %fusion.36 = f32[27,8192]{1,0:T(8,128)} fusion(bf16[64,8192]{1,0:T(8,128)(2,1)S(1)} %reshape.97, f32[27,64]{1,0:T(8,128)S(1)} %copy-done), kind=kOutput, calls=%fused_computation.45 | convolution fusion | flops 170090496 | bytes 1940224 | tf_op jit(solution)/shard_map/dot_general | solution.py:209
  (7 shorter events, 0.2 us)
Async XLA Ops:
  1.1 2.3 %collective-permute-start = (f32[27,4,1536]{2,1,0:T(4,128)S(1)}, f32[27,4,1536]{2,1,0:T(4,128)S(1)}, u32[]{:S(2)}, u32[]{:S(2)}) collective-permute-start(f32[27,4,1536]{2,1,0:T(4,128)S(1)} %dynamic-slice_bitcast_fusion.1), channel_id=1, source_target_pairs={{0,8},{8,0},{16,24},{24,16},{1,9},{9,1},{17,25},{25,17},{2,10},{10... | collective-permute-start | bytes 1990664 | tf_op jit(solution)/shard_map/ppermute | solution.py:152
  3.0 5.9 %collective-permute-start.2 = (f32[27,4,2560]{2,1,0:T(4,128)S(1)}, f32[27,4,2560]{2,1,0:T(4,128)}, u32[]{:S(2)}, u32[]{:S(2)}) collective-permute-start(f32[27,4,2560]{2,1,0:T(4,128)S(1)} %dynamic-slice_bitcast_fusion), channel_id=1, source_target_pairs={{0,8},{8,0},{16,24},{24,16},{1,9},{9,1},{17,25},{25,17},{2,10},{10... | collective-permute-start | bytes 3317768 | tf_op jit(solution)/shard_map/ppermute | solution.py:152
  5.9 11.8 %collective-permute-start.1 = (f32[1,2,27,1536]{3,1,2,0:T(2,128)}, f32[1,2,27,1536]{3,1,2,0:T(2,128)}, u32[]{:S(2)}, u32[]{:S(2)}) collective-permute-start(f32[1,2,27,1536]{3,1,2,0:T(2,128)} %dynamic-slice_bitcast_fusion.3), channel_id=1, source_target_pairs={{0,16},{8,24},{16,0},{24,8},{1,17},{9,25},{17,1},{25,9},{2,18},{10... | collective-permute-start | bytes 995336 | tf_op jit(solution)/shard_map/ppermute | solution.py:162
  11.6 17.4 %collective-permute-start.3 = (f32[1,2,27,2560]{3,1,2,0:T(2,128)S(1)}, f32[1,2,27,2560]{3,1,2,0:T(2,128)S(1)}, u32[]{:S(2)}, u32[]{:S(2)}) collective-permute-start(f32[1,2,27,2560]{3,1,2,0:T(2,128)S(1)} %dynamic-slice_bitcast_fusion.2), channel_id=1, source_target_pairs={{0,16},{8,24},{16,0},{24,8},{1,17},{9,25},{17,1},{25,9},{2,18},{10... | collective-permute-start | bytes 1658888 | tf_op jit(solution)/shard_map/ppermute | solution.py:162
  29.8 18.7 %copy-start.1 = (f32[27,8192]{1,0:T(8,128)S(1)}, f32[27,8192]{1,0:T(8,128)}, u32[]{:S(2)}) copy-start(f32[27,8192]{1,0:T(8,128)} %param.9) | copy-start | bytes 2654212
  29.8 18.7 %copy-start.3 = (s32[64]{0:T(128)S(1)}, s32[64]{0:T(128)}, u32[]{:S(2)}) copy-start(s32[64]{0:T(128)} %constant.277) | copy-start | bytes 772
  29.9 18.7 %copy-start.4 = (s32[64]{0:T(128)S(1)}, s32[64]{0:T(128)}, u32[]{:S(2)}) copy-start(s32[64]{0:T(128)} %constant.256) | copy-start | bytes 772
  29.9 18.7 %copy-start.5 = (pred[64]{0:T(512)(128)(4,1)S(1)}, pred[64]{0:T(512)(128)(4,1)}, u32[]{:S(2)}) copy-start(pred[64]{0:T(512)(128)(4,1)} %constant.237.clone) | copy-start | bytes 196
  29.9 2.0 %collective-permute-start.5 = (f32[27,2560]{1,0:T(8,128)S(1)}, f32[27,2560]{1,0:T(8,128)S(1)}, u32[]{:S(2)}, u32[]{:S(2)}) collective-permute-start(f32[27,2560]{1,0:T(8,128)S(1)} %bitcast.65), channel_id=1, source_target_pairs={{0,8},{8,0},{16,24},{24,16},{1,9},{9,1},{17,25},{25,17},{2,10},{10... | collective-permute-start | bytes 829448 | tf_op jit(solution)/shard_map/ppermute | solution.py:166
  30.3 1.6 %collective-permute-start.4 = (f32[27,1536]{1,0:T(8,128)S(1)}, f32[27,1536]{1,0:T(8,128)S(1)}, u32[]{:S(2)}, u32[]{:S(2)}) collective-permute-start(f32[27,1536]{1,0:T(8,128)S(1)} %bitcast.66), channel_id=1, source_target_pairs={{0,8},{8,0},{16,24},{24,16},{1,9},{9,1},{17,25},{25,17},{2,10},{10... | collective-permute-start | bytes 497672 | tf_op jit(solution)/shard_map/ppermute | solution.py:166
  34.1 13.1 %all-to-all-start = ((f32[32,1,1]{2,1,0:T(1,128)}), f32[32,1,1]{2,1,0:T(1,128)S(1)}, u32[]{:S(2)}, u32[]{:S(2)}) async-start(f32[32,1,1]{2,1,0:T(1,128)} %broadcast_in_dim.8), calls=%async_computation | async-start | bytes 32768 | tf_op jit(solution)/shard_map/all_to_all | solution.py:175
  50.6 4.2 %copy-start.2 = (s32[32]{0:T(128)S(1)}, s32[32]{0:T(128)}, u32[]{:S(2)}) copy-start(s32[32]{0:T(128)} %constant.238.clone) | copy-start | bytes 388
  52.1 30.2 %all-to-all-start.1 = ((bf16[32,2,8192]{2,1,0:T(2,128)(2,1)}), bf16[32,2,8192]{2,1,0:T(2,128)(2,1)S(1)}, u32[]{:S(2)}, u32[]{:S(2)}) async-start(bf16[32,2,8192]{2,1,0:T(2,128)(2,1)} %reshape.94), calls=%async_computation.1 | async-start | bytes 2097152 | tf_op jit(solution)/shard_map/all_to_all | solution.py:199
  90.3 30.1 %copy-start = (f32[27,64]{1,0:T(8,128)S(1)}, f32[27,64]{1,0:T(8,128)}, u32[]{:S(2)}) copy-start(f32[27,64]{1,0:T(8,128)} %constant.239.clone) | copy-start | bytes 20740

commit v8 on v7

--- a/solution.py
+++ b/solution.py
@@ -134,16 +134,17 @@
     devices_dp = lax.axis_size("dp")
     half = own_width // 2
     if devices_dp % 2 or half % 128:
-        return lax.psum_scatter(grad_parts[0], "dp", scatter_dimension=1, tiled=True).reshape(
+        gradient = lax.psum_scatter(grad_parts[0], "dp", scatter_dimension=1, tiled=True).reshape(
             TAPS, own_width
         )
+        return gradient, jnp.sum(gradient * gradient)
     d = lax.axis_index("dp")
     core = d % 2
     chip = d // 2
     chips = devices_dp // 2
     parts = grad_parts[0]
     pair = [(i, i ^ 1) for i in range(devices_dp)]
-    mine, theirs = [], []
+    mine, theirs, squares = [], [], []
     offset = 0
     for piece in piece_widths(half):
         keep = lax.dynamic_slice_in_dim(parts, core * half + offset, piece, axis=2)
@@ -161,13 +162,17 @@
             partner = [(i, i ^ (2 * width)) for i in range(devices_dp)]
             blocks = near + lax.ppermute(far, "dp", partner)
         blocks = blocks.reshape(2, TAPS, piece)
+        squares.append(jnp.sum(blocks * blocks))
         mine.append(lax.dynamic_index_in_dim(blocks, core, axis=0, keepdims=False))
         theirs.append(
             lax.ppermute(lax.dynamic_index_in_dim(blocks, 1 - core, axis=0, keepdims=False), "dp", pair)
         )
     own = jnp.concatenate(mine, axis=1)
     other = jnp.concatenate(theirs, axis=1)
-    return jnp.where(core == 0, jnp.concatenate([own, other], axis=1), jnp.concatenate([other, own], axis=1))
+    gradient = jnp.where(
+        core == 0, jnp.concatenate([own, other], axis=1), jnp.concatenate([other, own], axis=1)
+    )
+    return gradient, sum(squares)
 
 
 def total_over_devices(value, devices):
@@ -186,8 +191,7 @@
     own_width = kernel.shape[1]
     rows, backward, kinds = slot_plan(total_freq, stride)
 
-    gradient = reduce_over_dp(grad_parts, own_width)
-    local_square = jnp.sum(gradient * gradient)
+    gradient, local_square = reduce_over_dp(grad_parts, own_width)
     summed = total_over_devices(local_square, devices)
     factor = jnp.minimum(1.0, CLIP * math.sqrt(TAPS * C * C) / jnp.sqrt(summed + 1e-06))
     updated = kernel - factor * gradient

time: 122 us -> 122 us (level)
  waiting for transfers between devices: 50.7 us -> 48.9 us
  between operations: 1.63 us -> 2.92 us
    reduce_sum x1 -> x2, other arithmetic: 0.94 us -> 3.15 us  [reduce_over_dp(): squares.append(jnp.sum(blocks * blocks))]
    add x2 -> x0, other arithmetic: 1.5 us -> none  [reduce_over_dp(): blocks = near + lax.ppermute(far, 'dp', partner)]
  transfers between devices with their start and end apart: 8 -> 8, of which waited for: 6 -> 5; matrix products, arithmetic and copies ran while one was open for 7% -> 9% of each run, Pallas kernels for 0% -> 0%
where the time goes in v8:
time: 122 us; the launch traced here: 121 us
  waiting for transfers between devices  48.9 us (40%)
  blocking collectives  29.6 us (24%)
  starting transfers between devices  12.9 us (11%)
  local copies, waits for them, and re-layouts  11.5 us (9%)
  other arithmetic  8.47 us (7%)
  matrix products  6.11 us (5%)
  between operations  2.92 us (2%)
    all_to_all x1, blocking collectives, on_device(): returned = lax.all_to_all(back, AXES, 0, 0, tiled=True)  29.6 us
    all_to_all x1, waiting for transfers between devices, on_device(): whole = lax.all_to_all(sent, AXES, 0, 0, tiled=True)  26.3 us
    ppermute x2, waiting for transfers between devices, reduce_over_dp(): blocks = near + lax.ppermute(far, 'dp', partner)  15.3 us
    all_to_all x1, waiting for transfers between devices, total_over_devices(): gathered = lax.all_to_all(spread, AXES, 0, 0, tiled=True)  6.98 us
    all_to_all x1, starting transfers between devices, total_over_devices(): gathered = lax.all_to_all(spread, AXES, 0, 0, tiled=True)  6.07 us
    reduce_sum x2, other arithmetic, reduce_over_dp(): squares.append(jnp.sum(blocks * blocks))  3.15 us
    transpose x2, other arithmetic, reduce_over_dp(): blocks = (keep + lax.ppermute(send, 'dp', pair)).transpose(1, 0, 2)  3.13 us
    ppermute x2, starting transfers between devices, reduce_over_dp(): blocks = near + lax.ppermute(far, 'dp', partner)  2.96 us
  transfers between devices with their start and end apart: 8, of which 5 were waited for; matrix products, arithmetic and copies ran while one was open for 9% of the time, Pallas kernels for 0%

profile of v8, /device:TPU:0, one launch (start us, length us, event | category | flops | bytes accessed | tf_op | source)
XLA Modules:
  0.0 121.5 jit_solution(10334076093597868054)
XLA Ops:
  0.0 1.1 dynamic-slice_bitcast_fusion.1
  1.1 0.5 collective-permute-start
  1.7 1.3 %dynamic-slice_bitcast_fusion = f32[27,4,2560]{2,1,0:T(4,128)S(1)} fusion(f32[1,27,4,8192]{3,2,1,0:T(4,128)} %param.8, s32[]{:T(128)S(6)} %select_n.143), kind=kLoop, calls=%fused_computation.48 | loop fusion | bytes 2211844 | tf_op jit(solution)/shard_map/dynamic_slice | solution.py:151
  3.0 0.1 collective-permute-start.2
  3.1 0.3 collective-permute-done
  3.4 1.3 %fusion.54 = f32[4,27,1536]{2,0,1:T(4,128)S(1)} fusion(f32[27,4,1536]{2,1,0:T(4,128)S(1)} %collective-permute-done, f32[1,27,4,8192]{3,2,1,0:T(4,128)} %param.8, s32[]{:T(128)S(6)} %select_n.136), kind=kLoop, calls=%fused_computation.67 | loop fusion | flops 165888 | bytes 1990660 | tf_op jit(solution)/shard_map/transpose | solution.py:153
  4.7 0.5 reshape_reshape.6
  5.2 0.8 dynamic-slice_bitcast_fusion.3
  5.9 2.9 %collective-permute-start.1 = (f32[1,2,27,1536]{3,1,2,0:T(2,128)}, f32[1,2,27,1536]{3,1,2,0:T(2,128)}, u32[]{:S(2)}, u32[]{:S(2)}) collective-permute-start(f32[1,2,27,1536]{3,1,2,0:T(2,128)} %dynamic-slice_bitcast_fusion.3), channel_id=1, source_target_pairs={{0,16},{8,24},{16,0},{24,8},{1,17},{9,25},{17,1},{25,9},{2,18},{10... | collective-permute-start | bytes 995336 | tf_op jit(solution)/shard_map/ppermute | solution.py:163
  8.8 0.0 collective-permute-done.2
  8.8 1.9 %fusion.37 = f32[4,27,2560]{2,0,1:T(4,128)S(1)} fusion(f32[27,4,2560]{2,1,0:T(4,128)} %collective-permute-done.2, f32[1,27,4,8192]{3,2,1,0:T(4,128)} %param.8, s32[]{:T(128)S(6)} %select_n.142), kind=kLoop, calls=%fused_computation.47 | loop fusion | flops 276480 | bytes 3317764 | tf_op jit(solution)/shard_map/transpose | solution.py:153
  10.7 0.9 reshape_reshape.7
  11.6 0.1 collective-permute-start.3
  11.7 6.0 %collective-permute-done.1 = f32[1,2,27,1536]{3,1,2,0:T(2,128)} collective-permute-done((f32[1,2,27,1536]{3,1,2,0:T(2,128)}, f32[1,2,27,1536]{3,1,2,0:T(2,128)}, u32[]{:S(2)}, u32[]{:S(2)}) %collective-permute-start.1) | collective-permute-done | bytes 331808 | tf_op jit(solution)/shard_map/ppermute | solution.py:163
  17.7 2.0 %multiply_reduce_fusion.1 = (f32[]{:T(128)}, f32[1,2,27,1536]{3,1,2,0:T(2,128)S(1)}) fusion(f32[1,2,27,1536]{3,1,2,0:T(2,128)} %collective-permute-done.1, f32[2,1,2,27,1536]{4,2,0,3,1:T(2,128)S(1)} %reshape_reshape.6, s32[]{:T(128)S(6)} %select_n.140), kind=kLoop, calls=%fused_computation.75 | loop fusion | flops 248831 | bytes 995336 | tf_op jit(solution)/shard_map/reduce_sum | solution.py:165
  19.7 9.3 %collective-permute-done.3 = f32[1,2,27,2560]{3,1,2,0:T(2,128)S(1)} collective-permute-done((f32[1,2,27,2560]{3,1,2,0:T(2,128)S(1)}, f32[1,2,27,2560]{3,1,2,0:T(2,128)S(1)}, u32[]{:S(2)}, u32[]{:S(2)}) %collective-permute-start.3) | collective-permute-done | bytes 552992 | tf_op jit(solution)/shard_map/ppermute | solution.py:163
  29.0 1.2 multiply_reduce_fusion
  30.2 0.0 copy-start.1
  30.2 0.0 copy-start.3
  30.2 0.0 copy-start.4
  30.2 0.0 copy-start.5
  30.2 0.5 constant_dynamic-slice_fusion.1
  30.7 0.1 collective-permute-start.5
  30.8 0.3 constant_dynamic-slice_fusion.2
  31.1 0.6 collective-permute-start.4
  33.0 0.6 broadcast_in_dim.8
  33.6 6.1 %all-to-all-start = ((f32[32,1,1]{2,1,0:T(1,128)}), f32[32,1,1]{2,1,0:T(1,128)S(1)}, u32[]{:S(2)}, u32[]{:S(2)}) async-start(f32[32,1,1]{2,1,0:T(1,128)} %broadcast_in_dim.8), calls=%async_computation | async-start | bytes 32768 | tf_op jit(solution)/shard_map/all_to_all | solution.py:180
  39.7 7.0 %all-to-all-done = f32[32,1,1]{2,1,0:T(1,128)S(1)} async-done(((f32[32,1,1]{2,1,0:T(1,128)}), f32[32,1,1]{2,1,0:T(1,128)S(1)}, u32[]{:S(2)}, u32[]{:S(2)}) %all-to-all-start) | async-done | bytes 160 | tf_op jit(solution)/shard_map/all_to_all | solution.py:180
  46.7 0.6 reduce_sum.47
  48.0 0.0 collective-permute-done.4
  48.0 0.0 collective-permute-done.5
  48.1 0.0 copy-done.1
  48.1 0.0 copy-done.3
  48.1 0.0 copy-done.4
  48.1 0.0 copy-done.5
  48.1 2.0 %convolution_convert_fusion.1 = bf16[64,8192]{1,0:T(8,128)(2,1)S(1)} fusion(f32[27,8192]{1,0:T(8,128)S(1)} %copy-done.1, f32[27,2560]{1,0:T(8,128)S(1)} %collective-permute-done.5, f32[27,1536]{1,0:T(8,128)S(1)} %collective-permute-done.4, f32[27,2560]{1,0:T(8,128)S(1)} %bitcast.64, f32[27,1536]{1,0:T(8,128)S(1)} %bitcast.66, f32[]{:T(128)S(6)} %min_shard_map.3, ...), kind=kOutput, calls=%fused_computation.43 | convolution fusion | flops 172418816 | bytes 2818845 | tf_op jit(solution)/shard_map/dot_general | solution.py:201
  50.1 0.0 copy-start.2
  50.1 1.5 %reshape.96 = bf16[32,2,8192]{2,1,0:T(2,128)(2,1)} reshape(bf16[64,8192]{1,0:T(8,128)(2,1)S(1)} %convolution_convert_fusion.1) | data formatting | bytes 2097152 | tf_op jit(solution)/shard_map/reshape | solution.py:202
  51.6 2.6 %all-to-all-start.1 = ((bf16[32,2,8192]{2,1,0:T(2,128)(2,1)}), bf16[32,2,8192]{2,1,0:T(2,128)(2,1)S(1)}, u32[]{:S(2)}, u32[]{:S(2)}) async-start(bf16[32,2,8192]{2,1,0:T(2,128)(2,1)} %reshape.96), calls=%async_computation.1 | async-start | bytes 2097152 | tf_op jit(solution)/shard_map/all_to_all | solution.py:203
  54.3 0.0 copy-done.2
  54.3 0.6 dynamic_slice.51
  55.6 26.3 %all-to-all-done.1 = bf16[32,2,8192]{2,1,0:T(2,128)(2,1)S(1)} async-done(((bf16[32,2,8192]{2,1,0:T(2,128)(2,1)}), bf16[32,2,8192]{2,1,0:T(2,128)(2,1)S(1)}, u32[]{:S(2)}, u32[]{:S(2)}) %all-to-all-start.1) | async-done | bytes 1048608 | tf_op jit(solution)/shard_map/all_to_all | solution.py:203
  81.9 0.6 copy.15
  82.5 0.5 reshape.97
  83.0 5.2 %conditional.1 = (bf16[2,512,512]{2,1,0:T(8,128)(2,1)S(1)}) conditional(s32[]{:T(128)} %bitcast.4, bf16[2,512,512]{2,1,0:T(8,128)(2,1)S(1)} %reshape.97, bf16[2,512,512]{2,1,0:T(8,128)(2,1)S(1)} %reshape.97), branch_computations={%region_3.5_spmd, %region_5.7_spmd} | conditional | flops 2175270912 | bytes 19398728 | solution.py:208
  83.2 1.1 fusion.6
  85.1 0.2 fusion.7
  85.3 0.1 slice_bitcast_fusion.3
  85.4 1.3 %fusion.24 = bf16[512,1024]{1,0:T(8,128)(2,1)S(1)} fusion(bf16[512,512]{1,0:T(8,128)(2,1)S(1)} %fusion.35, bf16[512,512]{1,0:T(8,128)(2,1)S(1)} %get-tuple-element.19, bf16[512,512]{1,0:T(8,128)(2,1)S(1)} %get-tuple-element.18), kind=kOutput, calls=%fused_computation.27 | convolution fusion | flops 1084751872 | bytes 2621440 | tf_op jit(solution)/shard_map/cond/branch_1_fun/dot_general | solution.py:102
  86.7 0.1 slice_negate_fusion
  86.7 1.3 %subtract_convert_fusion.1 = bf16[512,1024]{1,0:T(8,128)(2,1)S(1)} fusion(bf16[512,512]{1,0:T(8,128)(2,1)S(1)} %get-tuple-element.17, bf16[512,512]{1,0:T(8,128)(2,1)S(1)} %get-tuple-element.16, bf16[512,1024]{1,0:T(8,128)(2,1)S(1)} %fusion.24, bf16[512,512]{1,0:T(8,128)(2,1)S(1)} %get-tuple-element.19, bf16[512,512]{1,0:T(8,128)(2,1)S(1)} %get-tuple-element.18), kind=kOutput, calls=%fused_computation.26 | convolution fusion | flops 1086324736 | bytes 4194304 | tf_op jit(solution)/shard_map/cond/branch_1_fun/dot_general | solution.py:109
  88.0 0.1 slice_bitcast_fusion.1
  88.1 0.1 pad_maximum_fusion
  88.2 0.5 reshape.98
  88.8 1.1 copy.28
  89.9 0.0 copy-start
  89.9 29.6 %all_to_all.16 = bf16[32,2,8192]{2,1,0:T(2,128)(2,1)S(1)} all-to-all(bf16[32,2,8192]{2,1,0:T(2,128)(2,1)S(1)} %bitcast.62), channel_id=1, replica_groups=mesh['dp'=4,'freq'=8] {'dp','freq'}, dimensions={0} | all-to-all | bytes 2097152 | tf_op jit(solution)/shard_map/all_to_all | solution.py:211
  119.5 0.4 reshape.99
  119.9 0.0 copy-done
  119.9 1.5 %fusion.36 = f32[27,8192]{1,0:T(8,128)} fusion(bf16[64,8192]{1,0:T(8,128)(2,1)S(1)} %reshape.99, f32[27,64]{1,0:T(8,128)S(1)} %copy-done), kind=kOutput, calls=%fused_computation.45 | convolution fusion | flops 170090496 | bytes 1940224 | tf_op jit(solution)/shard_map/dot_general | solution.py:213
  (7 shorter events, 0.2 us)
Async XLA Ops:
  1.1 2.3 %collective-permute-start = (f32[27,4,1536]{2,1,0:T(4,128)S(1)}, f32[27,4,1536]{2,1,0:T(4,128)S(1)}, u32[]{:S(2)}, u32[]{:S(2)}) collective-permute-start(f32[27,4,1536]{2,1,0:T(4,128)S(1)} %dynamic-slice_bitcast_fusion.1), channel_id=1, source_target_pairs={{0,8},{8,0},{16,24},{24,16},{1,9},{9,1},{17,25},{25,17},{2,10},{10... | collective-permute-start | bytes 1990664 | tf_op jit(solution)/shard_map/ppermute | solution.py:153
  3.0 5.9 %collective-permute-start.2 = (f32[27,4,2560]{2,1,0:T(4,128)S(1)}, f32[27,4,2560]{2,1,0:T(4,128)}, u32[]{:S(2)}, u32[]{:S(2)}) collective-permute-start(f32[27,4,2560]{2,1,0:T(4,128)S(1)} %dynamic-slice_bitcast_fusion), channel_id=1, source_target_pairs={{0,8},{8,0},{16,24},{24,16},{1,9},{9,1},{17,25},{25,17},{2,10},{10... | collective-permute-start | bytes 3317768 | tf_op jit(solution)/shard_map/ppermute | solution.py:153
  5.9 11.8 %collective-permute-start.1 = (f32[1,2,27,1536]{3,1,2,0:T(2,128)}, f32[1,2,27,1536]{3,1,2,0:T(2,128)}, u32[]{:S(2)}, u32[]{:S(2)}) collective-permute-start(f32[1,2,27,1536]{3,1,2,0:T(2,128)} %dynamic-slice_bitcast_fusion.3), channel_id=1, source_target_pairs={{0,16},{8,24},{16,0},{24,8},{1,17},{9,25},{17,1},{25,9},{2,18},{10... | collective-permute-start | bytes 995336 | tf_op jit(solution)/shard_map/ppermute | solution.py:163
  11.6 17.4 %collective-permute-start.3 = (f32[1,2,27,2560]{3,1,2,0:T(2,128)S(1)}, f32[1,2,27,2560]{3,1,2,0:T(2,128)S(1)}, u32[]{:S(2)}, u32[]{:S(2)}) collective-permute-start(f32[1,2,27,2560]{3,1,2,0:T(2,128)S(1)} %dynamic-slice_bitcast_fusion.2), channel_id=1, source_target_pairs={{0,16},{8,24},{16,0},{24,8},{1,17},{9,25},{17,1},{25,9},{2,18},{10... | collective-permute-start | bytes 1658888 | tf_op jit(solution)/shard_map/ppermute | solution.py:163
  30.2 17.9 %copy-start.1 = (f32[27,8192]{1,0:T(8,128)S(1)}, f32[27,8192]{1,0:T(8,128)}, u32[]{:S(2)}) copy-start(f32[27,8192]{1,0:T(8,128)} %param.9) | copy-start | bytes 2654212
  30.2 17.9 %copy-start.3 = (s32[64]{0:T(128)S(1)}, s32[64]{0:T(128)}, u32[]{:S(2)}) copy-start(s32[64]{0:T(128)} %constant.277) | copy-start | bytes 772
  30.2 17.9 %copy-start.4 = (s32[64]{0:T(128)S(1)}, s32[64]{0:T(128)}, u32[]{:S(2)}) copy-start(s32[64]{0:T(128)} %constant.256) | copy-start | bytes 772
  30.2 17.9 %copy-start.5 = (pred[64]{0:T(512)(128)(4,1)S(1)}, pred[64]{0:T(512)(128)(4,1)}, u32[]{:S(2)}) copy-start(pred[64]{0:T(512)(128)(4,1)} %constant.237.clone) | copy-start | bytes 196
  30.7 17.3 %collective-permute-start.5 = (f32[27,2560]{1,0:T(8,128)S(1)}, f32[27,2560]{1,0:T(8,128)S(1)}, u32[]{:S(2)}, u32[]{:S(2)}) collective-permute-start(f32[27,2560]{1,0:T(8,128)S(1)} %bitcast.63), channel_id=1, source_target_pairs={{0,8},{8,0},{16,24},{24,16},{1,9},{9,1},{17,25},{25,17},{2,10},{10... | collective-permute-start | bytes 829448 | tf_op jit(solution)/shard_map/ppermute | solution.py:168
  31.1 16.9 %collective-permute-start.4 = (f32[27,1536]{1,0:T(8,128)S(1)}, f32[27,1536]{1,0:T(8,128)S(1)}, u32[]{:S(2)}, u32[]{:S(2)}) collective-permute-start(f32[27,1536]{1,0:T(8,128)S(1)} %bitcast.65), channel_id=1, source_target_pairs={{0,8},{8,0},{16,24},{24,16},{1,9},{9,1},{17,25},{25,17},{2,10},{10... | collective-permute-start | bytes 497672 | tf_op jit(solution)/shard_map/ppermute | solution.py:168
  33.6 13.1 %all-to-all-start = ((f32[32,1,1]{2,1,0:T(1,128)}), f32[32,1,1]{2,1,0:T(1,128)S(1)}, u32[]{:S(2)}, u32[]{:S(2)}) async-start(f32[32,1,1]{2,1,0:T(1,128)} %broadcast_in_dim.8), calls=%async_computation | async-start | bytes 32768 | tf_op jit(solution)/shard_map/all_to_all | solution.py:180
  50.1 4.2 %copy-start.2 = (s32[32]{0:T(128)S(1)}, s32[32]{0:T(128)}, u32[]{:S(2)}) copy-start(s32[32]{0:T(128)} %constant.238.clone) | copy-start | bytes 388
  51.6 30.2 %all-to-all-start.1 = ((bf16[32,2,8192]{2,1,0:T(2,128)(2,1)}), bf16[32,2,8192]{2,1,0:T(2,128)(2,1)S(1)}, u32[]{:S(2)}, u32[]{:S(2)}) async-start(bf16[32,2,8192]{2,1,0:T(2,128)(2,1)} %reshape.96), calls=%async_computation.1 | async-start | bytes 2097152 | tf_op jit(solution)/shard_map/all_to_all | solution.py:203
  89.9 30.1 %copy-start = (f32[27,64]{1,0:T(8,128)S(1)}, f32[27,64]{1,0:T(8,128)}, u32[]{:S(2)}) copy-start(f32[27,64]{1,0:T(8,128)} %constant.239.clone) | copy-start | bytes 20740

commit v9 on v8

--- a/solution.py
+++ b/solution.py
@@ -130,18 +130,32 @@
     return [first * 128, width - first * 128] if tiles > 1 else [width]
 
 
-def reduce_over_dp(grad_parts, own_width):
+def tap_groups(total_freq, stride):
+    turns = turns_of(np.arange(total_freq), stride)
+    groups = {}
+    for t in range(TAPS):
+        groups.setdefault(tuple(turns[:, t]), []).append(t)
+    return list(groups.values())
+
+
+def group_sums(field, groups, axis=0):
+    taps = [lax.index_in_dim(field, t, axis=axis, keepdims=False) for t in range(TAPS)]
+    return jnp.stack([sum(taps[t] for t in group) for group in groups], axis=axis)
+
+
+def reduce_over_dp(grad_parts, own_width, groups):
     devices_dp = lax.axis_size("dp")
     half = own_width // 2
     if devices_dp % 2 or half % 128:
         gradient = lax.psum_scatter(grad_parts[0], "dp", scatter_dimension=1, tiled=True).reshape(
             TAPS, own_width
         )
-        return gradient, jnp.sum(gradient * gradient)
+        return group_sums(gradient, groups), jnp.sum(gradient * gradient)
     d = lax.axis_index("dp")
     core = d % 2
     chip = d // 2
     chips = devices_dp // 2
+    narrow = chips == 2 and 2 * len(groups) + TAPS < 2 * TAPS
     parts = grad_parts[0]
     pair = [(i, i ^ 1) for i in range(devices_dp)]
     mine, theirs, squares = [], [], []
@@ -152,27 +166,38 @@
         offset += piece
         blocks = (keep + lax.ppermute(send, "dp", pair)).transpose(1, 0, 2)
         blocks = blocks.reshape(chips, 2, TAPS, piece)
-        width = chips
-        while width > 1:
-            width //= 2
-            bit = (chip // width) % 2
-            split = blocks.reshape(2, width, 2, TAPS, piece)
-            near = lax.dynamic_index_in_dim(split, bit, axis=0, keepdims=False)
-            far = lax.dynamic_index_in_dim(split, 1 - bit, axis=0, keepdims=False)
-            partner = [(i, i ^ (2 * width)) for i in range(devices_dp)]
-            blocks = near + lax.ppermute(far, "dp", partner)
-        blocks = blocks.reshape(2, TAPS, piece)
-        squares.append(jnp.sum(blocks * blocks))
-        mine.append(lax.dynamic_index_in_dim(blocks, core, axis=0, keepdims=False))
+        if narrow:
+            near = lax.dynamic_index_in_dim(blocks, chip, axis=0, keepdims=False)
+            far = lax.dynamic_index_in_dim(blocks, 1 - chip, axis=0, keepdims=False)
+            partner = [(i, i ^ 2) for i in range(devices_dp)]
+            far_sums = lax.ppermute(group_sums(far, groups, axis=1), "dp", partner)
+            far_taps = lax.ppermute(far.astype(jnp.bfloat16), "dp", partner)
+            sums = group_sums(near, groups, axis=1) + far_sums
+            whole = near + far_taps.astype(jnp.float32)
+            squares.append(jnp.sum(whole * whole))
+        else:
+            width = chips
+            while width > 1:
+                width //= 2
+                bit = (chip // width) % 2
+                split = blocks.reshape(2, width, 2, TAPS, piece)
+                near = lax.dynamic_index_in_dim(split, bit, axis=0, keepdims=False)
+                far = lax.dynamic_index_in_dim(split, 1 - bit, axis=0, keepdims=False)
+                partner = [(i, i ^ (2 * width)) for i in range(devices_dp)]
+                blocks = near + lax.ppermute(far, "dp", partner)
+            blocks = blocks.reshape(2, TAPS, piece)
+            squares.append(jnp.sum(blocks * blocks))
+            sums = group_sums(blocks, groups, axis=1)
+        mine.append(lax.dynamic_index_in_dim(sums, core, axis=0, keepdims=False))
         theirs.append(
-            lax.ppermute(lax.dynamic_index_in_dim(blocks, 1 - core, axis=0, keepdims=False), "dp", pair)
+            lax.ppermute(lax.dynamic_index_in_dim(sums, 1 - core, axis=0, keepdims=False), "dp", pair)
         )
     own = jnp.concatenate(mine, axis=1)
     other = jnp.concatenate(theirs, axis=1)
-    gradient = jnp.where(
+    gradient_sums = jnp.where(
         core == 0, jnp.concatenate([own, other], axis=1), jnp.concatenate([other, own], axis=1)
     )
-    return gradient, sum(squares)
+    return gradient_sums, sum(squares)
 
 
 def total_over_devices(value, devices):
@@ -191,13 +216,15 @@
     own_width = kernel.shape[1]
     rows, backward, kinds = slot_plan(total_freq, stride)
 
-    gradient, local_square = reduce_over_dp(grad_parts, own_width)
+    groups = tap_groups(total_freq, stride)
+    gradient_sums, local_square = reduce_over_dp(grad_parts, own_width, groups)
     summed = total_over_devices(local_square, devices)
     factor = jnp.minimum(1.0, CLIP * math.sqrt(TAPS * C * C) / jnp.sqrt(summed + 1e-06))
-    updated = kernel - factor * gradient
+    updated = group_sums(kernel, groups) - factor * gradient_sums
 
     cosine, sine = tap_phases(jnp.asarray(rows[:, 0]), stride)
     forward = jnp.where(jnp.asarray(rows[:, 1] == 0)[:, None], cosine, -sine)
+    forward = forward[:, np.array([group[0] for group in groups])]
     spectra = jnp.dot(forward, updated, precision=HIGH).astype(jnp.bfloat16)
     sent = spectra.reshape(devices, 2, own_width)
     whole = lax.all_to_all(sent, AXES, 0, 0, tiled=True)

time: 122 us -> 129 us (1.057)
  other arithmetic: 8.47 us -> 11.7 us
  local copies, waits for them, and re-layouts: 11.5 us -> 13.4 us
  starting transfers between devices: 12.9 us -> 14.7 us
    add x0 -> x4, other arithmetic: none -> 1.99 us  [the longest x2 1.83 us: group_sums(): sum((taps[t] for t in group))]
    ppermute x4 -> x6, starting transfers between devices: 3.58 us -> 5.36 us  [the longest x2 4.85 us: reduce_over_dp(): far_taps = lax.ppermute(far.astype(jnp.bfloat16), 'dp', partner)]
    reshape x0 -> x2, local copies, waits for them, and re-layouts: none -> 1.37 us  [reduce_over_dp(): blocks = blocks.reshape(chips, 2, TAPS, piece)]
    ppermute x4 -> x6, waiting for transfers between devices: 15.3 us -> 14.9 us  [the longest x2 12.2 us: reduce_over_dp(): far_taps = lax.ppermute(far.astype(jnp.bfloat16), 'dp', partner)]
  transfers between devices with their start and end apart: 8 -> 10, of which waited for: 5 -> 6; matrix products, arithmetic and copies ran while one was open for 9% -> 13% of each run, Pallas kernels for 0% -> 0%
where the time goes in v9:
time: 129 us; the launch traced here: 128 us
  waiting for transfers between devices  47.7 us (37%)
  blocking collectives  29.6 us (23%)
  starting transfers between devices  14.7 us (11%)
  local copies, waits for them, and re-layouts  13.4 us (10%)
  other arithmetic  11.7 us (9%)
  matrix products  6.9 us (5%)
  between operations  3.16 us (2%)
    all_to_all x1, blocking collectives, on_device(): returned = lax.all_to_all(back, AXES, 0, 0, tiled=True)  29.6 us
    all_to_all x1, waiting for transfers between devices, on_device(): whole = lax.all_to_all(sent, AXES, 0, 0, tiled=True)  26.2 us
    ppermute x2, waiting for transfers between devices, reduce_over_dp(): far_taps = lax.ppermute(far.astype(jnp.bfloat16), 'dp', partner)  12.2 us
    all_to_all x1, waiting for transfers between devices, total_over_devices(): gathered = lax.all_to_all(spread, AXES, 0, 0, tiled=True)  6.53 us
    all_to_all x1, starting transfers between devices, total_over_devices(): gathered = lax.all_to_all(spread, AXES, 0, 0, tiled=True)  6.16 us
    ppermute x2, starting transfers between devices, reduce_over_dp(): far_taps = lax.ppermute(far.astype(jnp.bfloat16), 'dp', partner)  4.85 us
    dynamic_slice x2, local copies, waits for them, and re-layouts, reduce_over_dp(): lax.dynamic_slice_in_dim(parts, (1 - core) * half + offset, piece, axis=2)  3.38 us
    transpose x2, other arithmetic, reduce_over_dp(): blocks = (keep + lax.ppermute(send, 'dp', pair)).transpose(1, 0, 2)  3.27 us
  transfers between devices with their start and end apart: 10, of which 6 were waited for; matrix products, arithmetic and copies ran while one was open for 13% of the time, Pallas kernels for 0%

profile of v9, /device:TPU:0, one launch (start us, length us, event | category | flops | bytes accessed | tf_op | source)
XLA Modules:
  0.0 128.2 jit_solution(3191128068914957987)
XLA Ops:
  0.0 2.1 %dynamic-slice_bitcast_fusion.1 = f32[27,4,1536]{2,1,0:T(4,128)} fusion(f32[1,27,4,8192]{3,2,1,0:T(4,128)} %param.10, s32[]{:T(128)S(6)} %select_n.133), kind=kLoop, calls=%fused_computation.53 | loop fusion | bytes 1327108 | tf_op jit(solution)/shard_map/dynamic_slice | solution.py:165
  2.1 0.5 collective-permute-start
  2.5 1.3 %dynamic-slice_bitcast_fusion = f32[27,4,2560]{2,1,0:T(4,128)S(1)} fusion(f32[1,27,4,8192]{3,2,1,0:T(4,128)} %param.10, s32[]{:T(128)S(6)} %select_n.138), kind=kLoop, calls=%fused_computation.49 | loop fusion | bytes 2211844 | tf_op jit(solution)/shard_map/dynamic_slice | solution.py:165
  3.9 0.1 collective-permute-start.2
  4.0 1.0 slice_add_fusion
  5.0 0.8 slice_add_fusion.1
  5.8 0.6 iota_multiply_fusion
  6.4 0.2 negate_select_fusion.2
  6.6 0.0 collective-permute-done
  6.6 1.5 %fusion.38 = f32[4,27,1536]{2,0,1:T(4,128)S(1)} fusion(f32[27,4,1536]{2,1,0:T(4,128)} %collective-permute-done, f32[1,27,4,8192]{3,2,1,0:T(4,128)} %param.10, s32[]{:T(128)S(6)} %select_n.132), kind=kLoop, calls=%fused_computation.52 | loop fusion | flops 165888 | bytes 1990660 | tf_op jit(solution)/shard_map/transpose | solution.py:167
  8.1 0.5 reshape.90
  8.6 0.2 fusion.65
  9.0 3.0 %collective-permute-start.1 = (bf16[2,27,1536]{2,0,1:T(2,128)(2,1)S(1)}, bf16[2,27,1536]{2,0,1:T(2,128)(2,1)S(1)}, u32[]{:S(2)}, u32[]{:S(2)}) collective-permute-start(bf16[2,27,1536]{2,0,1:T(2,128)(2,1)S(1)} %get-tuple-element.16), channel_id=1, source_target_pairs={{0,16},{8,24},{16,0},{24,8},{1,17},{9,25},{17,1},{25,9},{2,18},{10... | collective-permute-start | bytes 497672 | tf_op jit(solution)/shard_map/ppermute | solution.py:174
  12.0 0.1 collective-permute-start.4
  12.1 4.9 %collective-permute-done.1 = bf16[2,27,1536]{2,0,1:T(2,128)(2,1)S(1)} collective-permute-done((bf16[2,27,1536]{2,0,1:T(2,128)(2,1)S(1)}, bf16[2,27,1536]{2,0,1:T(2,128)(2,1)S(1)}, u32[]{:S(2)}, u32[]{:S(2)}) %collective-permute-start.1) | collective-permute-done | bytes 165920 | tf_op jit(solution)/shard_map/ppermute | solution.py:174
  17.0 1.0 multiply_reduce_fusion.1
  18.3 0.5 collective-permute-done.4
  18.8 0.1 add.599
  18.9 0.7 constant_dynamic-slice_fusion.2
  19.6 0.6 copy.33
  20.2 0.0 collective-permute-start.6
  20.2 0.0 collective-permute-done.2
  20.2 1.8 %fusion.37 = f32[4,27,2560]{2,0,1:T(4,128)S(1)} fusion(f32[27,4,2560]{2,1,0:T(4,128)S(1)} %collective-permute-done.2, f32[1,27,4,8192]{3,2,1,0:T(4,128)} %param.10, s32[]{:T(128)S(6)} %select_n.137), kind=kLoop, calls=%fused_computation.48 | loop fusion | flops 276480 | bytes 3317764 | tf_op jit(solution)/shard_map/transpose | solution.py:167
  22.0 0.9 reshape.91
  22.9 0.3 fusion.64
  23.5 1.8 %collective-permute-start.3 = (bf16[2,27,2560]{2,0,1:T(2,128)(2,1)S(1)}, bf16[2,27,2560]{2,0,1:T(2,128)(2,1)S(1)}, u32[]{:S(2)}, u32[]{:S(2)}) collective-permute-start(bf16[2,27,2560]{2,0,1:T(2,128)(2,1)S(1)} %get-tuple-element.12), channel_id=1, source_target_pairs={{0,16},{8,24},{16,0},{24,8},{1,17},{9,25},{17,1},{25,9},{2,18},{10... | collective-permute-start | bytes 829448 | tf_op jit(solution)/shard_map/ppermute | solution.py:174
  25.4 0.4 collective-permute-start.5
  25.7 7.3 %collective-permute-done.3 = bf16[2,27,2560]{2,0,1:T(2,128)(2,1)S(1)} collective-permute-done((bf16[2,27,2560]{2,0,1:T(2,128)(2,1)S(1)}, bf16[2,27,2560]{2,0,1:T(2,128)(2,1)S(1)}, u32[]{:S(2)}, u32[]{:S(2)}) %collective-permute-start.3) | collective-permute-done | bytes 276512 | tf_op jit(solution)/shard_map/ppermute | solution.py:174
  33.0 1.2 multiply_reduce_fusion
  34.4 2.1 %collective-permute-done.5 = f32[2,9,2560]{2,0,1:T(2,128)S(1)} collective-permute-done((f32[2,9,2560]{2,0,1:T(2,128)S(1)}, f32[2,9,2560]{2,0,1:T(2,128)S(1)}, u32[]{:S(2)}, u32[]{:S(2)}) %collective-permute-start.5) | collective-permute-done | bytes 184352 | tf_op jit(solution)/shard_map/ppermute | solution.py:173
  36.6 0.1 add.637
  36.7 0.2 constant_dynamic-slice_fusion.1
  36.9 0.1 collective-permute-start.7
  37.0 0.6 gather_fusion
  38.8 0.6 broadcast_in_dim.14
  39.4 6.2 %all-to-all-start = ((f32[32,1,1]{2,1,0:T(1,128)}), f32[32,1,1]{2,1,0:T(1,128)S(1)}, u32[]{:S(2)}, u32[]{:S(2)}) async-start(f32[32,1,1]{2,1,0:T(1,128)} %broadcast_in_dim.14), calls=%async_computation | async-start | bytes 32768 | tf_op jit(solution)/shard_map/all_to_all | solution.py:205
  45.6 0.4 stack.16
  46.1 6.5 %all-to-all-done = f32[32,1,1]{2,1,0:T(1,128)S(1)} async-done(((f32[32,1,1]{2,1,0:T(1,128)}), f32[32,1,1]{2,1,0:T(1,128)S(1)}, u32[]{:S(2)}, u32[]{:S(2)}) %all-to-all-start) | async-done | bytes 160 | tf_op jit(solution)/shard_map/all_to_all | solution.py:205
  52.7 0.7 reduce_sum.47
  54.0 0.0 collective-permute-done.6
  54.1 0.0 collective-permute-done.7
  54.1 2.8 %convolution_convert_fusion.1 = bf16[64,8192]{1,0:T(8,128)(2,1)S(1)} fusion(f32[9,64]{1,0:T(8,128)S(1)} %gather_fusion, f32[9,8192]{1,0:T(8,128)S(1)} %stack.16, f32[9,2560]{1,0:T(8,128)S(1)} %collective-permute-done.7, f32[9,1536]{1,0:T(8,128)} %collective-permute-done.6, f32[9,2560]{1,0:T(8,128)S(1)} %bitcast.66, f32[9,1536]{1,0:T(8,128)S(1)} %bitcast.67, ...), kind=kOutput, calls=%fused_computation.44 | convolution fusion | flops 57810944 | bytes 1640709 | tf_op jit(solution)/shard_map/dot_general | solution.py:228
  56.9 0.0 copy-start.16
  56.9 1.5 %reshape.92 = bf16[32,2,8192]{2,1,0:T(2,128)(2,1)} reshape(bf16[64,8192]{1,0:T(8,128)(2,1)S(1)} %convolution_convert_fusion.1) | data formatting | bytes 2097152 | tf_op jit(solution)/shard_map/reshape | solution.py:229
  58.4 2.6 %all-to-all-start.1 = ((bf16[32,2,8192]{2,1,0:T(2,128)(2,1)}), bf16[32,2,8192]{2,1,0:T(2,128)(2,1)S(1)}, u32[]{:S(2)}, u32[]{:S(2)}) async-start(bf16[32,2,8192]{2,1,0:T(2,128)(2,1)} %reshape.92), calls=%async_computation.1 | async-start | bytes 2097152 | tf_op jit(solution)/shard_map/all_to_all | solution.py:230
  61.1 0.6 dynamic_slice.51
  62.4 26.2 %all-to-all-done.1 = bf16[32,2,8192]{2,1,0:T(2,128)(2,1)S(1)} async-done(((bf16[32,2,8192]{2,1,0:T(2,128)(2,1)}), bf16[32,2,8192]{2,1,0:T(2,128)(2,1)S(1)}, u32[]{:S(2)}, u32[]{:S(2)}) %all-to-all-start.1) | async-done | bytes 1048608 | tf_op jit(solution)/shard_map/all_to_all | solution.py:230
  88.6 0.6 copy.17
  89.2 0.5 reshape.93
  89.8 5.2 %conditional.1 = (bf16[2,512,512]{2,1,0:T(8,128)(2,1)S(1)}) conditional(s32[]{:T(128)} %bitcast.4, bf16[2,512,512]{2,1,0:T(8,128)(2,1)S(1)} %reshape.93, bf16[2,512,512]{2,1,0:T(8,128)(2,1)S(1)} %reshape.93), branch_computations={%region_3.5_spmd, %region_5.7_spmd} | conditional | flops 2175270912 | bytes 19398728 | solution.py:235
  90.0 1.1 fusion.6
  91.8 0.2 fusion.7
  92.1 0.1 slice_bitcast_fusion.3
  92.2 1.3 fusion.24
  93.4 0.1 slice_negate_fusion
  93.5 1.3 %subtract_convert_fusion.1 = bf16[512,1024]{1,0:T(8,128)(2,1)S(1)} fusion(bf16[512,512]{1,0:T(8,128)(2,1)S(1)} %get-tuple-element.21, bf16[512,512]{1,0:T(8,128)(2,1)S(1)} %get-tuple-element.20, bf16[512,1024]{1,0:T(8,128)(2,1)S(1)} %fusion.24, bf16[512,512]{1,0:T(8,128)(2,1)S(1)} %get-tuple-element.23, bf16[512,512]{1,0:T(8,128)(2,1)S(1)} %get-tuple-element.22), kind=kOutput, calls=%fused_computation.27 | convolution fusion | flops 1086324736 | bytes 4194304 | tf_op jit(solution)/shard_map/cond/branch_1_fun/dot_general | solution.py:109
  94.8 0.1 slice_bitcast_fusion.1
  94.9 0.1 pad_maximum_fusion
  95.0 0.5 reshape.94
  95.5 1.1 copy.30
  96.6 0.0 copy-start.11
  96.6 29.6 %all_to_all.16 = bf16[32,2,8192]{2,1,0:T(2,128)(2,1)S(1)} all-to-all(bf16[32,2,8192]{2,1,0:T(2,128)(2,1)S(1)} %bitcast.65), channel_id=1, replica_groups=mesh['dp'=4,'freq'=8] {'dp','freq'}, dimensions={0} | all-to-all | bytes 2097152 | tf_op jit(solution)/shard_map/all_to_all | solution.py:238
  126.3 0.4 reshape.95
  126.7 1.5 %fusion.36 = f32[27,8192]{1,0:T(8,128)} fusion(bf16[64,8192]{1,0:T(8,128)(2,1)S(1)} %reshape.95, f32[27,64]{1,0:T(8,128)S(1)} %copy-done.11), kind=kOutput, calls=%fused_computation.46 | convolution fusion | flops 170090496 | bytes 1940224 | tf_op jit(solution)/shard_map/dot_general | solution.py:240
  (74 shorter events, 0.9 us)
Async XLA Ops:
  0.0 4.0 %copy-start = (f32[27,8192]{1,0:T(8,128)S(1)}, f32[27,8192]{1,0:T(8,128)}, u32[]{:S(2)}) copy-start(f32[27,8192]{1,0:T(8,128)} %param.11) | copy-start | bytes 2654212
  0.0 6.4 %copy-start.13 = (s32[64]{0:T(128)S(1)}, s32[64]{0:T(128)}, u32[]{:S(2)}) copy-start(s32[64]{0:T(128)} %constant.266) | copy-start | bytes 772
  0.0 6.4 %copy-start.14 = (s32[64]{0:T(128)S(1)}, s32[64]{0:T(128)}, u32[]{:S(2)}) copy-start(s32[64]{0:T(128)} %constant.245) | copy-start | bytes 772
  0.0 6.4 %copy-start.15 = (pred[64]{0:T(512)(128)(4,1)S(1)}, pred[64]{0:T(512)(128)(4,1)}, u32[]{:S(2)}) copy-start(pred[64]{0:T(512)(128)(4,1)} %constant.224.clone) | copy-start | bytes 196
  2.1 4.5 %collective-permute-start = (f32[27,4,1536]{2,1,0:T(4,128)}, f32[27,4,1536]{2,1,0:T(4,128)}, u32[]{:S(2)}, u32[]{:S(2)}) collective-permute-start(f32[27,4,1536]{2,1,0:T(4,128)} %dynamic-slice_bitcast_fusion.1), channel_id=1, source_target_pairs={{0,8},{8,0},{16,24},{24,16},{1,9},{9,1},{17,25},{25,17},{2,10},{10... | collective-permute-start | bytes 1990664 | tf_op jit(solution)/shard_map/ppermute | solution.py:167
  3.9 16.4 %collective-permute-start.2 = (f32[27,4,2560]{2,1,0:T(4,128)S(1)}, f32[27,4,2560]{2,1,0:T(4,128)S(1)}, u32[]{:S(2)}, u32[]{:S(2)}) collective-permute-start(f32[27,4,2560]{2,1,0:T(4,128)S(1)} %dynamic-slice_bitcast_fusion), channel_id=1, source_target_pairs={{0,8},{8,0},{16,24},{24,16},{1,9},{9,1},{17,25},{25,17},{2,10},{10... | collective-permute-start | bytes 3317768 | tf_op jit(solution)/shard_map/ppermute | solution.py:167
  9.0 8.1 %collective-permute-start.1 = (bf16[2,27,1536]{2,0,1:T(2,128)(2,1)S(1)}, bf16[2,27,1536]{2,0,1:T(2,128)(2,1)S(1)}, u32[]{:S(2)}, u32[]{:S(2)}) collective-permute-start(bf16[2,27,1536]{2,0,1:T(2,128)(2,1)S(1)} %get-tuple-element.16), channel_id=1, source_target_pairs={{0,16},{8,24},{16,0},{24,8},{1,17},{9,25},{17,1},{25,9},{2,18},{10... | collective-permute-start | bytes 497672 | tf_op jit(solution)/shard_map/ppermute | solution.py:174
  12.0 6.8 %collective-permute-start.4 = (f32[2,9,1536]{2,0,1:T(2,128)S(1)}, f32[2,9,1536]{2,0,1:T(2,128)S(1)}, u32[]{:S(2)}, u32[]{:S(2)}) collective-permute-start(f32[2,9,1536]{2,0,1:T(2,128)S(1)} %constant_dynamic-update-slice_fusion.9), channel_id=1, source_target_pairs={{0,16},{8,24},{16,0},{24,8},{1,17},{9,25},{17,1},{25,9},{2,18},{10... | collective-permute-start | bytes 331784 | tf_op jit(solution)/shard_map/ppermute | solution.py:173
  20.2 33.8 %collective-permute-start.6 = (f32[9,1536]{1,0:T(8,128)}, f32[9,1536]{1,0:T(8,128)}, u32[]{:S(2)}, u32[]{:S(2)}) collective-permute-start(f32[9,1536]{1,0:T(8,128)} %bitcast.62), channel_id=1, source_target_pairs={{0,8},{8,0},{16,24},{24,16},{1,9},{9,1},{17,25},{25,17},{2,10},{10... | collective-permute-start | bytes 165896 | tf_op jit(solution)/shard_map/ppermute | solution.py:193
  23.2 13.7 %copy-start.12 = (s32[9]{0:T(128)S(1)}, s32[9]{0:T(128)}, u32[]{:S(2)}) copy-start(s32[9]{0:T(128)} %iota_multiply_fusion) | copy-start | bytes 112
  23.3 22.3 %copy-start.2 = (f32[1,8192]{1,0:T(1,128)S(1)}, f32[1,8192]{1,0:T(1,128)}, u32[]{:S(2)}) copy-start(f32[1,8192]{1,0:T(1,128)} %get-tuple-element.24) | copy-start | bytes 98308
  23.3 22.3 %copy-start.3 = (f32[1,8192]{1,0:T(1,128)S(1)}, f32[1,8192]{1,0:T(1,128)}, u32[]{:S(2)}) copy-start(f32[1,8192]{1,0:T(1,128)} %get-tuple-element.25) | copy-start | bytes 98308
  23.3 22.3 %copy-start.4 = (f32[1,8192]{1,0:T(1,128)S(1)}, f32[1,8192]{1,0:T(1,128)}, u32[]{:S(2)}) copy-start(f32[1,8192]{1,0:T(1,128)} %get-tuple-element.26) | copy-start | bytes 98308
  23.3 22.3 %copy-start.5 = (f32[1,8192]{1,0:T(1,128)S(1)}, f32[1,8192]{1,0:T(1,128)}, u32[]{:S(2)}) copy-start(f32[1,8192]{1,0:T(1,128)} %get-tuple-element.27) | copy-start | bytes 98308
  23.3 22.3 %copy-start.6 = (f32[1,8192]{1,0:T(1,128)S(1)}, f32[1,8192]{1,0:T(1,128)}, u32[]{:S(2)}) copy-start(f32[1,8192]{1,0:T(1,128)} %get-tuple-element.28) | copy-start | bytes 98308
  23.3 22.3 %copy-start.7 = (f32[1,8192]{1,0:T(1,128)S(1)}, f32[1,8192]{1,0:T(1,128)}, u32[]{:S(2)}) copy-start(f32[1,8192]{1,0:T(1,128)} %get-tuple-element.29) | copy-start | bytes 98308
  23.4 22.3 %copy-start.8 = (f32[1,8192]{1,0:T(1,128)S(1)}, f32[1,8192]{1,0:T(1,128)}, u32[]{:S(2)}) copy-start(f32[1,8192]{1,0:T(1,128)} %get-tuple-element.30) | copy-start | bytes 98308
  23.4 22.3 %copy-start.9 = (f32[1,8192]{1,0:T(1,128)S(1)}, f32[1,8192]{1,0:T(1,128)}, u32[]{:S(2)}) copy-start(f32[1,8192]{1,0:T(1,128)} %get-tuple-element.31) | copy-start | bytes 98308
  23.4 22.3 %copy-start.10 = (f32[1,8192]{1,0:T(1,128)S(1)}, f32[1,8192]{1,0:T(1,128)}, u32[]{:S(2)}) copy-start(f32[1,8192]{1,0:T(1,128)} %get-tuple-element.32) | copy-start | bytes 98308
  23.5 9.5 %collective-permute-start.3 = (bf16[2,27,2560]{2,0,1:T(2,128)(2,1)S(1)}, bf16[2,27,2560]{2,0,1:T(2,128)(2,1)S(1)}, u32[]{:S(2)}, u32[]{:S(2)}) collective-permute-start(bf16[2,27,2560]{2,0,1:T(2,128)(2,1)S(1)} %get-tuple-element.12), channel_id=1, source_target_pairs={{0,16},{8,24},{16,0},{24,8},{1,17},{9,25},{17,1},{25,9},{2,18},{10... | collective-permute-start | bytes 829448 | tf_op jit(solution)/shard_map/ppermute | solution.py:174
  25.4 20.7 %copy-start.1 = (f32[1,9,1536]{2,0,1:T(1,128)S(1)}, f32[1,9,1536]{2,0,1:T(1,128)}, u32[]{:S(2)}) copy-start(f32[1,9,1536]{2,0,1:T(1,128)} %get-tuple-element.35) | copy-start | bytes 165892
  25.4 11.2 %collective-permute-start.5 = (f32[2,9,2560]{2,0,1:T(2,128)S(1)}, f32[2,9,2560]{2,0,1:T(2,128)S(1)}, u32[]{:S(2)}, u32[]{:S(2)}) collective-permute-start(f32[2,9,2560]{2,0,1:T(2,128)S(1)} %constant_dynamic-update-slice_fusion.27), channel_id=1, source_target_pairs={{0,16},{8,24},{16,0},{24,8},{1,17},{9,25},{17,1},{25,9},{2,18},{10... | collective-permute-start | bytes 552968 | tf_op jit(solution)/shard_map/ppermute | solution.py:173
  36.9 17.2 %collective-permute-start.7 = (f32[9,2560]{1,0:T(8,128)S(1)}, f32[9,2560]{1,0:T(8,128)S(1)}, u32[]{:S(2)}, u32[]{:S(2)}) collective-permute-start(f32[9,2560]{1,0:T(8,128)S(1)} %bitcast.68), channel_id=1, source_target_pairs={{0,8},{8,0},{16,24},{24,16},{1,9},{9,1},{17,25},{25,17},{2,10},{10... | collective-permute-start | bytes 276488 | tf_op jit(solution)/shard_map/ppermute | solution.py:193
  39.4 13.3 %all-to-all-start = ((f32[32,1,1]{2,1,0:T(1,128)}), f32[32,1,1]{2,1,0:T(1,128)S(1)}, u32[]{:S(2)}, u32[]{:S(2)}) async-start(f32[32,1,1]{2,1,0:T(1,128)} %broadcast_in_dim.14), calls=%async_computation | async-start | bytes 32768 | tf_op jit(solution)/shard_map/all_to_all | solution.py:205
  56.9 4.2 %copy-start.16 = (s32[32]{0:T(128)S(1)}, s32[32]{0:T(128)}, u32[]{:S(2)}) copy-start(s32[32]{0:T(128)} %constant.227.clone) | copy-start | bytes 388
  58.4 30.2 %all-to-all-start.1 = ((bf16[32,2,8192]{2,1,0:T(2,128)(2,1)}), bf16[32,2,8192]{2,1,0:T(2,128)(2,1)S(1)}, u32[]{:S(2)}, u32[]{:S(2)}) async-start(bf16[32,2,8192]{2,1,0:T(2,128)(2,1)} %reshape.92), calls=%async_computation.1 | async-start | bytes 2097152 | tf_op jit(solution)/shard_map/all_to_all | solution.py:230
  96.6 30.1 %copy-start.11 = (f32[27,64]{1,0:T(8,128)S(1)}, f32[27,64]{1,0:T(8,128)}, u32[]{:S(2)}) copy-start(f32[27,64]{1,0:T(8,128)} %constant.228.clone) | copy-start | bytes 20740

commit v10 on v8

--- a/solution.py
+++ b/solution.py
@@ -90,7 +90,16 @@
     return forward, backward, np.array(kinds, np.int32)
 
 
-def polar_complex(values):
+def to_matrix(blocks):
+    return blocks.transpose(1, 0, 2).reshape(2, C, C)
+
+
+def to_blocks(matrix, sources):
+    return matrix.reshape(2, sources, -1).transpose(1, 0, 2)
+
+
+def polar_complex(blocks):
+    values = to_matrix(blocks)
     width = values.shape[-1]
     vals = values.astype(jnp.float32)
     mean_square = jnp.sum(vals * vals) / (2 * width * width)
@@ -108,10 +117,11 @@
     side = jnp.concatenate([real_part, imag_part], axis=1)
     product = jnp.dot(side, blocked, preferred_element_type=jnp.float32)
     result = (1.5 * side.astype(jnp.float32) - 0.5 * product).astype(jnp.bfloat16)
-    return jnp.stack([result[:, :width], result[:, width:]], axis=0)
-
-
-def polar_real(values):
+    return to_blocks(jnp.stack([result[:, :width], result[:, width:]], axis=0), blocks.shape[0])
+
+
+def polar_real(blocks):
+    values = to_matrix(blocks)
     width = values.shape[-1]
     vals = values.astype(jnp.float32)
     mean_square = jnp.sum(vals * vals, axis=(1, 2), keepdims=True) / (2 * width * width)
@@ -121,7 +131,8 @@
         jnp.bfloat16
     )
     product = jnp.einsum("nij,njk->nik", scaled, gram, preferred_element_type=jnp.float32)
-    return (1.5 * scaled.astype(jnp.float32) - 0.5 * product).astype(jnp.bfloat16)
+    result = (1.5 * scaled.astype(jnp.float32) - 0.5 * product).astype(jnp.bfloat16)
+    return to_blocks(result, blocks.shape[0])
 
 
 def piece_widths(width):
@@ -198,19 +209,18 @@
 
     cosine, sine = tap_phases(jnp.asarray(rows[:, 0]), stride)
     forward = jnp.where(jnp.asarray(rows[:, 1] == 0)[:, None], cosine, -sine)
-    spectra = jnp.dot(forward, updated, precision=HIGH).astype(jnp.bfloat16)
-    sent = spectra.reshape(devices, 2, own_width)
+    sent = jnp.einsum(
+        "kpt,tf->kpf", forward.reshape(devices, 2, TAPS), updated, precision=HIGH
+    ).astype(jnp.bfloat16)
     whole = lax.all_to_all(sent, AXES, 0, 0, tiled=True)
-    matrix = whole.transpose(1, 0, 2).reshape(2, C, C)
 
     me = lax.axis_index(AXES)
     is_pair = jnp.asarray(kinds)[me] == 1
-    polar_part = lax.cond(is_pair, polar_complex, polar_real, matrix)
-
-    back = polar_part.reshape(2, devices, own_width).transpose(1, 0, 2)
-    returned = lax.all_to_all(back, AXES, 0, 0, tiled=True)
-    planes = returned.reshape(2 * devices, own_width).astype(jnp.float32)
-    return jnp.dot(jnp.asarray(backward), planes, precision=HIGH) * scale_out
+    back = lax.cond(is_pair, polar_complex, polar_real, whole)
+
+    returned = lax.all_to_all(back, AXES, 0, 0, tiled=True).astype(jnp.float32)
+    weights = jnp.asarray(backward.reshape(TAPS, devices, 2))
+    return jnp.einsum("tkp,kpf->tf", weights, returned, precision=HIGH) * scale_out
 
 
 def solution(mesh):

time: 122 us -> 124 us (1.016)
  blocking collectives: 29.6 us -> 31.5 us
    reshape x5 -> x0, local copies, waits for them, and re-layouts: 4.05 us -> none  [the longest x2 1.61 us: on_device(): back = polar_part.reshape(2, devices, own_width).transpose(1, 0, 2)]
    convert_element_type x0 -> x1, local copies, waits for them, and re-layouts: none -> 2.05 us  [on_device(): sent = jnp.einsum('kpt,tf->kpf', forward.reshape(devices, 2, TAPS), updat...]
    all_to_all x1, blocking collectives: 29.6 us -> 31.5 us  [on_device(): returned = lax.all_to_all(back, AXES, 0, 0, tiled=True).astype(jnp.float32)]
  transfers between devices with their start and end apart: 8 -> 8, of which waited for: 5 -> 5; matrix products, arithmetic and copies ran while one was open for 9% -> 8% of each run, Pallas kernels for 0% -> 0%
where the time goes in v10:
time: 124 us; the launch traced here: 123 us
  waiting for transfers between devices  49.4 us (40%)
  blocking collectives  31.5 us (25%)
  starting transfers between devices  13.2 us (11%)
  local copies, waits for them, and re-layouts  10.4 us (8%)
  other arithmetic  8.23 us (7%)
  matrix products  6.66 us (5%)
  between operations  2.86 us (2%)
    all_to_all x1, blocking collectives, on_device(): returned = lax.all_to_all(back, AXES, 0, 0, tiled=True).astype(jnp.float32)  31.5 us
    all_to_all x1, waiting for transfers between devices, on_device(): whole = lax.all_to_all(sent, AXES, 0, 0, tiled=True)  26.3 us
    ppermute x2, waiting for transfers between devices, reduce_over_dp(): blocks = near + lax.ppermute(far, 'dp', partner)  15.8 us
    all_to_all x1, waiting for transfers between devices, total_over_devices(): gathered = lax.all_to_all(spread, AXES, 0, 0, tiled=True)  6.98 us
    all_to_all x1, starting transfers between devices, total_over_devices(): gathered = lax.all_to_all(spread, AXES, 0, 0, tiled=True)  6.07 us
    transpose x2, other arithmetic, reduce_over_dp(): blocks = (keep + lax.ppermute(send, 'dp', pair)).transpose(1, 0, 2)  3.28 us
    ppermute x2, starting transfers between devices, reduce_over_dp(): blocks = near + lax.ppermute(far, 'dp', partner)  3.27 us
    all_to_all x1, starting transfers between devices, on_device(): whole = lax.all_to_all(sent, AXES, 0, 0, tiled=True)  2.65 us
  transfers between devices with their start and end apart: 8, of which 5 were waited for; matrix products, arithmetic and copies ran while one was open for 8% of the time, Pallas kernels for 0%

profile of v10, /device:TPU:0, one launch (start us, length us, event | category | flops | bytes accessed | tf_op | source)
XLA Modules:
  0.0 123.2 jit_solution(3029916948923562562)
XLA Ops:
  0.0 1.1 dynamic-slice_bitcast_fusion.1
  1.1 0.5 collective-permute-start
  1.7 1.3 %dynamic-slice_bitcast_fusion = f32[27,4,2560]{2,1,0:T(4,128)S(1)} fusion(f32[1,27,4,8192]{3,2,1,0:T(4,128)} %param.8, s32[]{:T(128)S(6)} %select_n.145), kind=kLoop, calls=%fused_computation.41 | loop fusion | bytes 2211844 | tf_op jit(solution)/shard_map/dynamic_slice | solution.py:162
  3.0 0.1 collective-permute-start.2
  3.1 0.3 collective-permute-done
  3.4 1.4 %fusion.46 = f32[4,27,1536]{2,0,1:T(4,128)S(1)} fusion(f32[27,4,1536]{2,1,0:T(4,128)S(1)} %collective-permute-done, f32[1,27,4,8192]{3,2,1,0:T(4,128)} %param.8, s32[]{:T(128)S(6)} %select_n.138), kind=kLoop, calls=%fused_computation.61 | loop fusion | flops 165888 | bytes 1990660 | tf_op jit(solution)/shard_map/transpose | solution.py:164
  4.8 0.5 reshape_reshape.6
  5.4 3.0 %collective-permute-start.1 = (f32[1,2,27,1536]{3,1,2,0:T(2,128)S(1)}, f32[1,2,27,1536]{3,1,2,0:T(2,128)S(1)}, u32[]{:S(2)}, u32[]{:S(2)}) collective-permute-start(f32[1,2,27,1536]{3,1,2,0:T(2,128)S(1)} %dynamic-slice_bitcast_fusion.3), channel_id=1, source_target_pairs={{0,16},{8,24},{16,0},{24,8},{1,17},{9,25},{17,1},{25,9},{2,18},{10... | collective-permute-start | bytes 995336 | tf_op jit(solution)/shard_map/ppermute | solution.py:174
  8.3 0.0 collective-permute-done.2
  8.3 1.9 %fusion.27 = f32[4,27,2560]{2,0,1:T(4,128)S(1)} fusion(f32[27,4,2560]{2,1,0:T(4,128)} %collective-permute-done.2, f32[1,27,4,8192]{3,2,1,0:T(4,128)} %param.8, s32[]{:T(128)S(6)} %select_n.144), kind=kLoop, calls=%fused_computation.40 | loop fusion | flops 276480 | bytes 3317764 | tf_op jit(solution)/shard_map/transpose | solution.py:164
  10.2 0.9 reshape_reshape.7
  11.1 0.3 collective-permute-start.3
  11.4 5.5 %collective-permute-done.1 = f32[1,2,27,1536]{3,1,2,0:T(2,128)S(1)} collective-permute-done((f32[1,2,27,1536]{3,1,2,0:T(2,128)S(1)}, f32[1,2,27,1536]{3,1,2,0:T(2,128)S(1)}, u32[]{:S(2)}, u32[]{:S(2)}) %collective-permute-start.1) | collective-permute-done | bytes 331808 | tf_op jit(solution)/shard_map/ppermute | solution.py:174
  16.9 1.0 multiply_reduce_fusion.1
  17.9 10.4 %collective-permute-done.3 = f32[1,2,27,2560]{3,1,2,0:T(2,128)S(1)} collective-permute-done((f32[1,2,27,2560]{3,1,2,0:T(2,128)S(1)}, f32[1,2,27,2560]{3,1,2,0:T(2,128)S(1)}, u32[]{:S(2)}, u32[]{:S(2)}) %collective-permute-start.3) | collective-permute-done | bytes 552992 | tf_op jit(solution)/shard_map/ppermute | solution.py:174
  28.3 1.2 multiply_reduce_fusion
  29.5 0.0 copy-start.1
  29.5 0.0 copy-start.3
  29.5 0.0 copy-start.4
  29.5 0.0 copy-start.5
  29.5 0.5 constant_dynamic-slice_fusion.1
  30.0 0.1 collective-permute-start.5
  30.1 0.3 constant_dynamic-slice_fusion.2
  30.4 0.6 collective-permute-start.4
  32.3 0.6 broadcast_in_dim.14
  32.9 6.1 %all-to-all-start = ((f32[32,1,1]{2,1,0:T(1,128)}), f32[32,1,1]{2,1,0:T(1,128)S(1)}, u32[]{:S(2)}, u32[]{:S(2)}) async-start(f32[32,1,1]{2,1,0:T(1,128)} %broadcast_in_dim.14), calls=%async_computation | async-start | bytes 32768 | tf_op jit(solution)/shard_map/all_to_all | solution.py:191
  39.0 7.0 %all-to-all-done = f32[32,1,1]{2,1,0:T(1,128)S(1)} async-done(((f32[32,1,1]{2,1,0:T(1,128)}), f32[32,1,1]{2,1,0:T(1,128)S(1)}, u32[]{:S(2)}, u32[]{:S(2)}) %all-to-all-start) | async-done | bytes 160 | tf_op jit(solution)/shard_map/all_to_all | solution.py:191
  46.0 0.6 reduce_sum.47
  47.3 0.0 collective-permute-done.4
  47.3 0.0 collective-permute-done.5
  47.3 0.0 copy-done.1
  47.4 0.0 copy-done.3
  47.4 0.0 copy-done.4
  47.4 0.0 copy-done.5
  47.4 2.0 %convolution_convert_fusion.1 = bf16[32,2,8192]{2,0,1:T(8,128)(2,1)S(1)} fusion(f32[27,8192]{1,0:T(8,128)S(1)} %copy-done.1, f32[27,2560]{1,0:T(8,128)S(1)} %collective-permute-done.5, f32[27,1536]{1,0:T(8,128)S(1)} %collective-permute-done.4, f32[27,2560]{1,0:T(8,128)S(1)} %bitcast.66, f32[27,1536]{1,0:T(8,128)S(1)} %bitcast.68, f32[]{:T(128)S(6)} %min_shard_map.3, ...), kind=kOutput, calls=%fused_computation.35 | convolution fusion | flops 172418816 | bytes 2818845 | tf_op jit(solution)/shard_map/kpt,tf->kpf/dot_general | solution.py:212
  49.4 0.0 copy-start.2
  49.4 2.1 %copy.21 = bf16[32,2,8192]{2,1,0:T(2,128)(2,1)} copy(bf16[32,2,8192]{2,0,1:T(8,128)(2,1)S(1)} %convolution_convert_fusion.1) | data formatting | bytes 2097152 | tf_op jit(solution)/shard_map/convert_element_type | solution.py:214
  51.5 2.6 %all-to-all-start.1 = ((bf16[32,2,8192]{2,1,0:T(2,128)(2,1)}), bf16[32,2,8192]{2,1,0:T(2,128)(2,1)S(1)}, u32[]{:S(2)}, u32[]{:S(2)}) async-start(bf16[32,2,8192]{2,1,0:T(2,128)(2,1)} %copy.21), calls=%async_computation.1 | async-start | bytes 2097152 | tf_op jit(solution)/shard_map/all_to_all | solution.py:215
  54.1 0.0 copy-done.2
  54.1 0.6 dynamic_slice.51
  55.4 26.3 %all-to-all-done.1 = bf16[32,2,8192]{2,1,0:T(2,128)(2,1)S(1)} async-done(((bf16[32,2,8192]{2,1,0:T(2,128)(2,1)}), bf16[32,2,8192]{2,1,0:T(2,128)(2,1)S(1)}, u32[]{:S(2)}, u32[]{:S(2)}) %all-to-all-start.1) | async-done | bytes 1048608 | tf_op jit(solution)/shard_map/all_to_all | solution.py:215
  81.7 6.7 %conditional.1 = (bf16[32,2,8192]{2,0,1:T(8,128)(2,1)S(1)}) conditional(s32[]{:T(128)} %bitcast.4, bf16[32,2,8192]{2,1,0:T(2,128)(2,1)S(1)} %all-to-all-done.1, bf16[32,2,8192]{2,1,0:T(2,128)(2,1)S(1)} %all-to-all-done.1), branch_computations={%region_3.5_spmd, %region_5.7_spmd} | conditional | flops 2167930880 | bytes 26738760 | solution.py:219
  81.7 1.2 fusion.3
  83.6 0.6 fusion.22
  84.2 0.1 fusion.82
  84.3 0.2 squeeze.27
  84.5 0.2 squeeze.26
  84.8 0.2 fusion.83
  85.0 0.1 constant_dynamic-update-slice_fusion.2
  85.1 1.3 %fusion.19 = bf16[512,1024]{1,0:T(8,128)(2,1)S(1)} fusion(bf16[1024,512]{1,0:T(8,128)(2,1)S(1)} %get-tuple-element.23, bf16[512,512]{1,0:T(8,128)(2,1)S(1)} %get-tuple-element.20, bf16[512,512]{1,0:T(8,128)(2,1)S(1)} %squeeze.27), kind=kOutput, calls=%fused_computation.25 | convolution fusion | flops 1080557568 | bytes 3145728 | tf_op jit(solution)/shard_map/cond/branch_1_fun/dot_general | solution.py:111
  86.4 0.1 slice_negate_fusion
  86.4 1.3 %subtract_convert_fusion.1 = bf16[512,1024]{1,0:T(8,128)(2,1)S(1)} fusion(bf16[512,1024]{1,0:T(8,128)(2,1)S(1)} %get-tuple-element.24, bf16[512,512]{1,0:T(8,128)(2,1)S(1)} %get-tuple-element.17, bf16[512,512]{1,0:T(8,128)(2,1)S(1)} %get-tuple-element.16, bf16[512,1024]{1,0:T(8,128)(2,1)S(1)} %fusion.19), kind=kOutput, calls=%fused_computation.24 | convolution fusion | flops 1082654720 | bytes 4194304 | tf_op jit(solution)/shard_map/cond/branch_1_fun/dot_general | solution.py:118
  87.7 0.1 fusion.81
  87.8 0.2 stack.6
  88.1 0.2 stack.7
  88.3 0.1 maximum_bitcast_fusion
  88.4 0.0 copy-start
  88.4 1.1 copy.24
  89.5 31.5 %all_to_all.22 = bf16[32,2,8192]{2,1,0:T(2,128)(2,1)S(1)} all-to-all(bf16[32,2,8192]{2,1,0:T(2,128)(2,1)S(1)} %copy.24), channel_id=1, replica_groups=mesh['dp'=4,'freq'=8] {'dp','freq'}, dimensions={0} | all-to-all | bytes 2097152 | tf_op jit(solution)/shard_map/all_to_all | solution.py:221
  121.1 0.0 copy-done
  121.1 2.1 %fusion.26 = f32[27,8192]{1,0:T(8,128)} fusion(f32[27,32,2]{1,0,2:T(8,128)S(1)} %copy-done, bf16[32,2,8192]{2,1,0:T(2,128)(2,1)S(1)} %all_to_all.22), kind=kOutput, calls=%fused_computation.38 | convolution fusion | flops 170090496 | bytes 1940224 | tf_op jit(solution)/shard_map/tkp,kpf->tf/dot_general | solution.py:223
  (7 shorter events, 0.2 us)
Async XLA Ops:
  1.1 2.3 %collective-permute-start = (f32[27,4,1536]{2,1,0:T(4,128)S(1)}, f32[27,4,1536]{2,1,0:T(4,128)S(1)}, u32[]{:S(2)}, u32[]{:S(2)}) collective-permute-start(f32[27,4,1536]{2,1,0:T(4,128)S(1)} %dynamic-slice_bitcast_fusion.1), channel_id=1, source_target_pairs={{0,8},{8,0},{16,24},{24,16},{1,9},{9,1},{17,25},{25,17},{2,10},{10... | collective-permute-start | bytes 1990664 | tf_op jit(solution)/shard_map/ppermute | solution.py:164
  3.0 5.4 %collective-permute-start.2 = (f32[27,4,2560]{2,1,0:T(4,128)S(1)}, f32[27,4,2560]{2,1,0:T(4,128)}, u32[]{:S(2)}, u32[]{:S(2)}) collective-permute-start(f32[27,4,2560]{2,1,0:T(4,128)S(1)} %dynamic-slice_bitcast_fusion), channel_id=1, source_target_pairs={{0,8},{8,0},{16,24},{24,16},{1,9},{9,1},{17,25},{25,17},{2,10},{10... | collective-permute-start | bytes 3317768 | tf_op jit(solution)/shard_map/ppermute | solution.py:164
  5.4 11.5 %collective-permute-start.1 = (f32[1,2,27,1536]{3,1,2,0:T(2,128)S(1)}, f32[1,2,27,1536]{3,1,2,0:T(2,128)S(1)}, u32[]{:S(2)}, u32[]{:S(2)}) collective-permute-start(f32[1,2,27,1536]{3,1,2,0:T(2,128)S(1)} %dynamic-slice_bitcast_fusion.3), channel_id=1, source_target_pairs={{0,16},{8,24},{16,0},{24,8},{1,17},{9,25},{17,1},{25,9},{2,18},{10... | collective-permute-start | bytes 995336 | tf_op jit(solution)/shard_map/ppermute | solution.py:174
  11.1 17.2 %collective-permute-start.3 = (f32[1,2,27,2560]{3,1,2,0:T(2,128)S(1)}, f32[1,2,27,2560]{3,1,2,0:T(2,128)S(1)}, u32[]{:S(2)}, u32[]{:S(2)}) collective-permute-start(f32[1,2,27,2560]{3,1,2,0:T(2,128)S(1)} %dynamic-slice_bitcast_fusion.2), channel_id=1, source_target_pairs={{0,16},{8,24},{16,0},{24,8},{1,17},{9,25},{17,1},{25,9},{2,18},{10... | collective-permute-start | bytes 1658888 | tf_op jit(solution)/shard_map/ppermute | solution.py:174
  29.5 17.9 %copy-start.1 = (f32[27,8192]{1,0:T(8,128)S(1)}, f32[27,8192]{1,0:T(8,128)}, u32[]{:S(2)}) copy-start(f32[27,8192]{1,0:T(8,128)} %param.9) | copy-start | bytes 2654212
  29.5 17.9 %copy-start.3 = (s32[32,2]{0,1:T(2,128)S(1)}, s32[32,2]{0,1:T(2,128)}, u32[]{:S(2)}) copy-start(s32[32,2]{0,1:T(2,128)} %constant.280) | copy-start | bytes 772
  29.5 17.9 %copy-start.4 = (s32[32,2]{0,1:T(2,128)S(1)}, s32[32,2]{0,1:T(2,128)}, u32[]{:S(2)}) copy-start(s32[32,2]{0,1:T(2,128)} %constant.258) | copy-start | bytes 772
  29.5 17.9 %copy-start.5 = (pred[32,2]{0,1:T(4,128)(4,1)S(1)}, pred[32,2]{0,1:T(4,128)(4,1)}, u32[]{:S(2)}) copy-start(pred[32,2]{0,1:T(4,128)(4,1)} %constant.241) | copy-start | bytes 196
  30.0 17.3 %collective-permute-start.5 = (f32[27,2560]{1,0:T(8,128)S(1)}, f32[27,2560]{1,0:T(8,128)S(1)}, u32[]{:S(2)}, u32[]{:S(2)}) collective-permute-start(f32[27,2560]{1,0:T(8,128)S(1)} %bitcast.65), channel_id=1, source_target_pairs={{0,8},{8,0},{16,24},{24,16},{1,9},{9,1},{17,25},{25,17},{2,10},{10... | collective-permute-start | bytes 829448 | tf_op jit(solution)/shard_map/ppermute | solution.py:179
  30.4 16.9 %collective-permute-start.4 = (f32[27,1536]{1,0:T(8,128)S(1)}, f32[27,1536]{1,0:T(8,128)S(1)}, u32[]{:S(2)}, u32[]{:S(2)}) collective-permute-start(f32[27,1536]{1,0:T(8,128)S(1)} %bitcast.67), channel_id=1, source_target_pairs={{0,8},{8,0},{16,24},{24,16},{1,9},{9,1},{17,25},{25,17},{2,10},{10... | collective-permute-start | bytes 497672 | tf_op jit(solution)/shard_map/ppermute | solution.py:179
  32.9 13.1 %all-to-all-start = ((f32[32,1,1]{2,1,0:T(1,128)}), f32[32,1,1]{2,1,0:T(1,128)S(1)}, u32[]{:S(2)}, u32[]{:S(2)}) async-start(f32[32,1,1]{2,1,0:T(1,128)} %broadcast_in_dim.14), calls=%async_computation | async-start | bytes 32768 | tf_op jit(solution)/shard_map/all_to_all | solution.py:191
  49.4 4.7 %copy-start.2 = (s32[32]{0:T(128)S(1)}, s32[32]{0:T(128)}, u32[]{:S(2)}) copy-start(s32[32]{0:T(128)} %constant.238.clone) | copy-start | bytes 388
  51.5 30.2 %all-to-all-start.1 = ((bf16[32,2,8192]{2,1,0:T(2,128)(2,1)}), bf16[32,2,8192]{2,1,0:T(2,128)(2,1)S(1)}, u32[]{:S(2)}, u32[]{:S(2)}) async-start(bf16[32,2,8192]{2,1,0:T(2,128)(2,1)} %copy.21), calls=%async_computation.1 | async-start | bytes 2097152 | tf_op jit(solution)/shard_map/all_to_all | solution.py:215
  88.4 32.6 %copy-start = (f32[27,32,2]{1,0,2:T(8,128)S(1)}, f32[27,32,2]{1,0,2:T(8,128)}, u32[]{:S(2)}) copy-start(f32[27,32,2]{1,0,2:T(8,128)} %constant.239.clone) | copy-start | bytes 20740

commit v11 on v8

--- a/solution.py
+++ b/solution.py
@@ -126,6 +126,9 @@
 
 def piece_widths(width):
     tiles = width // 128
+    if tiles >= 8:
+        first, last = (tiles * 3) // 16, tiles // 4
+        return [first * 128, (tiles - first - last) * 128, last * 128]
     first = max(1, (tiles * 3) // 8)
     return [first * 128, width - first * 128] if tiles > 1 else [width]
 

time: 122 us -> 128 us (1.049)
  waiting for transfers between devices: 48.9 us -> 44.5 us
  local copies, waits for them, and re-layouts: 11.5 us -> 15.4 us
  starting transfers between devices: 12.9 us -> 15.4 us
  other arithmetic: 8.47 us -> 10.6 us
    ppermute x2 -> x3, waiting for transfers between devices: 15.3 us -> 12.5 us  [reduce_over_dp(): blocks = near + lax.ppermute(far, 'dp', partner)]
    ppermute x2 -> x3, starting transfers between devices: 2.96 us -> 4.9 us  [reduce_over_dp(): blocks = near + lax.ppermute(far, 'dp', partner)]
    unnamed x16 -> x23, local copies, waits for them, and re-layouts: 0.12 us -> 1.78 us
    reduce_sum x2 -> x3, other arithmetic: 3.15 us -> 4.63 us  [reduce_over_dp(): squares.append(jnp.sum(blocks * blocks))]
    dynamic_slice x2 -> x3, local copies, waits for them, and re-layouts: 2.45 us -> 3.31 us  [reduce_over_dp(): lax.dynamic_slice_in_dim(parts, (1 - core) * half + offset, piece, axis=2)]
    transpose x2 -> x3, other arithmetic: 3.13 us -> 3.8 us  [reduce_over_dp(): blocks = (keep + lax.ppermute(send, 'dp', pair)).transpose(1, 0, 2)]
  transfers between devices with their start and end apart: 8 -> 11, of which waited for: 5 -> 4; matrix products, arithmetic and copies ran while one was open for 9% -> 15% of each run, Pallas kernels for 0% -> 0%
where the time goes in v11:
time: 128 us; the launch traced here: 127 us
  waiting for transfers between devices  44.5 us (35%)
  blocking collectives  29.6 us (23%)
  local copies, waits for them, and re-layouts  15.4 us (12%)
  starting transfers between devices  15.4 us (12%)
  other arithmetic  10.6 us (8%)
  matrix products  7.35 us (6%)
  between operations  3.52 us (3%)
    all_to_all x1, blocking collectives, on_device(): returned = lax.all_to_all(back, AXES, 0, 0, tiled=True)  29.6 us
    all_to_all x1, waiting for transfers between devices, on_device(): whole = lax.all_to_all(sent, AXES, 0, 0, tiled=True)  26.3 us
    ppermute x3, waiting for transfers between devices, reduce_over_dp(): blocks = near + lax.ppermute(far, 'dp', partner)  12.5 us
    all_to_all x1, starting transfers between devices, total_over_devices(): gathered = lax.all_to_all(spread, AXES, 0, 0, tiled=True)  6.07 us
    all_to_all x1, waiting for transfers between devices, total_over_devices(): gathered = lax.all_to_all(spread, AXES, 0, 0, tiled=True)  5.71 us
    ppermute x3, starting transfers between devices, reduce_over_dp(): blocks = near + lax.ppermute(far, 'dp', partner)  4.9 us
    reduce_sum x3, other arithmetic, reduce_over_dp(): squares.append(jnp.sum(blocks * blocks))  4.63 us
    transpose x3, other arithmetic, reduce_over_dp(): blocks = (keep + lax.ppermute(send, 'dp', pair)).transpose(1, 0, 2)  3.8 us
  transfers between devices with their start and end apart: 11, of which 4 were waited for; matrix products, arithmetic and copies ran while one was open for 15% of the time, Pallas kernels for 0%

profile of v11, /device:TPU:0, one launch (start us, length us, event | category | flops | bytes accessed | tf_op | source)
XLA Modules:
  0.0 127.4 jit_solution(16009160145147746099)
XLA Ops:
  0.0 1.0 dynamic-slice_bitcast_fusion.3
  1.0 0.5 collective-permute-start
  1.5 1.0 dynamic-slice_bitcast_fusion.2
  2.6 0.1 collective-permute-start.4
  2.7 1.3 dynamic-slice_bitcast_fusion
  4.0 0.5 collective-permute-start.2
  4.5 0.0 collective-permute-done
  4.5 1.1 fusion.44
  5.6 0.3 reshape_reshape.9
  5.8 0.7 dynamic-slice_bitcast_fusion.5
  6.5 2.6 %collective-permute-start.1 = (f32[1,2,27,768]{3,1,2,0:T(2,128)}, f32[1,2,27,768]{3,1,2,0:T(2,128)}, u32[]{:S(2)}, u32[]{:S(2)}) collective-permute-start(f32[1,2,27,768]{3,1,2,0:T(2,128)} %dynamic-slice_bitcast_fusion.5), channel_id=1, source_target_pairs={{0,16},{8,24},{16,0},{24,8},{1,17},{9,25},{17,1},{25,9},{2,18},{10... | collective-permute-start | bytes 497672 | tf_op jit(solution)/shard_map/ppermute | solution.py:166
  9.1 0.0 collective-permute-done.4
  9.1 1.3 fusion.43
  10.4 0.3 reshape_reshape.11
  10.8 0.7 dynamic-slice_bitcast_fusion.4
  11.5 0.0 collective-permute-start.5
  11.5 2.8 %collective-permute-done.1 = f32[1,2,27,768]{3,1,2,0:T(2,128)} collective-permute-done((f32[1,2,27,768]{3,1,2,0:T(2,128)}, f32[1,2,27,768]{3,1,2,0:T(2,128)}, u32[]{:S(2)}, u32[]{:S(2)}) %collective-permute-start.1) | collective-permute-done | bytes 165920 | tf_op jit(solution)/shard_map/ppermute | solution.py:166
  14.3 1.7 %multiply_reduce_fusion.2 = (f32[]{:T(128)}, f32[1,2,27,768]{3,1,2,0:T(2,128)S(1)}) fusion(f32[1,2,27,768]{3,1,2,0:T(2,128)} %collective-permute-done.1, f32[2,1,2,27,768]{4,2,0,3,1:T(2,128)S(1)} %reshape_reshape.9, s32[]{:T(128)S(6)} %select_n.155), kind=kLoop, calls=%fused_computation.71 | loop fusion | flops 124415 | bytes 497672 | tf_op jit(solution)/shard_map/reduce_sum | solution.py:168
  16.0 0.8 constant_dynamic-slice_fusion.1
  16.7 0.6 copy.38
  17.4 0.0 collective-permute-start.6
  17.4 1.5 %fusion.40 = f32[4,27,2304]{2,0,1:T(4,128)S(1)} fusion(f32[27,4,2304]{2,1,0:T(4,128)S(1)} %collective-permute-done.2, f32[1,27,4,8192]{3,2,1,0:T(4,128)} %param.8, s32[]{:T(128)S(6)} %select_n.157), kind=kLoop, calls=%fused_computation.51 | loop fusion | flops 248832 | bytes 2985988 | tf_op jit(solution)/shard_map/transpose | solution.py:156
  18.9 0.8 reshape_reshape.10
  19.7 2.3 %collective-permute-start.3 = (f32[1,2,27,2304]{3,1,2,0:T(2,128)S(1)}, f32[1,2,27,2304]{3,1,2,0:T(2,128)S(1)}, u32[]{:S(2)}, u32[]{:S(2)}) collective-permute-start(f32[1,2,27,2304]{3,1,2,0:T(2,128)S(1)} %dynamic-slice_bitcast_fusion.1), channel_id=1, source_target_pairs={{0,16},{8,24},{16,0},{24,8},{1,17},{9,25},{17,1},{25,9},{2,18},{10... | collective-permute-start | bytes 1493000 | tf_op jit(solution)/shard_map/ppermute | solution.py:166
  22.0 1.8 %multiply_reduce_fusion.1 = (f32[]{:T(128)}, f32[1,2,27,1024]{3,1,2,0:T(2,128)S(1)}) fusion(f32[1,2,27,1024]{3,1,2,0:T(2,128)} %collective-permute-done.5, f32[2,1,2,27,1024]{4,2,0,3,1:T(2,128)S(1)} %reshape_reshape.11, s32[]{:T(128)S(6)} %select_n.155), kind=kLoop, calls=%fused_computation.68 | loop fusion | flops 165887 | bytes 663560 | tf_op jit(solution)/shard_map/reduce_sum | solution.py:168
  23.8 0.2 constant_dynamic-slice_fusion.5
  24.1 0.3 collective-permute-start.8
  24.4 9.7 %collective-permute-done.3 = f32[1,2,27,2304]{3,1,2,0:T(2,128)S(1)} collective-permute-done((f32[1,2,27,2304]{3,1,2,0:T(2,128)S(1)}, f32[1,2,27,2304]{3,1,2,0:T(2,128)S(1)}, u32[]{:S(2)}, u32[]{:S(2)}) %collective-permute-start.3) | collective-permute-done | bytes 497696 | tf_op jit(solution)/shard_map/ppermute | solution.py:166
  34.0 1.1 multiply_reduce_fusion
  35.2 0.4 constant_dynamic-slice_fusion
  35.6 0.0 copy-start.2
  35.6 0.0 copy-start.3
  35.6 0.0 copy-start.4
  37.5 0.6 broadcast_in_dim.8
  38.1 6.1 %all-to-all-start = ((f32[32,1,1]{2,1,0:T(1,128)}), f32[32,1,1]{2,1,0:T(1,128)S(1)}, u32[]{:S(2)}, u32[]{:S(2)}) async-start(f32[32,1,1]{2,1,0:T(1,128)} %broadcast_in_dim.8), calls=%async_computation | async-start | bytes 32768 | tf_op jit(solution)/shard_map/all_to_all | solution.py:183
  44.2 0.3 collective-permute-start.7
  44.6 0.9 constant_dynamic-update-slice_fusion.5
  45.5 5.7 %all-to-all-done = f32[32,1,1]{2,1,0:T(1,128)S(1)} async-done(((f32[32,1,1]{2,1,0:T(1,128)}), f32[32,1,1]{2,1,0:T(1,128)S(1)}, u32[]{:S(2)}, u32[]{:S(2)}) %all-to-all-start) | async-done | bytes 160 | tf_op jit(solution)/shard_map/all_to_all | solution.py:183
  51.2 0.6 reduce_sum.57
  52.5 0.0 collective-permute-done.7
  52.6 0.0 collective-permute-done.8
  52.8 3.3 %convolution_convert_fusion.1 = bf16[64,8192]{1,0:T(8,128)(2,1)S(1)} fusion(f32[27,8192]{1,0:T(8,128)} %param.9, f32[27,8192]{1,0:T(8,128)S(1)} %get-tuple-element.31, f32[27,8192]{1,0:T(8,128)S(1)} %bitcast_dynamic-update-slice_fusion.2, f32[]{:T(128)S(6)} %min_shard_map.3, pred[]{:T(512)S(6)} %eq.21, s32[27]{0:T(128)S(1)} %get-tuple-element.34, ...), kind=kOutput, calls=%fused_computation.43 | convolution fusion | flops 171091712 | bytes 3703581 | tf_op jit(solution)/shard_map/dot_general | solution.py:204
  56.0 0.0 copy-start.5
  56.0 1.5 %reshape.104 = bf16[32,2,8192]{2,1,0:T(2,128)(2,1)} reshape(bf16[64,8192]{1,0:T(8,128)(2,1)S(1)} %convolution_convert_fusion.1) | data formatting | bytes 2097152 | tf_op jit(solution)/shard_map/reshape | solution.py:205
  57.5 2.6 %all-to-all-start.1 = ((bf16[32,2,8192]{2,1,0:T(2,128)(2,1)}), bf16[32,2,8192]{2,1,0:T(2,128)(2,1)S(1)}, u32[]{:S(2)}, u32[]{:S(2)}) async-start(bf16[32,2,8192]{2,1,0:T(2,128)(2,1)} %reshape.104), calls=%async_computation.1 | async-start | bytes 2097152 | tf_op jit(solution)/shard_map/all_to_all | solution.py:206
  60.2 0.6 dynamic_slice.75
  61.5 26.3 %all-to-all-done.1 = bf16[32,2,8192]{2,1,0:T(2,128)(2,1)S(1)} async-done(((bf16[32,2,8192]{2,1,0:T(2,128)(2,1)}), bf16[32,2,8192]{2,1,0:T(2,128)(2,1)S(1)}, u32[]{:S(2)}, u32[]{:S(2)}) %all-to-all-start.1) | async-done | bytes 1048608 | tf_op jit(solution)/shard_map/all_to_all | solution.py:206
  87.8 0.6 copy.15
  88.4 0.5 reshape.105
  88.9 5.2 %conditional.1 = (bf16[2,512,512]{2,1,0:T(8,128)(2,1)S(1)}) conditional(s32[]{:T(128)} %bitcast.4, bf16[2,512,512]{2,1,0:T(8,128)(2,1)S(1)} %reshape.105, bf16[2,512,512]{2,1,0:T(8,128)(2,1)S(1)} %reshape.105), branch_computations={%region_4.6_spmd, %region_6.8_spmd} | conditional | flops 2175270912 | bytes 19398728 | solution.py:211
  89.1 1.1 fusion.6
  91.0 0.2 fusion.7
  91.2 0.1 slice_bitcast_fusion.3
  91.3 1.3 fusion.24
  92.6 0.1 slice_negate_fusion
  92.7 1.3 %subtract_convert_fusion.1 = bf16[512,1024]{1,0:T(8,128)(2,1)S(1)} fusion(bf16[512,512]{1,0:T(8,128)(2,1)S(1)} %get-tuple-element.19, bf16[512,512]{1,0:T(8,128)(2,1)S(1)} %get-tuple-element.18, bf16[512,1024]{1,0:T(8,128)(2,1)S(1)} %fusion.24, bf16[512,512]{1,0:T(8,128)(2,1)S(1)} %get-tuple-element.21, bf16[512,512]{1,0:T(8,128)(2,1)S(1)} %get-tuple-element.20), kind=kOutput, calls=%fused_computation.26 | convolution fusion | flops 1086324736 | bytes 4194304 | tf_op jit(solution)/shard_map/cond/branch_1_fun/dot_general | solution.py:109
  93.9 0.1 slice_bitcast_fusion.1
  94.0 0.1 pad_maximum_fusion
  94.1 0.5 reshape.106
  94.7 1.1 copy.35
  95.8 0.0 copy-start.1
  95.8 29.6 %all_to_all.16 = bf16[32,2,8192]{2,1,0:T(2,128)(2,1)S(1)} all-to-all(bf16[32,2,8192]{2,1,0:T(2,128)(2,1)S(1)} %bitcast.83), channel_id=1, replica_groups=mesh['dp'=4,'freq'=8] {'dp','freq'}, dimensions={0} | all-to-all | bytes 2097152 | tf_op jit(solution)/shard_map/all_to_all | solution.py:214
  125.4 0.4 reshape.107
  125.8 1.5 %fusion.36 = f32[27,8192]{1,0:T(8,128)} fusion(bf16[64,8192]{1,0:T(8,128)(2,1)S(1)} %reshape.107, f32[27,64]{1,0:T(8,128)S(1)} %copy-done.1), kind=kOutput, calls=%fused_computation.45 | convolution fusion | flops 170090496 | bytes 1940224 | tf_op jit(solution)/shard_map/dot_general | solution.py:216
  (23 shorter events, 0.3 us)
Async XLA Ops:
  1.0 3.5 %collective-permute-start = (f32[27,4,768]{2,1,0:T(4,128)S(1)}, f32[27,4,768]{2,1,0:T(4,128)S(1)}, u32[]{:S(2)}, u32[]{:S(2)}) collective-permute-start(f32[27,4,768]{2,1,0:T(4,128)S(1)} %dynamic-slice_bitcast_fusion.3), channel_id=1, source_target_pairs={{0,8},{8,0},{16,24},{24,16},{1,9},{9,1},{17,25},{25,17},{2,10},{10... | collective-permute-start | bytes 995336 | tf_op jit(solution)/shard_map/ppermute | solution.py:156
  2.6 6.6 %collective-permute-start.4 = (f32[27,4,1024]{2,1,0:T(4,128)S(1)}, f32[27,4,1024]{2,1,0:T(4,128)}, u32[]{:S(2)}, u32[]{:S(2)}) collective-permute-start(f32[27,4,1024]{2,1,0:T(4,128)S(1)} %dynamic-slice_bitcast_fusion.2), channel_id=1, source_target_pairs={{0,8},{8,0},{16,24},{24,16},{1,9},{9,1},{17,25},{25,17},{2,10},{10... | collective-permute-start | bytes 1327112 | tf_op jit(solution)/shard_map/ppermute | solution.py:156
  4.0 13.4 %collective-permute-start.2 = (f32[27,4,2304]{2,1,0:T(4,128)S(1)}, f32[27,4,2304]{2,1,0:T(4,128)S(1)}, u32[]{:S(2)}, u32[]{:S(2)}) collective-permute-start(f32[27,4,2304]{2,1,0:T(4,128)S(1)} %dynamic-slice_bitcast_fusion), channel_id=1, source_target_pairs={{0,8},{8,0},{16,24},{24,16},{1,9},{9,1},{17,25},{25,17},{2,10},{10... | collective-permute-start | bytes 2985992 | tf_op jit(solution)/shard_map/ppermute | solution.py:156
  6.5 7.7 %collective-permute-start.1 = (f32[1,2,27,768]{3,1,2,0:T(2,128)}, f32[1,2,27,768]{3,1,2,0:T(2,128)}, u32[]{:S(2)}, u32[]{:S(2)}) collective-permute-start(f32[1,2,27,768]{3,1,2,0:T(2,128)} %dynamic-slice_bitcast_fusion.5), channel_id=1, source_target_pairs={{0,16},{8,24},{16,0},{24,8},{1,17},{9,25},{17,1},{25,9},{2,18},{10... | collective-permute-start | bytes 497672 | tf_op jit(solution)/shard_map/ppermute | solution.py:166
  11.5 10.5 %collective-permute-start.5 = (f32[1,2,27,1024]{3,1,2,0:T(2,128)}, f32[1,2,27,1024]{3,1,2,0:T(2,128)}, u32[]{:S(2)}, u32[]{:S(2)}) collective-permute-start(f32[1,2,27,1024]{3,1,2,0:T(2,128)} %dynamic-slice_bitcast_fusion.4), channel_id=1, source_target_pairs={{0,16},{8,24},{16,0},{24,8},{1,17},{9,25},{17,1},{25,9},{2,18},{10... | collective-permute-start | bytes 663560 | tf_op jit(solution)/shard_map/ppermute | solution.py:166
  17.4 27.2 %collective-permute-start.6 = (f32[27,768]{1,0:T(8,128)}, f32[27,768]{1,0:T(8,128)}, u32[]{:S(2)}, u32[]{:S(2)}) collective-permute-start(f32[27,768]{1,0:T(8,128)} %bitcast.81), channel_id=1, source_target_pairs={{0,8},{8,0},{16,24},{24,16},{1,9},{9,1},{17,25},{25,17},{2,10},{10... | collective-permute-start | bytes 248840 | tf_op jit(solution)/shard_map/ppermute | solution.py:171
  18.9 3.1 %copy-start = (f32[1,1,27,768]{3,1,2,0:T(1,128)S(1)}, f32[1,1,27,768]{3,1,2,0:T(1,128)}, u32[]{:S(2)}) copy-start(f32[1,1,27,768]{3,1,2,0:T(1,128)} %get-tuple-element.29) | copy-start | bytes 248836
  19.7 14.3 %collective-permute-start.3 = (f32[1,2,27,2304]{3,1,2,0:T(2,128)S(1)}, f32[1,2,27,2304]{3,1,2,0:T(2,128)S(1)}, u32[]{:S(2)}, u32[]{:S(2)}) collective-permute-start(f32[1,2,27,2304]{3,1,2,0:T(2,128)S(1)} %dynamic-slice_bitcast_fusion.1), channel_id=1, source_target_pairs={{0,16},{8,24},{16,0},{24,8},{1,17},{9,25},{17,1},{25,9},{2,18},{10... | collective-permute-start | bytes 1493000 | tf_op jit(solution)/shard_map/ppermute | solution.py:166
  24.1 28.6 %collective-permute-start.8 = (f32[27,1024]{1,0:T(8,128)S(1)}, f32[27,1024]{1,0:T(8,128)S(1)}, u32[]{:S(2)}, u32[]{:S(2)}) collective-permute-start(f32[27,1024]{1,0:T(8,128)S(1)} %bitcast.85), channel_id=1, source_target_pairs={{0,8},{8,0},{16,24},{24,16},{1,9},{9,1},{17,25},{25,17},{2,10},{10... | collective-permute-start | bytes 331784 | tf_op jit(solution)/shard_map/ppermute | solution.py:171
  35.6 17.1 %copy-start.2 = (s32[64]{0:T(128)S(1)}, s32[64]{0:T(128)}, u32[]{:S(2)}) copy-start(s32[64]{0:T(128)} %constant.302) | copy-start | bytes 772
  35.6 17.1 %copy-start.3 = (s32[64]{0:T(128)S(1)}, s32[64]{0:T(128)}, u32[]{:S(2)}) copy-start(s32[64]{0:T(128)} %constant.281) | copy-start | bytes 772
  35.6 17.1 %copy-start.4 = (pred[64]{0:T(512)(128)(4,1)S(1)}, pred[64]{0:T(512)(128)(4,1)}, u32[]{:S(2)}) copy-start(pred[64]{0:T(512)(128)(4,1)} %constant.262.clone) | copy-start | bytes 196
  38.1 13.1 %all-to-all-start = ((f32[32,1,1]{2,1,0:T(1,128)}), f32[32,1,1]{2,1,0:T(1,128)S(1)}, u32[]{:S(2)}, u32[]{:S(2)}) async-start(f32[32,1,1]{2,1,0:T(1,128)} %broadcast_in_dim.8), calls=%async_computation | async-start | bytes 32768 | tf_op jit(solution)/shard_map/all_to_all | solution.py:183
  44.2 8.3 %collective-permute-start.7 = (f32[27,2304]{1,0:T(8,128)S(1)}, f32[27,2304]{1,0:T(8,128)S(1)}, u32[]{:S(2)}, u32[]{:S(2)}) collective-permute-start(f32[27,2304]{1,0:T(8,128)S(1)} %bitcast.84), channel_id=1, source_target_pairs={{0,8},{8,0},{16,24},{24,16},{1,9},{9,1},{17,25},{25,17},{2,10},{10... | collective-permute-start | bytes 746504 | tf_op jit(solution)/shard_map/ppermute | solution.py:171
  56.0 4.2 %copy-start.5 = (s32[32]{0:T(128)S(1)}, s32[32]{0:T(128)}, u32[]{:S(2)}) copy-start(s32[32]{0:T(128)} %constant.263.clone) | copy-start | bytes 388
  57.5 30.2 %all-to-all-start.1 = ((bf16[32,2,8192]{2,1,0:T(2,128)(2,1)}), bf16[32,2,8192]{2,1,0:T(2,128)(2,1)S(1)}, u32[]{:S(2)}, u32[]{:S(2)}) async-start(bf16[32,2,8192]{2,1,0:T(2,128)(2,1)} %reshape.104), calls=%async_computation.1 | async-start | bytes 2097152 | tf_op jit(solution)/shard_map/all_to_all | solution.py:206
  95.8 30.1 %copy-start.1 = (f32[27,64]{1,0:T(8,128)S(1)}, f32[27,64]{1,0:T(8,128)}, u32[]{:S(2)}) copy-start(f32[27,64]{1,0:T(8,128)} %constant.264.clone) | copy-start | bytes 20740

commit v12 on v8

--- a/solution.py
+++ b/solution.py
@@ -126,7 +126,7 @@
 
 def piece_widths(width):
     tiles = width // 128
-    first = max(1, (tiles * 3) // 8)
+    first = max(1, tiles // 4)
     return [first * 128, width - first * 128] if tiles > 1 else [width]
 
 

time: 122 us -> 124 us (1.016)
  waiting for transfers between devices: 48.9 us -> 50.3 us
where the time goes in v12:
time: 124 us; the launch traced here: 123 us
  waiting for transfers between devices  50.3 us (41%)
  blocking collectives  29.6 us (24%)
  starting transfers between devices  12.6 us (10%)
  local copies, waits for them, and re-layouts  11.6 us (9%)
  other arithmetic  7.74 us (6%)
  matrix products  7.25 us (6%)
  between operations  2.86 us (2%)
    all_to_all x1, blocking collectives, on_device(): returned = lax.all_to_all(back, AXES, 0, 0, tiled=True)  29.6 us
    all_to_all x1, waiting for transfers between devices, on_device(): whole = lax.all_to_all(sent, AXES, 0, 0, tiled=True)  26.3 us
    ppermute x2, waiting for transfers between devices, reduce_over_dp(): blocks = near + lax.ppermute(far, 'dp', partner)  16.1 us
    all_to_all x1, waiting for transfers between devices, total_over_devices(): gathered = lax.all_to_all(spread, AXES, 0, 0, tiled=True)  6.93 us
    all_to_all x1, starting transfers between devices, total_over_devices(): gathered = lax.all_to_all(spread, AXES, 0, 0, tiled=True)  6.16 us
    transpose x2, other arithmetic, reduce_over_dp(): blocks = (keep + lax.ppermute(send, 'dp', pair)).transpose(1, 0, 2)  3.34 us
    dynamic_slice x2, local copies, waits for them, and re-layouts, reduce_over_dp(): lax.dynamic_slice_in_dim(parts, (1 - core) * half + offset, piece, axis=2)  3.21 us
    dot_general x1, matrix products, on_device(): spectra = jnp.dot(forward, updated, precision=HIGH).astype(jnp.bfloat16)  3.16 us
  transfers between devices with their start and end apart: 8, of which 5 were waited for; matrix products, arithmetic and copies ran while one was open for 9% of the time, Pallas kernels for 0%

profile of v12, /device:TPU:0, one launch (start us, length us, event | category | flops | bytes accessed | tf_op | source)
XLA Modules:
  0.0 123.0 jit_solution(17874035395098240289)
XLA Ops:
  0.0 1.4 %dynamic-slice_bitcast_fusion = f32[27,4,3072]{2,1,0:T(4,128)S(1)} fusion(f32[1,27,4,8192]{3,2,1,0:T(4,128)} %param.8, s32[]{:T(128)S(6)} %select_n.143), kind=kLoop, calls=%fused_computation.48 | loop fusion | bytes 2654212 | tf_op jit(solution)/shard_map/dynamic_slice | solution.py:151
  1.4 0.5 collective-permute-start.2
  1.9 1.8 %dynamic-slice_bitcast_fusion.2 = f32[27,4,1024]{2,1,0:T(4,128)} fusion(f32[1,27,4,8192]{3,2,1,0:T(4,128)} %param.8, s32[]{:T(128)S(6)} %select_n.137), kind=kLoop, calls=%fused_computation.73 | loop fusion | bytes 884740 | tf_op jit(solution)/shard_map/dynamic_slice | solution.py:151
  3.7 0.1 collective-permute-start
  3.8 1.0 collective-permute-done.2
  4.7 2.1 %fusion.37 = f32[4,27,3072]{2,0,1:T(4,128)S(1)} fusion(f32[27,4,3072]{2,1,0:T(4,128)} %collective-permute-done.2, f32[1,27,4,8192]{3,2,1,0:T(4,128)} %param.8, s32[]{:T(128)S(6)} %select_n.142), kind=kLoop, calls=%fused_computation.47 | loop fusion | flops 331776 | bytes 3981316 | tf_op jit(solution)/shard_map/transpose | solution.py:153
  6.8 1.0 reshape_reshape.7
  7.9 0.1 dynamic-slice_bitcast_fusion.1
  7.9 3.0 %collective-permute-start.3 = (f32[1,2,27,3072]{3,1,2,0:T(2,128)S(1)}, f32[1,2,27,3072]{3,1,2,0:T(2,128)S(1)}, u32[]{:S(2)}, u32[]{:S(2)}) collective-permute-start(f32[1,2,27,3072]{3,1,2,0:T(2,128)S(1)} %dynamic-slice_bitcast_fusion.1), channel_id=1, source_target_pairs={{0,16},{8,24},{16,0},{24,8},{1,17},{9,25},{17,1},{25,9},{2,18},{10... | collective-permute-start | bytes 1990664 | tf_op jit(solution)/shard_map/ppermute | solution.py:163
  10.9 0.0 collective-permute-done
  10.9 1.3 %fusion.56 = f32[4,27,1024]{2,0,1:T(4,128)S(1)} fusion(f32[27,4,1024]{2,1,0:T(4,128)} %collective-permute-done, f32[1,27,4,8192]{3,2,1,0:T(4,128)} %param.8, s32[]{:T(128)S(6)} %select_n.136), kind=kLoop, calls=%fused_computation.72 | loop fusion | flops 110592 | bytes 1327108 | tf_op jit(solution)/shard_map/transpose | solution.py:153
  12.1 0.3 reshape_reshape.6
  12.5 0.1 collective-permute-start.1
  12.7 13.9 %collective-permute-done.3 = f32[1,2,27,3072]{3,1,2,0:T(2,128)S(1)} collective-permute-done((f32[1,2,27,3072]{3,1,2,0:T(2,128)S(1)}, f32[1,2,27,3072]{3,1,2,0:T(2,128)S(1)}, u32[]{:S(2)}, u32[]{:S(2)}) %collective-permute-start.3) | collective-permute-done | bytes 663584 | tf_op jit(solution)/shard_map/ppermute | solution.py:163
  26.6 1.3 %multiply_reduce_fusion = (f32[]{:T(128)}, f32[1,2,27,3072]{3,1,2,0:T(2,128)S(1)}) fusion(f32[1,2,27,3072]{3,1,2,0:T(2,128)S(1)} %collective-permute-done.3, f32[2,1,2,27,3072]{4,2,0,3,1:T(2,128)S(1)} %reshape_reshape.7, s32[]{:T(128)S(6)} %select_n.140), kind=kLoop, calls=%fused_computation.67 | loop fusion | flops 497663 | bytes 1990664 | tf_op jit(solution)/shard_map/reduce_sum | solution.py:165
  27.9 0.0 copy-start.1
  27.9 0.0 copy-start.3
  27.9 0.0 copy-start.4
  27.9 0.0 copy-start.5
  27.9 0.6 constant_dynamic-slice_fusion.1
  28.5 0.1 copy.29
  28.5 0.1 collective-permute-start.5
  28.6 2.2 %collective-permute-done.1 = f32[1,2,27,1024]{3,1,2,0:T(2,128)S(1)} collective-permute-done((f32[1,2,27,1024]{3,1,2,0:T(2,128)S(1)}, f32[1,2,27,1024]{3,1,2,0:T(2,128)S(1)}, u32[]{:S(2)}, u32[]{:S(2)}) %collective-permute-start.1) | collective-permute-done | bytes 221216 | tf_op jit(solution)/shard_map/ppermute | solution.py:163
  30.8 0.9 multiply_reduce_fusion.1
  31.7 0.2 constant_dynamic-slice_fusion.2
  31.9 0.1 collective-permute-start.4
  33.3 0.6 broadcast_in_dim.8
  33.9 6.2 %all-to-all-start = ((f32[32,1,1]{2,1,0:T(1,128)}), f32[32,1,1]{2,1,0:T(1,128)S(1)}, u32[]{:S(2)}, u32[]{:S(2)}) async-start(f32[32,1,1]{2,1,0:T(1,128)} %broadcast_in_dim.8), calls=%async_computation | async-start | bytes 32768 | tf_op jit(solution)/shard_map/all_to_all | solution.py:180
  40.1 0.1 copy.30
  40.2 6.9 %all-to-all-done = f32[32,1,1]{2,1,0:T(1,128)S(1)} async-done(((f32[32,1,1]{2,1,0:T(1,128)}), f32[32,1,1]{2,1,0:T(1,128)S(1)}, u32[]{:S(2)}, u32[]{:S(2)}) %all-to-all-start) | async-done | bytes 160 | tf_op jit(solution)/shard_map/all_to_all | solution.py:180
  47.1 0.6 reduce_sum.47
  48.5 0.0 collective-permute-done.4
  48.5 0.0 collective-permute-done.5
  48.5 0.0 copy-done.1
  48.5 0.0 copy-done.3
  48.5 0.0 copy-done.4
  48.5 0.0 copy-done.5
  48.5 3.2 %convolution_convert_fusion.1 = bf16[64,8192]{1,0:T(8,128)(2,1)S(1)} fusion(f32[27,8192]{1,0:T(8,128)S(1)} %copy-done.1, f32[27,3072]{1,0:T(8,128)} %collective-permute-done.5, f32[27,1024]{1,0:T(8,128)S(1)} %collective-permute-done.4, f32[27,3072]{1,0:T(8,128)S(1)} %bitcast.64, f32[27,1024]{1,0:T(8,128)S(1)} %bitcast.66, f32[]{:T(128)S(6)} %min_shard_map.3, ...), kind=kOutput, calls=%fused_computation.43 | convolution fusion | flops 172418816 | bytes 2818845 | tf_op jit(solution)/shard_map/dot_general | solution.py:201
  51.7 0.0 copy-start.2
  51.7 1.5 %reshape.96 = bf16[32,2,8192]{2,1,0:T(2,128)(2,1)} reshape(bf16[64,8192]{1,0:T(8,128)(2,1)S(1)} %convolution_convert_fusion.1) | data formatting | bytes 2097152 | tf_op jit(solution)/shard_map/reshape | solution.py:202
  53.2 2.6 %all-to-all-start.1 = ((bf16[32,2,8192]{2,1,0:T(2,128)(2,1)}), bf16[32,2,8192]{2,1,0:T(2,128)(2,1)S(1)}, u32[]{:S(2)}, u32[]{:S(2)}) async-start(bf16[32,2,8192]{2,1,0:T(2,128)(2,1)} %reshape.96), calls=%async_computation.1 | async-start | bytes 2097152 | tf_op jit(solution)/shard_map/all_to_all | solution.py:203
  55.9 0.0 copy-done.2
  55.9 0.6 dynamic_slice.51
  57.1 26.3 %all-to-all-done.1 = bf16[32,2,8192]{2,1,0:T(2,128)(2,1)S(1)} async-done(((bf16[32,2,8192]{2,1,0:T(2,128)(2,1)}), bf16[32,2,8192]{2,1,0:T(2,128)(2,1)S(1)}, u32[]{:S(2)}, u32[]{:S(2)}) %all-to-all-start.1) | async-done | bytes 1048608 | tf_op jit(solution)/shard_map/all_to_all | solution.py:203
  83.4 0.6 copy.15
  84.0 0.5 reshape.97
  84.6 5.2 %conditional.1 = (bf16[2,512,512]{2,1,0:T(8,128)(2,1)S(1)}) conditional(s32[]{:T(128)} %bitcast.4, bf16[2,512,512]{2,1,0:T(8,128)(2,1)S(1)} %reshape.97, bf16[2,512,512]{2,1,0:T(8,128)(2,1)S(1)} %reshape.97), branch_computations={%region_3.5_spmd, %region_5.7_spmd} | conditional | flops 2175270912 | bytes 19398728 | solution.py:208
  84.8 1.1 fusion.6
  86.6 0.2 fusion.7
  86.9 0.1 slice_bitcast_fusion.3
  87.0 1.3 %fusion.24 = bf16[512,1024]{1,0:T(8,128)(2,1)S(1)} fusion(bf16[512,512]{1,0:T(8,128)(2,1)S(1)} %fusion.35, bf16[512,512]{1,0:T(8,128)(2,1)S(1)} %get-tuple-element.19, bf16[512,512]{1,0:T(8,128)(2,1)S(1)} %get-tuple-element.18), kind=kOutput, calls=%fused_computation.27 | convolution fusion | flops 1084751872 | bytes 2621440 | tf_op jit(solution)/shard_map/cond/branch_1_fun/dot_general | solution.py:102
  88.2 0.1 slice_negate_fusion
  88.3 1.3 %subtract_convert_fusion.1 = bf16[512,1024]{1,0:T(8,128)(2,1)S(1)} fusion(bf16[512,512]{1,0:T(8,128)(2,1)S(1)} %get-tuple-element.17, bf16[512,512]{1,0:T(8,128)(2,1)S(1)} %get-tuple-element.16, bf16[512,1024]{1,0:T(8,128)(2,1)S(1)} %fusion.24, bf16[512,512]{1,0:T(8,128)(2,1)S(1)} %get-tuple-element.19, bf16[512,512]{1,0:T(8,128)(2,1)S(1)} %get-tuple-element.18), kind=kOutput, calls=%fused_computation.26 | convolution fusion | flops 1086324736 | bytes 4194304 | tf_op jit(solution)/shard_map/cond/branch_1_fun/dot_general | solution.py:109
  89.6 0.1 slice_bitcast_fusion.1
  89.7 0.1 pad_maximum_fusion
  89.8 0.5 reshape.98
  90.3 1.1 copy.28
  91.4 0.0 copy-start
  91.4 29.6 %all_to_all.16 = bf16[32,2,8192]{2,1,0:T(2,128)(2,1)S(1)} all-to-all(bf16[32,2,8192]{2,1,0:T(2,128)(2,1)S(1)} %bitcast.62), channel_id=1, replica_groups=mesh['dp'=4,'freq'=8] {'dp','freq'}, dimensions={0} | all-to-all | bytes 2097152 | tf_op jit(solution)/shard_map/all_to_all | solution.py:211
  121.0 0.4 reshape.99
  121.5 0.0 copy-done
  121.5 1.5 %fusion.36 = f32[27,8192]{1,0:T(8,128)} fusion(bf16[64,8192]{1,0:T(8,128)(2,1)S(1)} %reshape.99, f32[27,64]{1,0:T(8,128)S(1)} %copy-done), kind=kOutput, calls=%fused_computation.45 | convolution fusion | flops 170090496 | bytes 1940224 | tf_op jit(solution)/shard_map/dot_general | solution.py:213
  (5 shorter events, 0.1 us)
Async XLA Ops:
  1.4 3.3 %collective-permute-start.2 = (f32[27,4,3072]{2,1,0:T(4,128)S(1)}, f32[27,4,3072]{2,1,0:T(4,128)}, u32[]{:S(2)}, u32[]{:S(2)}) collective-permute-start(f32[27,4,3072]{2,1,0:T(4,128)S(1)} %dynamic-slice_bitcast_fusion), channel_id=1, source_target_pairs={{0,8},{8,0},{16,24},{24,16},{1,9},{9,1},{17,25},{25,17},{2,10},{10... | collective-permute-start | bytes 3981320 | tf_op jit(solution)/shard_map/ppermute | solution.py:153
  3.7 7.1 %collective-permute-start = (f32[27,4,1024]{2,1,0:T(4,128)}, f32[27,4,1024]{2,1,0:T(4,128)}, u32[]{:S(2)}, u32[]{:S(2)}) collective-permute-start(f32[27,4,1024]{2,1,0:T(4,128)} %dynamic-slice_bitcast_fusion.2), channel_id=1, source_target_pairs={{0,8},{8,0},{16,24},{24,16},{1,9},{9,1},{17,25},{25,17},{2,10},{10... | collective-permute-start | bytes 1327112 | tf_op jit(solution)/shard_map/ppermute | solution.py:153
  7.9 18.6 %collective-permute-start.3 = (f32[1,2,27,3072]{3,1,2,0:T(2,128)S(1)}, f32[1,2,27,3072]{3,1,2,0:T(2,128)S(1)}, u32[]{:S(2)}, u32[]{:S(2)}) collective-permute-start(f32[1,2,27,3072]{3,1,2,0:T(2,128)S(1)} %dynamic-slice_bitcast_fusion.1), channel_id=1, source_target_pairs={{0,16},{8,24},{16,0},{24,8},{1,17},{9,25},{17,1},{25,9},{2,18},{10... | collective-permute-start | bytes 1990664 | tf_op jit(solution)/shard_map/ppermute | solution.py:163
  12.5 18.3 %collective-permute-start.1 = (f32[1,2,27,1024]{3,1,2,0:T(2,128)S(1)}, f32[1,2,27,1024]{3,1,2,0:T(2,128)S(1)}, u32[]{:S(2)}, u32[]{:S(2)}) collective-permute-start(f32[1,2,27,1024]{3,1,2,0:T(2,128)S(1)} %dynamic-slice_bitcast_fusion.3), channel_id=1, source_target_pairs={{0,16},{8,24},{16,0},{24,8},{1,17},{9,25},{17,1},{25,9},{2,18},{10... | collective-permute-start | bytes 663560 | tf_op jit(solution)/shard_map/ppermute | solution.py:163
  27.9 20.6 %copy-start.1 = (f32[27,8192]{1,0:T(8,128)S(1)}, f32[27,8192]{1,0:T(8,128)}, u32[]{:S(2)}) copy-start(f32[27,8192]{1,0:T(8,128)} %param.9) | copy-start | bytes 2654212
  27.9 20.6 %copy-start.3 = (s32[64]{0:T(128)S(1)}, s32[64]{0:T(128)}, u32[]{:S(2)}) copy-start(s32[64]{0:T(128)} %constant.275) | copy-start | bytes 772
  27.9 20.6 %copy-start.4 = (s32[64]{0:T(128)S(1)}, s32[64]{0:T(128)}, u32[]{:S(2)}) copy-start(s32[64]{0:T(128)} %constant.254) | copy-start | bytes 772
  27.9 20.6 %copy-start.5 = (pred[64]{0:T(512)(128)(4,1)S(1)}, pred[64]{0:T(512)(128)(4,1)}, u32[]{:S(2)}) copy-start(pred[64]{0:T(512)(128)(4,1)} %constant.235.clone) | copy-start | bytes 196
  28.5 19.9 %collective-permute-start.5 = (f32[27,3072]{1,0:T(8,128)S(1)}, f32[27,3072]{1,0:T(8,128)}, u32[]{:S(2)}, u32[]{:S(2)}) collective-permute-start(f32[27,3072]{1,0:T(8,128)S(1)} %bitcast.63), channel_id=1, source_target_pairs={{0,8},{8,0},{16,24},{24,16},{1,9},{9,1},{17,25},{25,17},{2,10},{10... | collective-permute-start | bytes 995336 | tf_op jit(solution)/shard_map/ppermute | solution.py:168
  31.9 16.5 %collective-permute-start.4 = (f32[27,1024]{1,0:T(8,128)S(1)}, f32[27,1024]{1,0:T(8,128)S(1)}, u32[]{:S(2)}, u32[]{:S(2)}) collective-permute-start(f32[27,1024]{1,0:T(8,128)S(1)} %bitcast.65), channel_id=1, source_target_pairs={{0,8},{8,0},{16,24},{24,16},{1,9},{9,1},{17,25},{25,17},{2,10},{10... | collective-permute-start | bytes 331784 | tf_op jit(solution)/shard_map/ppermute | solution.py:168
  33.9 13.2 %all-to-all-start = ((f32[32,1,1]{2,1,0:T(1,128)}), f32[32,1,1]{2,1,0:T(1,128)S(1)}, u32[]{:S(2)}, u32[]{:S(2)}) async-start(f32[32,1,1]{2,1,0:T(1,128)} %broadcast_in_dim.8), calls=%async_computation | async-start | bytes 32768 | tf_op jit(solution)/shard_map/all_to_all | solution.py:180
  51.7 4.2 %copy-start.2 = (s32[32]{0:T(128)S(1)}, s32[32]{0:T(128)}, u32[]{:S(2)}) copy-start(s32[32]{0:T(128)} %constant.236.clone) | copy-start | bytes 388
  53.2 30.2 %all-to-all-start.1 = ((bf16[32,2,8192]{2,1,0:T(2,128)(2,1)}), bf16[32,2,8192]{2,1,0:T(2,128)(2,1)S(1)}, u32[]{:S(2)}, u32[]{:S(2)}) async-start(bf16[32,2,8192]{2,1,0:T(2,128)(2,1)} %reshape.96), calls=%async_computation.1 | async-start | bytes 2097152 | tf_op jit(solution)/shard_map/all_to_all | solution.py:203
  91.4 30.1 %copy-start = (f32[27,64]{1,0:T(8,128)S(1)}, f32[27,64]{1,0:T(8,128)}, u32[]{:S(2)}) copy-start(f32[27,64]{1,0:T(8,128)} %constant.237.clone) | copy-start | bytes 20740

commit v13 on v8

--- a/solution.py
+++ b/solution.py
@@ -162,7 +162,7 @@
             partner = [(i, i ^ (2 * width)) for i in range(devices_dp)]
             blocks = near + lax.ppermute(far, "dp", partner)
         blocks = blocks.reshape(2, TAPS, piece)
-        squares.append(jnp.sum(blocks * blocks))
+        squares.append(jnp.sum(lax.optimization_barrier(jnp.sum(blocks * blocks, axis=(0, 1)))))
         mine.append(lax.dynamic_index_in_dim(blocks, core, axis=0, keepdims=False))
         theirs.append(
             lax.ppermute(lax.dynamic_index_in_dim(blocks, 1 - core, axis=0, keepdims=False), "dp", pair)

time: 122 us -> 122 us (level)
    reduce_sum x2 -> x4, other arithmetic: 3.15 us -> 2.84 us  [the longest x2 1.63 us: reduce_over_dp(): jnp.sum(blocks * blocks, axis=(0, 1))]
where the time goes in v13:
time: 122 us
  waiting for transfers between devices  49.7 us (41%)
  blocking collectives  29.6 us (24%)
  starting transfers between devices  13 us (11%)
  local copies, waits for them, and re-layouts  11.5 us (9%)
  other arithmetic  8.16 us (7%)
  matrix products  6.13 us (5%)
  between operations  2.92 us (2%)
    all_to_all x1, blocking collectives, on_device(): returned = lax.all_to_all(back, AXES, 0, 0, tiled=True)  29.6 us
    all_to_all x1, waiting for transfers between devices, on_device(): whole = lax.all_to_all(sent, AXES, 0, 0, tiled=True)  26.3 us
    ppermute x2, waiting for transfers between devices, reduce_over_dp(): blocks = near + lax.ppermute(far, 'dp', partner)  16.1 us
    all_to_all x1, waiting for transfers between devices, total_over_devices(): gathered = lax.all_to_all(spread, AXES, 0, 0, tiled=True)  6.98 us
    all_to_all x1, starting transfers between devices, total_over_devices(): gathered = lax.all_to_all(spread, AXES, 0, 0, tiled=True)  6.08 us
    transpose x2, other arithmetic, reduce_over_dp(): blocks = (keep + lax.ppermute(send, 'dp', pair)).transpose(1, 0, 2)  3.13 us
    ppermute x2, starting transfers between devices, reduce_over_dp(): blocks = near + lax.ppermute(far, 'dp', partner)  2.96 us
    all_to_all x1, starting transfers between devices, on_device(): whole = lax.all_to_all(sent, AXES, 0, 0, tiled=True)  2.65 us
  transfers between devices with their start and end apart: 8, of which 5 were waited for; matrix products, arithmetic and copies ran while one was open for 9% of the time, Pallas kernels for 0%

profile of v13, /device:TPU:0, one launch (start us, length us, event | category | flops | bytes accessed | tf_op | source)
XLA Modules:
  0.0 122.0 jit_solution(15614636577202091014)
XLA Ops:
  0.0 1.1 dynamic-slice_bitcast_fusion.1
  1.1 0.5 collective-permute-start
  1.7 1.3 %dynamic-slice_bitcast_fusion = f32[27,4,2560]{2,1,0:T(4,128)S(1)} fusion(f32[1,27,4,8192]{3,2,1,0:T(4,128)} %param.8, s32[]{:T(128)S(6)} %select_n.143), kind=kLoop, calls=%fused_computation.48 | loop fusion | bytes 2211844 | tf_op jit(solution)/shard_map/dynamic_slice | solution.py:151
  3.0 0.1 collective-permute-start.2
  3.1 0.3 collective-permute-done
  3.4 1.3 %fusion.54 = f32[4,27,1536]{2,0,1:T(4,128)S(1)} fusion(f32[27,4,1536]{2,1,0:T(4,128)S(1)} %collective-permute-done, f32[1,27,4,8192]{3,2,1,0:T(4,128)} %param.8, s32[]{:T(128)S(6)} %select_n.136), kind=kLoop, calls=%fused_computation.67 | loop fusion | flops 165888 | bytes 1990660 | tf_op jit(solution)/shard_map/transpose | solution.py:153
  4.7 0.5 reshape_reshape.6
  5.2 0.8 dynamic-slice_bitcast_fusion.3
  5.9 2.9 %collective-permute-start.1 = (f32[1,2,27,1536]{3,1,2,0:T(2,128)}, f32[1,2,27,1536]{3,1,2,0:T(2,128)}, u32[]{:S(2)}, u32[]{:S(2)}) collective-permute-start(f32[1,2,27,1536]{3,1,2,0:T(2,128)} %dynamic-slice_bitcast_fusion.3), channel_id=1, source_target_pairs={{0,16},{8,24},{16,0},{24,8},{1,17},{9,25},{17,1},{25,9},{2,18},{10... | collective-permute-start | bytes 995336 | tf_op jit(solution)/shard_map/ppermute | solution.py:163
  8.8 0.0 collective-permute-done.2
  8.8 1.9 %fusion.37 = f32[4,27,2560]{2,0,1:T(4,128)S(1)} fusion(f32[27,4,2560]{2,1,0:T(4,128)} %collective-permute-done.2, f32[1,27,4,8192]{3,2,1,0:T(4,128)} %param.8, s32[]{:T(128)S(6)} %select_n.142), kind=kLoop, calls=%fused_computation.47 | loop fusion | flops 276480 | bytes 3317764 | tf_op jit(solution)/shard_map/transpose | solution.py:153
  10.7 0.9 reshape_reshape.7
  11.6 0.1 collective-permute-start.3
  11.7 6.0 %collective-permute-done.1 = f32[1,2,27,1536]{3,1,2,0:T(2,128)} collective-permute-done((f32[1,2,27,1536]{3,1,2,0:T(2,128)}, f32[1,2,27,1536]{3,1,2,0:T(2,128)}, u32[]{:S(2)}, u32[]{:S(2)}) %collective-permute-start.1) | collective-permute-done | bytes 331808 | tf_op jit(solution)/shard_map/ppermute | solution.py:163
  17.7 1.2 multiply_reduce_fusion.1
  18.9 10.1 %collective-permute-done.3 = f32[1,2,27,2560]{3,1,2,0:T(2,128)S(1)} collective-permute-done((f32[1,2,27,2560]{3,1,2,0:T(2,128)S(1)}, f32[1,2,27,2560]{3,1,2,0:T(2,128)S(1)}, u32[]{:S(2)}, u32[]{:S(2)}) %collective-permute-start.3) | collective-permute-done | bytes 552992 | tf_op jit(solution)/shard_map/ppermute | solution.py:163
  29.0 0.4 multiply_reduce_fusion
  29.4 0.0 copy-start.1
  29.4 0.0 copy-start.3
  29.4 0.0 copy-start.4
  29.4 0.0 copy-start.5
  29.5 0.5 constant_dynamic-slice_fusion.1
  30.0 0.1 collective-permute-start.5
  30.1 0.3 constant_dynamic-slice_fusion.2
  30.4 0.6 collective-permute-start.4
  31.0 0.6 reduce_sum.64
  31.6 0.6 reduce_sum.66
  33.4 0.6 broadcast_in_dim.8
  34.1 6.1 %all-to-all-start = ((f32[32,1,1]{2,1,0:T(1,128)}), f32[32,1,1]{2,1,0:T(1,128)S(1)}, u32[]{:S(2)}, u32[]{:S(2)}) async-start(f32[32,1,1]{2,1,0:T(1,128)} %broadcast_in_dim.8), calls=%async_computation | async-start | bytes 32768 | tf_op jit(solution)/shard_map/all_to_all | solution.py:180
  40.2 7.0 %all-to-all-done = f32[32,1,1]{2,1,0:T(1,128)S(1)} async-done(((f32[32,1,1]{2,1,0:T(1,128)}), f32[32,1,1]{2,1,0:T(1,128)S(1)}, u32[]{:S(2)}, u32[]{:S(2)}) %all-to-all-start) | async-done | bytes 160 | tf_op jit(solution)/shard_map/all_to_all | solution.py:180
  47.2 0.6 reduce_sum.67
  48.5 0.0 collective-permute-done.4
  48.5 0.0 collective-permute-done.5
  48.5 0.0 copy-done.1
  48.5 0.0 copy-done.3
  48.6 0.0 copy-done.4
  48.6 0.0 copy-done.5
  48.6 2.0 %convolution_convert_fusion.1 = bf16[64,8192]{1,0:T(8,128)(2,1)S(1)} fusion(f32[27,8192]{1,0:T(8,128)S(1)} %copy-done.1, f32[27,2560]{1,0:T(8,128)S(1)} %collective-permute-done.5, f32[27,1536]{1,0:T(8,128)S(1)} %collective-permute-done.4, f32[27,2560]{1,0:T(8,128)S(1)} %bitcast.64, f32[27,1536]{1,0:T(8,128)S(1)} %bitcast.66, f32[]{:T(128)S(6)} %min_shard_map.3, ...), kind=kOutput, calls=%fused_computation.43 | convolution fusion | flops 172418816 | bytes 2818845 | tf_op jit(solution)/shard_map/dot_general | solution.py:201
  50.6 0.0 copy-start.2
  50.6 1.5 %reshape.96 = bf16[32,2,8192]{2,1,0:T(2,128)(2,1)} reshape(bf16[64,8192]{1,0:T(8,128)(2,1)S(1)} %convolution_convert_fusion.1) | data formatting | bytes 2097152 | tf_op jit(solution)/shard_map/reshape | solution.py:202
  52.1 2.6 %all-to-all-start.1 = ((bf16[32,2,8192]{2,1,0:T(2,128)(2,1)}), bf16[32,2,8192]{2,1,0:T(2,128)(2,1)S(1)}, u32[]{:S(2)}, u32[]{:S(2)}) async-start(bf16[32,2,8192]{2,1,0:T(2,128)(2,1)} %reshape.96), calls=%async_computation.1 | async-start | bytes 2097152 | tf_op jit(solution)/shard_map/all_to_all | solution.py:203
  54.8 0.0 copy-done.2
  54.8 0.6 dynamic_slice.51
  56.0 26.3 %all-to-all-done.1 = bf16[32,2,8192]{2,1,0:T(2,128)(2,1)S(1)} async-done(((bf16[32,2,8192]{2,1,0:T(2,128)(2,1)}), bf16[32,2,8192]{2,1,0:T(2,128)(2,1)S(1)}, u32[]{:S(2)}, u32[]{:S(2)}) %all-to-all-start.1) | async-done | bytes 1048608 | tf_op jit(solution)/shard_map/all_to_all | solution.py:203
  82.4 0.6 copy.15
  83.0 0.5 reshape.97
  83.5 5.2 %conditional.1 = (bf16[2,512,512]{2,1,0:T(8,128)(2,1)S(1)}) conditional(s32[]{:T(128)} %bitcast.4, bf16[2,512,512]{2,1,0:T(8,128)(2,1)S(1)} %reshape.97, bf16[2,512,512]{2,1,0:T(8,128)(2,1)S(1)} %reshape.97), branch_computations={%region_5.7_spmd, %region_7.9_spmd} | conditional | flops 2175270912 | bytes 19398728 | solution.py:208
  83.7 1.1 fusion.6
  85.6 0.2 fusion.7
  85.8 0.1 slice_bitcast_fusion.3
  85.9 1.3 %fusion.24 = bf16[512,1024]{1,0:T(8,128)(2,1)S(1)} fusion(bf16[512,512]{1,0:T(8,128)(2,1)S(1)} %fusion.35, bf16[512,512]{1,0:T(8,128)(2,1)S(1)} %get-tuple-element.19, bf16[512,512]{1,0:T(8,128)(2,1)S(1)} %get-tuple-element.18), kind=kOutput, calls=%fused_computation.27 | convolution fusion | flops 1084751872 | bytes 2621440 | tf_op jit(solution)/shard_map/cond/branch_1_fun/dot_general | solution.py:102
  87.2 0.1 slice_negate_fusion
  87.2 1.3 %subtract_convert_fusion.1 = bf16[512,1024]{1,0:T(8,128)(2,1)S(1)} fusion(bf16[512,512]{1,0:T(8,128)(2,1)S(1)} %get-tuple-element.17, bf16[512,512]{1,0:T(8,128)(2,1)S(1)} %get-tuple-element.16, bf16[512,1024]{1,0:T(8,128)(2,1)S(1)} %fusion.24, bf16[512,512]{1,0:T(8,128)(2,1)S(1)} %get-tuple-element.19, bf16[512,512]{1,0:T(8,128)(2,1)S(1)} %get-tuple-element.18), kind=kOutput, calls=%fused_computation.26 | convolution fusion | flops 1086324736 | bytes 4194304 | tf_op jit(solution)/shard_map/cond/branch_1_fun/dot_general | solution.py:109
  88.5 0.1 slice_bitcast_fusion.1
  88.6 0.1 pad_maximum_fusion
  88.7 0.5 reshape.98
  89.3 1.1 copy.28
  90.4 0.0 copy-start
  90.4 29.6 %all_to_all.16 = bf16[32,2,8192]{2,1,0:T(2,128)(2,1)S(1)} all-to-all(bf16[32,2,8192]{2,1,0:T(2,128)(2,1)S(1)} %bitcast.62), channel_id=1, replica_groups=mesh['dp'=4,'freq'=8] {'dp','freq'}, dimensions={0} | all-to-all | bytes 2097152 | tf_op jit(solution)/shard_map/all_to_all | solution.py:211
  120.0 0.4 reshape.99
  120.4 0.0 copy-done
  120.4 1.5 %fusion.36 = f32[27,8192]{1,0:T(8,128)} fusion(bf16[64,8192]{1,0:T(8,128)(2,1)S(1)} %reshape.99, f32[27,64]{1,0:T(8,128)S(1)} %copy-done), kind=kOutput, calls=%fused_computation.45 | convolution fusion | flops 170090496 | bytes 1940224 | tf_op jit(solution)/shard_map/dot_general | solution.py:213
  (7 shorter events, 0.2 us)
Async XLA Ops:
  1.1 2.3 %collective-permute-start = (f32[27,4,1536]{2,1,0:T(4,128)S(1)}, f32[27,4,1536]{2,1,0:T(4,128)S(1)}, u32[]{:S(2)}, u32[]{:S(2)}) collective-permute-start(f32[27,4,1536]{2,1,0:T(4,128)S(1)} %dynamic-slice_bitcast_fusion.1), channel_id=1, source_target_pairs={{0,8},{8,0},{16,24},{24,16},{1,9},{9,1},{17,25},{25,17},{2,10},{10... | collective-permute-start | bytes 1990664 | tf_op jit(solution)/shard_map/ppermute | solution.py:153
  3.0 5.9 %collective-permute-start.2 = (f32[27,4,2560]{2,1,0:T(4,128)S(1)}, f32[27,4,2560]{2,1,0:T(4,128)}, u32[]{:S(2)}, u32[]{:S(2)}) collective-permute-start(f32[27,4,2560]{2,1,0:T(4,128)S(1)} %dynamic-slice_bitcast_fusion), channel_id=1, source_target_pairs={{0,8},{8,0},{16,24},{24,16},{1,9},{9,1},{17,25},{25,17},{2,10},{10... | collective-permute-start | bytes 3317768 | tf_op jit(solution)/shard_map/ppermute | solution.py:153
  5.9 11.8 %collective-permute-start.1 = (f32[1,2,27,1536]{3,1,2,0:T(2,128)}, f32[1,2,27,1536]{3,1,2,0:T(2,128)}, u32[]{:S(2)}, u32[]{:S(2)}) collective-permute-start(f32[1,2,27,1536]{3,1,2,0:T(2,128)} %dynamic-slice_bitcast_fusion.3), channel_id=1, source_target_pairs={{0,16},{8,24},{16,0},{24,8},{1,17},{9,25},{17,1},{25,9},{2,18},{10... | collective-permute-start | bytes 995336 | tf_op jit(solution)/shard_map/ppermute | solution.py:163
  11.6 17.4 %collective-permute-start.3 = (f32[1,2,27,2560]{3,1,2,0:T(2,128)S(1)}, f32[1,2,27,2560]{3,1,2,0:T(2,128)S(1)}, u32[]{:S(2)}, u32[]{:S(2)}) collective-permute-start(f32[1,2,27,2560]{3,1,2,0:T(2,128)S(1)} %dynamic-slice_bitcast_fusion.2), channel_id=1, source_target_pairs={{0,16},{8,24},{16,0},{24,8},{1,17},{9,25},{17,1},{25,9},{2,18},{10... | collective-permute-start | bytes 1658888 | tf_op jit(solution)/shard_map/ppermute | solution.py:163
  29.4 19.1 %copy-start.1 = (f32[27,8192]{1,0:T(8,128)S(1)}, f32[27,8192]{1,0:T(8,128)}, u32[]{:S(2)}) copy-start(f32[27,8192]{1,0:T(8,128)} %param.9) | copy-start | bytes 2654212
  29.4 19.1 %copy-start.3 = (s32[64]{0:T(128)S(1)}, s32[64]{0:T(128)}, u32[]{:S(2)}) copy-start(s32[64]{0:T(128)} %constant.277) | copy-start | bytes 772
  29.4 19.1 %copy-start.4 = (s32[64]{0:T(128)S(1)}, s32[64]{0:T(128)}, u32[]{:S(2)}) copy-start(s32[64]{0:T(128)} %constant.256) | copy-start | bytes 772
  29.4 19.1 %copy-start.5 = (pred[64]{0:T(512)(128)(4,1)S(1)}, pred[64]{0:T(512)(128)(4,1)}, u32[]{:S(2)}) copy-start(pred[64]{0:T(512)(128)(4,1)} %constant.237.clone) | copy-start | bytes 196
  30.0 18.5 %collective-permute-start.5 = (f32[27,2560]{1,0:T(8,128)S(1)}, f32[27,2560]{1,0:T(8,128)S(1)}, u32[]{:S(2)}, u32[]{:S(2)}) collective-permute-start(f32[27,2560]{1,0:T(8,128)S(1)} %bitcast.63), channel_id=1, source_target_pairs={{0,8},{8,0},{16,24},{24,16},{1,9},{9,1},{17,25},{25,17},{2,10},{10... | collective-permute-start | bytes 829448 | tf_op jit(solution)/shard_map/ppermute | solution.py:168
  30.4 18.1 %collective-permute-start.4 = (f32[27,1536]{1,0:T(8,128)S(1)}, f32[27,1536]{1,0:T(8,128)S(1)}, u32[]{:S(2)}, u32[]{:S(2)}) collective-permute-start(f32[27,1536]{1,0:T(8,128)S(1)} %bitcast.65), channel_id=1, source_target_pairs={{0,8},{8,0},{16,24},{24,16},{1,9},{9,1},{17,25},{25,17},{2,10},{10... | collective-permute-start | bytes 497672 | tf_op jit(solution)/shard_map/ppermute | solution.py:168
  34.1 13.1 %all-to-all-start = ((f32[32,1,1]{2,1,0:T(1,128)}), f32[32,1,1]{2,1,0:T(1,128)S(1)}, u32[]{:S(2)}, u32[]{:S(2)}) async-start(f32[32,1,1]{2,1,0:T(1,128)} %broadcast_in_dim.8), calls=%async_computation | async-start | bytes 32768 | tf_op jit(solution)/shard_map/all_to_all | solution.py:180
  50.6 4.2 %copy-start.2 = (s32[32]{0:T(128)S(1)}, s32[32]{0:T(128)}, u32[]{:S(2)}) copy-start(s32[32]{0:T(128)} %constant.238.clone) | copy-start | bytes 388
  52.1 30.2 %all-to-all-start.1 = ((bf16[32,2,8192]{2,1,0:T(2,128)(2,1)}), bf16[32,2,8192]{2,1,0:T(2,128)(2,1)S(1)}, u32[]{:S(2)}, u32[]{:S(2)}) async-start(bf16[32,2,8192]{2,1,0:T(2,128)(2,1)} %reshape.96), calls=%async_computation.1 | async-start | bytes 2097152 | tf_op jit(solution)/shard_map/all_to_all | solution.py:203
  90.4 30.1 %copy-start = (f32[27,64]{1,0:T(8,128)S(1)}, f32[27,64]{1,0:T(8,128)}, u32[]{:S(2)}) copy-start(f32[27,64]{1,0:T(8,128)} %constant.239.clone) | copy-start | bytes 20740

commit v14 on v8

--- a/solution.py
+++ b/solution.py
@@ -199,15 +199,16 @@
     cosine, sine = tap_phases(jnp.asarray(rows[:, 0]), stride)
     forward = jnp.where(jnp.asarray(rows[:, 1] == 0)[:, None], cosine, -sine)
     spectra = jnp.dot(forward, updated, precision=HIGH).astype(jnp.bfloat16)
-    sent = spectra.reshape(devices, 2, own_width)
+    rows_each = own_width // C
+    sent = spectra.reshape(devices, 2, rows_each, C)
     whole = lax.all_to_all(sent, AXES, 0, 0, tiled=True)
-    matrix = whole.transpose(1, 0, 2).reshape(2, C, C)
+    matrix = whole.transpose(1, 0, 2, 3).reshape(2, C, C)
 
     me = lax.axis_index(AXES)
     is_pair = jnp.asarray(kinds)[me] == 1
     polar_part = lax.cond(is_pair, polar_complex, polar_real, matrix)
 
-    back = polar_part.reshape(2, devices, own_width).transpose(1, 0, 2)
+    back = polar_part.reshape(2, devices, rows_each, C).transpose(1, 0, 2, 3)
     returned = lax.all_to_all(back, AXES, 0, 0, tiled=True)
     planes = returned.reshape(2 * devices, own_width).astype(jnp.float32)
     return jnp.dot(jnp.asarray(backward), planes, precision=HIGH) * scale_out

time: 122 us -> 119 us (0.975)
  local copies, waits for them, and re-layouts: 11.5 us -> 8.96 us
    reshape x5 -> x1, local copies, waits for them, and re-layouts: 4.05 us -> 0.09 us  [on_device(): back = polar_part.reshape(2, devices, rows_each, C).transpose(1, 0, 2, 3)]
    unnamed x16 -> x18, local copies, waits for them, and re-layouts: 0.12 us -> 2.05 us
where the time goes in v14:
time: 119 us
  waiting for transfers between devices  48.9 us (41%)
  blocking collectives  29.6 us (25%)
  starting transfers between devices  12.9 us (11%)
  local copies, waits for them, and re-layouts  8.96 us (8%)
  other arithmetic  8.47 us (7%)
  matrix products  6.13 us (5%)
  between operations  2.9 us (2%)
    all_to_all x1, blocking collectives, on_device(): returned = lax.all_to_all(back, AXES, 0, 0, tiled=True)  29.6 us
    all_to_all x1, waiting for transfers between devices, on_device(): whole = lax.all_to_all(sent, AXES, 0, 0, tiled=True)  26.3 us
    ppermute x2, waiting for transfers between devices, reduce_over_dp(): blocks = near + lax.ppermute(far, 'dp', partner)  15.3 us
    all_to_all x1, waiting for transfers between devices, total_over_devices(): gathered = lax.all_to_all(spread, AXES, 0, 0, tiled=True)  6.98 us
    all_to_all x1, starting transfers between devices, total_over_devices(): gathered = lax.all_to_all(spread, AXES, 0, 0, tiled=True)  6.07 us
    reduce_sum x2, other arithmetic, reduce_over_dp(): squares.append(jnp.sum(blocks * blocks))  3.15 us
    transpose x2, other arithmetic, reduce_over_dp(): blocks = (keep + lax.ppermute(send, 'dp', pair)).transpose(1, 0, 2)  3.13 us
    ppermute x2, starting transfers between devices, reduce_over_dp(): blocks = near + lax.ppermute(far, 'dp', partner)  2.96 us
  transfers between devices with their start and end apart: 8, of which 5 were waited for; matrix products, arithmetic and copies ran while one was open for 9% of the time, Pallas kernels for 0%

profile of v14, /device:TPU:0, one launch (start us, length us, event | category | flops | bytes accessed | tf_op | source)
XLA Modules:
  0.0 118.9 jit_solution(9486577909378484334)
XLA Ops:
  0.0 1.1 dynamic-slice_bitcast_fusion.1
  1.1 0.5 collective-permute-start
  1.7 1.3 %dynamic-slice_bitcast_fusion = f32[27,4,2560]{2,1,0:T(4,128)S(1)} fusion(f32[1,27,4,8192]{3,2,1,0:T(4,128)} %param.8, s32[]{:T(128)S(6)} %select_n.143), kind=kLoop, calls=%fused_computation.48 | loop fusion | bytes 2211844 | tf_op jit(solution)/shard_map/dynamic_slice | solution.py:151
  3.0 0.1 collective-permute-start.2
  3.1 0.3 collective-permute-done
  3.4 1.3 %fusion.54 = f32[4,27,1536]{2,0,1:T(4,128)S(1)} fusion(f32[27,4,1536]{2,1,0:T(4,128)S(1)} %collective-permute-done, f32[1,27,4,8192]{3,2,1,0:T(4,128)} %param.8, s32[]{:T(128)S(6)} %select_n.136), kind=kLoop, calls=%fused_computation.67 | loop fusion | flops 165888 | bytes 1990660 | tf_op jit(solution)/shard_map/transpose | solution.py:153
  4.7 0.5 reshape_reshape.6
  5.2 0.8 dynamic-slice_bitcast_fusion.3
  5.9 2.9 %collective-permute-start.1 = (f32[1,2,27,1536]{3,1,2,0:T(2,128)}, f32[1,2,27,1536]{3,1,2,0:T(2,128)}, u32[]{:S(2)}, u32[]{:S(2)}) collective-permute-start(f32[1,2,27,1536]{3,1,2,0:T(2,128)} %dynamic-slice_bitcast_fusion.3), channel_id=1, source_target_pairs={{0,16},{8,24},{16,0},{24,8},{1,17},{9,25},{17,1},{25,9},{2,18},{10... | collective-permute-start | bytes 995336 | tf_op jit(solution)/shard_map/ppermute | solution.py:163
  8.8 0.0 collective-permute-done.2
  8.8 1.9 %fusion.37 = f32[4,27,2560]{2,0,1:T(4,128)S(1)} fusion(f32[27,4,2560]{2,1,0:T(4,128)} %collective-permute-done.2, f32[1,27,4,8192]{3,2,1,0:T(4,128)} %param.8, s32[]{:T(128)S(6)} %select_n.142), kind=kLoop, calls=%fused_computation.47 | loop fusion | flops 276480 | bytes 3317764 | tf_op jit(solution)/shard_map/transpose | solution.py:153
  10.7 0.9 reshape_reshape.7
  11.6 0.1 collective-permute-start.3
  11.7 6.0 %collective-permute-done.1 = f32[1,2,27,1536]{3,1,2,0:T(2,128)} collective-permute-done((f32[1,2,27,1536]{3,1,2,0:T(2,128)}, f32[1,2,27,1536]{3,1,2,0:T(2,128)}, u32[]{:S(2)}, u32[]{:S(2)}) %collective-permute-start.1) | collective-permute-done | bytes 331808 | tf_op jit(solution)/shard_map/ppermute | solution.py:163
  17.7 2.0 %multiply_reduce_fusion.1 = (f32[]{:T(128)}, f32[1,2,27,1536]{3,1,2,0:T(2,128)S(1)}) fusion(f32[1,2,27,1536]{3,1,2,0:T(2,128)} %collective-permute-done.1, f32[2,1,2,27,1536]{4,2,0,3,1:T(2,128)S(1)} %reshape_reshape.6, s32[]{:T(128)S(6)} %select_n.140), kind=kLoop, calls=%fused_computation.75 | loop fusion | flops 248831 | bytes 995336 | tf_op jit(solution)/shard_map/reduce_sum | solution.py:165
  19.7 9.3 %collective-permute-done.3 = f32[1,2,27,2560]{3,1,2,0:T(2,128)S(1)} collective-permute-done((f32[1,2,27,2560]{3,1,2,0:T(2,128)S(1)}, f32[1,2,27,2560]{3,1,2,0:T(2,128)S(1)}, u32[]{:S(2)}, u32[]{:S(2)}) %collective-permute-start.3) | collective-permute-done | bytes 552992 | tf_op jit(solution)/shard_map/ppermute | solution.py:163
  29.0 1.2 %multiply_reduce_fusion = (f32[]{:T(128)}, f32[1,2,27,2560]{3,1,2,0:T(2,128)S(1)}) fusion(f32[1,2,27,2560]{3,1,2,0:T(2,128)S(1)} %collective-permute-done.3, f32[2,1,2,27,2560]{4,2,0,3,1:T(2,128)S(1)} %reshape_reshape.7, s32[]{:T(128)S(6)} %select_n.140), kind=kLoop, calls=%fused_computation.70 | loop fusion | flops 414719 | bytes 1658888 | tf_op jit(solution)/shard_map/reduce_sum | solution.py:165
  30.2 0.0 copy-start.1
  30.2 0.0 copy-start.3
  30.2 0.0 copy-start.4
  30.2 0.0 copy-start.5
  30.2 0.5 constant_dynamic-slice_fusion.1
  30.7 0.1 collective-permute-start.5
  30.8 0.3 constant_dynamic-slice_fusion.2
  31.1 0.6 collective-permute-start.4
  33.0 0.6 broadcast_in_dim.8
  33.6 6.1 %all-to-all-start = ((f32[32,1,1]{2,1,0:T(1,128)}), f32[32,1,1]{2,1,0:T(1,128)S(1)}, u32[]{:S(2)}, u32[]{:S(2)}) async-start(f32[32,1,1]{2,1,0:T(1,128)} %broadcast_in_dim.8), calls=%async_computation | async-start | bytes 32768 | tf_op jit(solution)/shard_map/all_to_all | solution.py:180
  39.7 7.0 %all-to-all-done = f32[32,1,1]{2,1,0:T(1,128)S(1)} async-done(((f32[32,1,1]{2,1,0:T(1,128)}), f32[32,1,1]{2,1,0:T(1,128)S(1)}, u32[]{:S(2)}, u32[]{:S(2)}) %all-to-all-start) | async-done | bytes 160 | tf_op jit(solution)/shard_map/all_to_all | solution.py:180
  46.7 0.6 reduce_sum.47
  48.0 0.0 collective-permute-done.4
  48.0 0.0 collective-permute-done.5
  48.1 0.0 copy-done.1
  48.1 0.0 copy-done.3
  48.1 0.0 copy-done.4
  48.1 0.0 copy-done.5
  48.1 2.0 %convolution_convert_fusion.1 = bf16[64,8192]{1,0:T(8,128)(2,1)S(1)} fusion(f32[27,8192]{1,0:T(8,128)S(1)} %copy-done.1, f32[27,2560]{1,0:T(8,128)S(1)} %collective-permute-done.5, f32[27,1536]{1,0:T(8,128)S(1)} %collective-permute-done.4, f32[27,2560]{1,0:T(8,128)S(1)} %bitcast.78, f32[27,1536]{1,0:T(8,128)S(1)} %bitcast.80, f32[]{:T(128)S(6)} %min_shard_map.3, ...), kind=kOutput, calls=%fused_computation.43 | convolution fusion | flops 172418816 | bytes 2818845 | tf_op jit(solution)/shard_map/dot_general | solution.py:201
  50.1 0.0 copy-start.2
  50.2 1.3 %copy.23 = bf16[8,8,16,512]{3,2,1,0:T(8,128)(2,1)} copy(bf16[8,8,16,512]{3,1,2,0:T(8,128)(2,1)S(1)} %bitcast.75) | data formatting | bytes 2097152
  51.5 2.6 %all-to-all-start.1 = ((bf16[32,2,16,512]{3,2,1,0:T(8,128)(2,1)}), bf16[32,2,16,512]{3,2,1,0:T(8,128)(2,1)S(1)}, u32[]{:S(2)}, u32[]{:S(2)}) async-start(bf16[32,2,16,512]{3,2,1,0:T(8,128)(2,1)} %bitcast.28), calls=%async_computation.1 | async-start | bytes 2097152 | tf_op jit(solution)/shard_map/all_to_all | solution.py:204
  54.1 0.0 copy-done.2
  54.2 0.6 dynamic_slice.51
  55.4 26.3 %all-to-all-done.1 = bf16[32,2,16,512]{3,2,1,0:T(8,128)(2,1)S(1)} async-done(((bf16[32,2,16,512]{3,2,1,0:T(8,128)(2,1)}), bf16[32,2,16,512]{3,2,1,0:T(8,128)(2,1)S(1)}, u32[]{:S(2)}, u32[]{:S(2)}) %all-to-all-start.1) | async-done | bytes 1048608 | tf_op jit(solution)/shard_map/all_to_all | solution.py:204
  81.7 0.1 copy.15
  81.8 5.2 %conditional.1 = (bf16[2,512,512]{2,1,0:T(8,128)(2,1)S(1)}) conditional(s32[]{:T(128)} %bitcast.4, bf16[2,512,512]{2,1,0:T(8,128)(2,1)S(1)} %bitcast.69, bf16[2,512,512]{2,1,0:T(8,128)(2,1)S(1)} %bitcast.70), branch_computations={%region_3.5_spmd, %region_5.7_spmd} | conditional | flops 2175270912 | bytes 19398728 | solution.py:209
  82.0 1.1 fusion.6
  83.9 0.2 fusion.7
  84.1 0.1 slice_bitcast_fusion.3
  84.2 1.3 %fusion.24 = bf16[512,1024]{1,0:T(8,128)(2,1)S(1)} fusion(bf16[512,512]{1,0:T(8,128)(2,1)S(1)} %fusion.35, bf16[512,512]{1,0:T(8,128)(2,1)S(1)} %get-tuple-element.19, bf16[512,512]{1,0:T(8,128)(2,1)S(1)} %get-tuple-element.18), kind=kOutput, calls=%fused_computation.27 | convolution fusion | flops 1084751872 | bytes 2621440 | tf_op jit(solution)/shard_map/cond/branch_1_fun/dot_general | solution.py:102
  85.5 0.1 slice_negate_fusion
  85.6 1.3 %subtract_convert_fusion.1 = bf16[512,1024]{1,0:T(8,128)(2,1)S(1)} fusion(bf16[512,512]{1,0:T(8,128)(2,1)S(1)} %get-tuple-element.17, bf16[512,512]{1,0:T(8,128)(2,1)S(1)} %get-tuple-element.16, bf16[512,1024]{1,0:T(8,128)(2,1)S(1)} %fusion.24, bf16[512,512]{1,0:T(8,128)(2,1)S(1)} %get-tuple-element.19, bf16[512,512]{1,0:T(8,128)(2,1)S(1)} %get-tuple-element.18), kind=kOutput, calls=%fused_computation.26 | convolution fusion | flops 1086324736 | bytes 4194304 | tf_op jit(solution)/shard_map/cond/branch_1_fun/dot_general | solution.py:109
  86.9 0.1 slice_bitcast_fusion.1
  86.9 0.1 pad_maximum_fusion
  87.0 0.1 copy.30
  87.1 0.0 copy-start
  87.1 29.6 %all_to_all.16 = bf16[32,2,16,512]{3,2,1,0:T(8,128)(2,1)S(1)} all-to-all(bf16[32,2,16,512]{3,2,1,0:T(8,128)(2,1)S(1)} %bitcast.73), channel_id=1, replica_groups=mesh['dp'=4,'freq'=8] {'dp','freq'}, dimensions={0} | all-to-all | bytes 2097152 | tf_op jit(solution)/shard_map/all_to_all | solution.py:212
  116.8 0.6 copy.24
  117.4 0.0 copy-done
  117.4 1.5 %fusion.36 = f32[27,8192]{1,0:T(8,128)} fusion(bf16[64,8192]{1,0:T(8,128)(2,1)S(1)} %bitcast.72, f32[27,64]{1,0:T(8,128)S(1)} %copy-done), kind=kOutput, calls=%fused_computation.45 | convolution fusion | flops 170090496 | bytes 1940224 | tf_op jit(solution)/shard_map/dot_general | solution.py:214
  (7 shorter events, 0.2 us)
Async XLA Ops:
  1.1 2.3 %collective-permute-start = (f32[27,4,1536]{2,1,0:T(4,128)S(1)}, f32[27,4,1536]{2,1,0:T(4,128)S(1)}, u32[]{:S(2)}, u32[]{:S(2)}) collective-permute-start(f32[27,4,1536]{2,1,0:T(4,128)S(1)} %dynamic-slice_bitcast_fusion.1), channel_id=1, source_target_pairs={{0,8},{8,0},{16,24},{24,16},{1,9},{9,1},{17,25},{25,17},{2,10},{10... | collective-permute-start | bytes 1990664 | tf_op jit(solution)/shard_map/ppermute | solution.py:153
  3.0 5.9 %collective-permute-start.2 = (f32[27,4,2560]{2,1,0:T(4,128)S(1)}, f32[27,4,2560]{2,1,0:T(4,128)}, u32[]{:S(2)}, u32[]{:S(2)}) collective-permute-start(f32[27,4,2560]{2,1,0:T(4,128)S(1)} %dynamic-slice_bitcast_fusion), channel_id=1, source_target_pairs={{0,8},{8,0},{16,24},{24,16},{1,9},{9,1},{17,25},{25,17},{2,10},{10... | collective-permute-start | bytes 3317768 | tf_op jit(solution)/shard_map/ppermute | solution.py:153
  5.9 11.8 %collective-permute-start.1 = (f32[1,2,27,1536]{3,1,2,0:T(2,128)}, f32[1,2,27,1536]{3,1,2,0:T(2,128)}, u32[]{:S(2)}, u32[]{:S(2)}) collective-permute-start(f32[1,2,27,1536]{3,1,2,0:T(2,128)} %dynamic-slice_bitcast_fusion.3), channel_id=1, source_target_pairs={{0,16},{8,24},{16,0},{24,8},{1,17},{9,25},{17,1},{25,9},{2,18},{10... | collective-permute-start | bytes 995336 | tf_op jit(solution)/shard_map/ppermute | solution.py:163
  11.6 17.4 %collective-permute-start.3 = (f32[1,2,27,2560]{3,1,2,0:T(2,128)S(1)}, f32[1,2,27,2560]{3,1,2,0:T(2,128)S(1)}, u32[]{:S(2)}, u32[]{:S(2)}) collective-permute-start(f32[1,2,27,2560]{3,1,2,0:T(2,128)S(1)} %dynamic-slice_bitcast_fusion.2), channel_id=1, source_target_pairs={{0,16},{8,24},{16,0},{24,8},{1,17},{9,25},{17,1},{25,9},{2,18},{10... | collective-permute-start | bytes 1658888 | tf_op jit(solution)/shard_map/ppermute | solution.py:163
  30.2 17.9 %copy-start.1 = (f32[27,8192]{1,0:T(8,128)S(1)}, f32[27,8192]{1,0:T(8,128)}, u32[]{:S(2)}) copy-start(f32[27,8192]{1,0:T(8,128)} %param.9) | copy-start | bytes 2654212
  30.2 17.9 %copy-start.3 = (s32[64]{0:T(128)S(1)}, s32[64]{0:T(128)}, u32[]{:S(2)}) copy-start(s32[64]{0:T(128)} %constant.277) | copy-start | bytes 772
  30.2 17.9 %copy-start.4 = (s32[64]{0:T(128)S(1)}, s32[64]{0:T(128)}, u32[]{:S(2)}) copy-start(s32[64]{0:T(128)} %constant.256) | copy-start | bytes 772
  30.2 17.9 %copy-start.5 = (pred[64]{0:T(512)(128)(4,1)S(1)}, pred[64]{0:T(512)(128)(4,1)}, u32[]{:S(2)}) copy-start(pred[64]{0:T(512)(128)(4,1)} %constant.237.clone) | copy-start | bytes 196
  30.7 17.3 %collective-permute-start.5 = (f32[27,2560]{1,0:T(8,128)S(1)}, f32[27,2560]{1,0:T(8,128)S(1)}, u32[]{:S(2)}, u32[]{:S(2)}) collective-permute-start(f32[27,2560]{1,0:T(8,128)S(1)} %bitcast.77), channel_id=1, source_target_pairs={{0,8},{8,0},{16,24},{24,16},{1,9},{9,1},{17,25},{25,17},{2,10},{10... | collective-permute-start | bytes 829448 | tf_op jit(solution)/shard_map/ppermute | solution.py:168
  31.1 16.9 %collective-permute-start.4 = (f32[27,1536]{1,0:T(8,128)S(1)}, f32[27,1536]{1,0:T(8,128)S(1)}, u32[]{:S(2)}, u32[]{:S(2)}) collective-permute-start(f32[27,1536]{1,0:T(8,128)S(1)} %bitcast.79), channel_id=1, source_target_pairs={{0,8},{8,0},{16,24},{24,16},{1,9},{9,1},{17,25},{25,17},{2,10},{10... | collective-permute-start | bytes 497672 | tf_op jit(solution)/shard_map/ppermute | solution.py:168
  33.6 13.1 %all-to-all-start = ((f32[32,1,1]{2,1,0:T(1,128)}), f32[32,1,1]{2,1,0:T(1,128)S(1)}, u32[]{:S(2)}, u32[]{:S(2)}) async-start(f32[32,1,1]{2,1,0:T(1,128)} %broadcast_in_dim.8), calls=%async_computation | async-start | bytes 32768 | tf_op jit(solution)/shard_map/all_to_all | solution.py:180
  50.1 4.0 %copy-start.2 = (s32[32]{0:T(128)S(1)}, s32[32]{0:T(128)}, u32[]{:S(2)}) copy-start(s32[32]{0:T(128)} %constant.238.clone) | copy-start | bytes 388
  51.5 30.2 %all-to-all-start.1 = ((bf16[32,2,16,512]{3,2,1,0:T(8,128)(2,1)}), bf16[32,2,16,512]{3,2,1,0:T(8,128)(2,1)S(1)}, u32[]{:S(2)}, u32[]{:S(2)}) async-start(bf16[32,2,16,512]{3,2,1,0:T(8,128)(2,1)} %bitcast.28), calls=%async_computation.1 | async-start | bytes 2097152 | tf_op jit(solution)/shard_map/all_to_all | solution.py:204
  87.1 30.3 %copy-start = (f32[27,64]{1,0:T(8,128)S(1)}, f32[27,64]{1,0:T(8,128)}, u32[]{:S(2)}) copy-start(f32[27,64]{1,0:T(8,128)} %constant.239.clone) | copy-start | bytes 20740

commit v15 on v14

--- a/solution.py
+++ b/solution.py
@@ -202,13 +202,18 @@
     rows_each = own_width // C
     sent = spectra.reshape(devices, 2, rows_each, C)
     whole = lax.all_to_all(sent, AXES, 0, 0, tiled=True)
-    matrix = whole.transpose(1, 0, 2, 3).reshape(2, C, C)
 
     me = lax.axis_index(AXES)
     is_pair = jnp.asarray(kinds)[me] == 1
-    polar_part = lax.cond(is_pair, polar_complex, polar_real, matrix)
-
-    back = polar_part.reshape(2, devices, rows_each, C).transpose(1, 0, 2, 3)
+
+    def in_blocks(polar):
+        def step(blocks):
+            matrix = blocks.transpose(1, 0, 2, 3).reshape(2, C, C)
+            return polar(matrix).reshape(2, devices, rows_each, C).transpose(1, 0, 2, 3)
+
+        return step
+
+    back = lax.cond(is_pair, in_blocks(polar_complex), in_blocks(polar_real), whole)
     returned = lax.all_to_all(back, AXES, 0, 0, tiled=True)
     planes = returned.reshape(2 * devices, own_width).astype(jnp.float32)
     return jnp.dot(jnp.asarray(backward), planes, precision=HIGH) * scale_out

time: 119 us -> 119 us (level)
  no operation moved by 1% of the time
where the time goes in v15:
time: 119 us
  waiting for transfers between devices  48.9 us (41%)
  blocking collectives  29.6 us (25%)
  starting transfers between devices  12.9 us (11%)
  local copies, waits for them, and re-layouts  8.89 us (7%)
  other arithmetic  8.55 us (7%)
  matrix products  6.13 us (5%)
  between operations  2.89 us (2%)
    all_to_all x1, blocking collectives, on_device(): returned = lax.all_to_all(back, AXES, 0, 0, tiled=True)  29.6 us
    all_to_all x1, waiting for transfers between devices, on_device(): whole = lax.all_to_all(sent, AXES, 0, 0, tiled=True)  26.3 us
    ppermute x2, waiting for transfers between devices, reduce_over_dp(): blocks = near + lax.ppermute(far, 'dp', partner)  15.3 us
    all_to_all x1, waiting for transfers between devices, total_over_devices(): gathered = lax.all_to_all(spread, AXES, 0, 0, tiled=True)  6.98 us
    all_to_all x1, starting transfers between devices, total_over_devices(): gathered = lax.all_to_all(spread, AXES, 0, 0, tiled=True)  6.07 us
    reduce_sum x2, other arithmetic, reduce_over_dp(): squares.append(jnp.sum(blocks * blocks))  3.15 us
    transpose x2, other arithmetic, reduce_over_dp(): blocks = (keep + lax.ppermute(send, 'dp', pair)).transpose(1, 0, 2)  3.13 us
    ppermute x2, starting transfers between devices, reduce_over_dp(): blocks = near + lax.ppermute(far, 'dp', partner)  2.96 us
  transfers between devices with their start and end apart: 8, of which 5 were waited for; matrix products, arithmetic and copies ran while one was open for 9% of the time, Pallas kernels for 0%

profile of v15, /device:TPU:0, one launch (start us, length us, event | category | flops | bytes accessed | tf_op | source)
XLA Modules:
  0.0 118.7 jit_solution(15838820223594154467)
XLA Ops:
  0.0 1.1 dynamic-slice_bitcast_fusion.1
  1.1 0.5 collective-permute-start
  1.7 1.3 %dynamic-slice_bitcast_fusion = f32[27,4,2560]{2,1,0:T(4,128)S(1)} fusion(f32[1,27,4,8192]{3,2,1,0:T(4,128)} %param.8, s32[]{:T(128)S(6)} %select_n.143), kind=kLoop, calls=%fused_computation.44 | loop fusion | bytes 2211844 | tf_op jit(solution)/shard_map/dynamic_slice | solution.py:151
  3.0 0.1 collective-permute-start.2
  3.1 0.3 collective-permute-done
  3.4 1.3 %fusion.49 = f32[4,27,1536]{2,0,1:T(4,128)S(1)} fusion(f32[27,4,1536]{2,1,0:T(4,128)S(1)} %collective-permute-done, f32[1,27,4,8192]{3,2,1,0:T(4,128)} %param.8, s32[]{:T(128)S(6)} %select_n.136), kind=kLoop, calls=%fused_computation.62 | loop fusion | flops 165888 | bytes 1990660 | tf_op jit(solution)/shard_map/transpose | solution.py:153
  4.7 0.5 reshape_reshape.6
  5.2 0.8 dynamic-slice_bitcast_fusion.3
  5.9 2.9 %collective-permute-start.1 = (f32[1,2,27,1536]{3,1,2,0:T(2,128)}, f32[1,2,27,1536]{3,1,2,0:T(2,128)}, u32[]{:S(2)}, u32[]{:S(2)}) collective-permute-start(f32[1,2,27,1536]{3,1,2,0:T(2,128)} %dynamic-slice_bitcast_fusion.3), channel_id=1, source_target_pairs={{0,16},{8,24},{16,0},{24,8},{1,17},{9,25},{17,1},{25,9},{2,18},{10... | collective-permute-start | bytes 995336 | tf_op jit(solution)/shard_map/ppermute | solution.py:163
  8.8 0.0 collective-permute-done.2
  8.8 1.9 %fusion.32 = f32[4,27,2560]{2,0,1:T(4,128)S(1)} fusion(f32[27,4,2560]{2,1,0:T(4,128)} %collective-permute-done.2, f32[1,27,4,8192]{3,2,1,0:T(4,128)} %param.8, s32[]{:T(128)S(6)} %select_n.142), kind=kLoop, calls=%fused_computation.43 | loop fusion | flops 276480 | bytes 3317764 | tf_op jit(solution)/shard_map/transpose | solution.py:153
  10.7 0.9 reshape_reshape.7
  11.6 0.1 collective-permute-start.3
  11.7 6.0 %collective-permute-done.1 = f32[1,2,27,1536]{3,1,2,0:T(2,128)} collective-permute-done((f32[1,2,27,1536]{3,1,2,0:T(2,128)}, f32[1,2,27,1536]{3,1,2,0:T(2,128)}, u32[]{:S(2)}, u32[]{:S(2)}) %collective-permute-start.1) | collective-permute-done | bytes 331808 | tf_op jit(solution)/shard_map/ppermute | solution.py:163
  17.7 2.0 %multiply_reduce_fusion.2 = (f32[]{:T(128)}, f32[1,2,27,1536]{3,1,2,0:T(2,128)S(1)}) fusion(f32[1,2,27,1536]{3,1,2,0:T(2,128)} %collective-permute-done.1, f32[2,1,2,27,1536]{4,2,0,3,1:T(2,128)S(1)} %reshape_reshape.6, s32[]{:T(128)S(6)} %select_n.140), kind=kLoop, calls=%fused_computation.70 | loop fusion | flops 248831 | bytes 995336 | tf_op jit(solution)/shard_map/reduce_sum | solution.py:165
  19.7 9.3 %collective-permute-done.3 = f32[1,2,27,2560]{3,1,2,0:T(2,128)S(1)} collective-permute-done((f32[1,2,27,2560]{3,1,2,0:T(2,128)S(1)}, f32[1,2,27,2560]{3,1,2,0:T(2,128)S(1)}, u32[]{:S(2)}, u32[]{:S(2)}) %collective-permute-start.3) | collective-permute-done | bytes 552992 | tf_op jit(solution)/shard_map/ppermute | solution.py:163
  29.0 1.2 %multiply_reduce_fusion.1 = (f32[]{:T(128)}, f32[1,2,27,2560]{3,1,2,0:T(2,128)S(1)}) fusion(f32[1,2,27,2560]{3,1,2,0:T(2,128)S(1)} %collective-permute-done.3, f32[2,1,2,27,2560]{4,2,0,3,1:T(2,128)S(1)} %reshape_reshape.7, s32[]{:T(128)S(6)} %select_n.140), kind=kLoop, calls=%fused_computation.65 | loop fusion | flops 414719 | bytes 1658888 | tf_op jit(solution)/shard_map/reduce_sum | solution.py:165
  30.2 0.0 copy-start.1
  30.2 0.0 copy-start.3
  30.2 0.0 copy-start.4
  30.2 0.0 copy-start.5
  30.2 0.5 constant_dynamic-slice_fusion.1
  30.7 0.1 collective-permute-start.5
  30.8 0.3 constant_dynamic-slice_fusion.2
  31.1 0.6 collective-permute-start.4
  33.0 0.6 broadcast_in_dim.8
  33.6 6.1 %all-to-all-start = ((f32[32,1,1]{2,1,0:T(1,128)}), f32[32,1,1]{2,1,0:T(1,128)S(1)}, u32[]{:S(2)}, u32[]{:S(2)}) async-start(f32[32,1,1]{2,1,0:T(1,128)} %broadcast_in_dim.8), calls=%async_computation | async-start | bytes 32768 | tf_op jit(solution)/shard_map/all_to_all | solution.py:180
  39.7 7.0 %all-to-all-done = f32[32,1,1]{2,1,0:T(1,128)S(1)} async-done(((f32[32,1,1]{2,1,0:T(1,128)}), f32[32,1,1]{2,1,0:T(1,128)S(1)}, u32[]{:S(2)}, u32[]{:S(2)}) %all-to-all-start) | async-done | bytes 160 | tf_op jit(solution)/shard_map/all_to_all | solution.py:180
  46.7 0.6 reduce_sum.47
  48.0 0.0 collective-permute-done.4
  48.0 0.0 collective-permute-done.5
  48.1 0.0 copy-done.1
  48.1 0.0 copy-done.3
  48.1 0.0 copy-done.4
  48.1 0.0 copy-done.5
  48.1 2.0 %convolution_convert_fusion.1 = bf16[64,8192]{1,0:T(8,128)(2,1)S(1)} fusion(f32[27,8192]{1,0:T(8,128)S(1)} %copy-done.1, f32[27,2560]{1,0:T(8,128)S(1)} %collective-permute-done.5, f32[27,1536]{1,0:T(8,128)S(1)} %collective-permute-done.4, f32[27,2560]{1,0:T(8,128)S(1)} %bitcast.85, f32[27,1536]{1,0:T(8,128)S(1)} %bitcast.87, f32[]{:T(128)S(6)} %min_shard_map.3, ...), kind=kOutput, calls=%fused_computation.39 | convolution fusion | flops 172418816 | bytes 2818845 | tf_op jit(solution)/shard_map/dot_general | solution.py:201
  50.1 0.0 copy-start.2
  50.2 1.3 %copy.29 = bf16[8,8,16,512]{3,2,1,0:T(8,128)(2,1)} copy(bf16[8,8,16,512]{3,1,2,0:T(8,128)(2,1)S(1)} %bitcast.80) | data formatting | bytes 2097152
  51.5 2.6 %all-to-all-start.1 = ((bf16[32,2,16,512]{3,2,1,0:T(8,128)(2,1)}), bf16[32,2,16,512]{3,2,1,0:T(8,128)(2,1)S(1)}, u32[]{:S(2)}, u32[]{:S(2)}) async-start(bf16[32,2,16,512]{3,2,1,0:T(8,128)(2,1)} %bitcast.32), calls=%async_computation.1 | async-start | bytes 2097152 | tf_op jit(solution)/shard_map/all_to_all | solution.py:204
  54.1 0.0 copy-done.2
  54.2 0.6 dynamic_slice.51
  55.4 26.3 %all-to-all-done.1 = bf16[32,2,16,512]{3,2,1,0:T(8,128)(2,1)S(1)} async-done(((bf16[32,2,16,512]{3,2,1,0:T(8,128)(2,1)}), bf16[32,2,16,512]{3,2,1,0:T(8,128)(2,1)S(1)}, u32[]{:S(2)}, u32[]{:S(2)}) %all-to-all-start.1) | async-done | bytes 1048608 | tf_op jit(solution)/shard_map/all_to_all | solution.py:204
  81.7 5.1 %conditional.1 = (bf16[32,2,16,512]{3,2,0,1:T(8,128)(2,1)S(1)}) conditional(s32[]{:T(128)} %bitcast.10, bf16[32,2,16,512]{3,2,1,0:T(8,128)(2,1)S(1)} %all-to-all-done.1, bf16[32,2,16,512]{3,2,1,0:T(8,128)(2,1)S(1)} %all-to-all-done.1), branch_computations={%region_3.5_spmd, %region_5.7_spmd} | conditional | flops 2175270912 | bytes 19398728 | solution.py:216
  81.7 1.1 fusion.1
  83.6 0.2 fusion.22
  83.8 0.1 fusion.85
  83.9 0.1 bitcast_negate_fusion
  84.0 1.3 %fusion.19 = bf16[512,1024]{1,0:T(8,128)(2,1)S(1)} fusion(bf16[512,512]{1,0:T(8,128)(2,1)S(1)} %bitcast_negate_fusion, bf16[512,512]{1,0:T(8,128)(2,1)S(1)} %bitcast.82, bf16[512,512]{1,0:T(8,128)(2,1)S(1)} %bitcast.76), kind=kOutput, calls=%fused_computation.26 | convolution fusion | flops 1084751872 | bytes 2621440 | tf_op jit(solution)/shard_map/cond/branch_1_fun/dot_general | solution.py:102
  85.3 0.1 slice_negate_fusion
  85.3 1.3 %subtract_convert_fusion.1 = bf16[512,1024]{1,0:T(8,128)(2,1)S(1)} fusion(bf16[512,512]{1,0:T(8,128)(2,1)S(1)} %get-tuple-element.17, bf16[512,512]{1,0:T(8,128)(2,1)S(1)} %get-tuple-element.16, bf16[512,1024]{1,0:T(8,128)(2,1)S(1)} %fusion.19, bf16[512,512]{1,0:T(8,128)(2,1)S(1)} %bitcast.83, bf16[512,512]{1,0:T(8,128)(2,1)S(1)} %bitcast.77), kind=kOutput, calls=%fused_computation.25 | convolution fusion | flops 1086324736 | bytes 4194304 | tf_op jit(solution)/shard_map/cond/branch_1_fun/dot_general | solution.py:109
  86.6 0.1 fusion.84
  86.7 0.1 maximum_bitcast_fusion
  86.8 0.1 copy.22
  86.9 0.0 copy-start
  86.9 29.6 %all_to_all.22 = bf16[32,2,16,512]{3,2,1,0:T(8,128)(2,1)S(1)} all-to-all(bf16[32,2,16,512]{3,2,1,0:T(8,128)(2,1)S(1)} %copy.22), channel_id=1, replica_groups=mesh['dp'=4,'freq'=8] {'dp','freq'}, dimensions={0} | all-to-all | bytes 2097152 | tf_op jit(solution)/shard_map/all_to_all | solution.py:217
  116.6 0.6 copy.30
  117.2 0.0 copy-done
  117.2 1.5 %fusion.31 = f32[27,8192]{1,0:T(8,128)} fusion(bf16[64,8192]{1,0:T(8,128)(2,1)S(1)} %bitcast.74, f32[27,64]{1,0:T(8,128)S(1)} %copy-done), kind=kOutput, calls=%fused_computation.41 | convolution fusion | flops 170090496 | bytes 1940224 | tf_op jit(solution)/shard_map/dot_general | solution.py:219
  (6 shorter events, 0.2 us)
Async XLA Ops:
  1.1 2.3 %collective-permute-start = (f32[27,4,1536]{2,1,0:T(4,128)S(1)}, f32[27,4,1536]{2,1,0:T(4,128)S(1)}, u32[]{:S(2)}, u32[]{:S(2)}) collective-permute-start(f32[27,4,1536]{2,1,0:T(4,128)S(1)} %dynamic-slice_bitcast_fusion.1), channel_id=1, source_target_pairs={{0,8},{8,0},{16,24},{24,16},{1,9},{9,1},{17,25},{25,17},{2,10},{10... | collective-permute-start | bytes 1990664 | tf_op jit(solution)/shard_map/ppermute | solution.py:153
  3.0 5.9 %collective-permute-start.2 = (f32[27,4,2560]{2,1,0:T(4,128)S(1)}, f32[27,4,2560]{2,1,0:T(4,128)}, u32[]{:S(2)}, u32[]{:S(2)}) collective-permute-start(f32[27,4,2560]{2,1,0:T(4,128)S(1)} %dynamic-slice_bitcast_fusion), channel_id=1, source_target_pairs={{0,8},{8,0},{16,24},{24,16},{1,9},{9,1},{17,25},{25,17},{2,10},{10... | collective-permute-start | bytes 3317768 | tf_op jit(solution)/shard_map/ppermute | solution.py:153
  5.9 11.8 %collective-permute-start.1 = (f32[1,2,27,1536]{3,1,2,0:T(2,128)}, f32[1,2,27,1536]{3,1,2,0:T(2,128)}, u32[]{:S(2)}, u32[]{:S(2)}) collective-permute-start(f32[1,2,27,1536]{3,1,2,0:T(2,128)} %dynamic-slice_bitcast_fusion.3), channel_id=1, source_target_pairs={{0,16},{8,24},{16,0},{24,8},{1,17},{9,25},{17,1},{25,9},{2,18},{10... | collective-permute-start | bytes 995336 | tf_op jit(solution)/shard_map/ppermute | solution.py:163
  11.6 17.4 %collective-permute-start.3 = (f32[1,2,27,2560]{3,1,2,0:T(2,128)S(1)}, f32[1,2,27,2560]{3,1,2,0:T(2,128)S(1)}, u32[]{:S(2)}, u32[]{:S(2)}) collective-permute-start(f32[1,2,27,2560]{3,1,2,0:T(2,128)S(1)} %dynamic-slice_bitcast_fusion.2), channel_id=1, source_target_pairs={{0,16},{8,24},{16,0},{24,8},{1,17},{9,25},{17,1},{25,9},{2,18},{10... | collective-permute-start | bytes 1658888 | tf_op jit(solution)/shard_map/ppermute | solution.py:163
  30.2 17.9 %copy-start.1 = (f32[27,8192]{1,0:T(8,128)S(1)}, f32[27,8192]{1,0:T(8,128)}, u32[]{:S(2)}) copy-start(f32[27,8192]{1,0:T(8,128)} %param.9) | copy-start | bytes 2654212
  30.2 17.9 %copy-start.3 = (s32[64]{0:T(128)S(1)}, s32[64]{0:T(128)}, u32[]{:S(2)}) copy-start(s32[64]{0:T(128)} %constant.277) | copy-start | bytes 772
  30.2 17.9 %copy-start.4 = (s32[64]{0:T(128)S(1)}, s32[64]{0:T(128)}, u32[]{:S(2)}) copy-start(s32[64]{0:T(128)} %constant.256) | copy-start | bytes 772
  30.2 17.9 %copy-start.5 = (pred[64]{0:T(512)(128)(4,1)S(1)}, pred[64]{0:T(512)(128)(4,1)}, u32[]{:S(2)}) copy-start(pred[64]{0:T(512)(128)(4,1)} %constant.237.clone) | copy-start | bytes 196
  30.7 17.3 %collective-permute-start.5 = (f32[27,2560]{1,0:T(8,128)S(1)}, f32[27,2560]{1,0:T(8,128)S(1)}, u32[]{:S(2)}, u32[]{:S(2)}) collective-permute-start(f32[27,2560]{1,0:T(8,128)S(1)} %bitcast.84), channel_id=1, source_target_pairs={{0,8},{8,0},{16,24},{24,16},{1,9},{9,1},{17,25},{25,17},{2,10},{10... | collective-permute-start | bytes 829448 | tf_op jit(solution)/shard_map/ppermute | solution.py:168
  31.1 16.9 %collective-permute-start.4 = (f32[27,1536]{1,0:T(8,128)S(1)}, f32[27,1536]{1,0:T(8,128)S(1)}, u32[]{:S(2)}, u32[]{:S(2)}) collective-permute-start(f32[27,1536]{1,0:T(8,128)S(1)} %bitcast.86), channel_id=1, source_target_pairs={{0,8},{8,0},{16,24},{24,16},{1,9},{9,1},{17,25},{25,17},{2,10},{10... | collective-permute-start | bytes 497672 | tf_op jit(solution)/shard_map/ppermute | solution.py:168
  33.6 13.1 %all-to-all-start = ((f32[32,1,1]{2,1,0:T(1,128)}), f32[32,1,1]{2,1,0:T(1,128)S(1)}, u32[]{:S(2)}, u32[]{:S(2)}) async-start(f32[32,1,1]{2,1,0:T(1,128)} %broadcast_in_dim.8), calls=%async_computation | async-start | bytes 32768 | tf_op jit(solution)/shard_map/all_to_all | solution.py:180
  50.1 4.0 %copy-start.2 = (s32[32]{0:T(128)S(1)}, s32[32]{0:T(128)}, u32[]{:S(2)}) copy-start(s32[32]{0:T(128)} %constant.238.clone) | copy-start | bytes 388
  51.5 30.2 %all-to-all-start.1 = ((bf16[32,2,16,512]{3,2,1,0:T(8,128)(2,1)}), bf16[32,2,16,512]{3,2,1,0:T(8,128)(2,1)S(1)}, u32[]{:S(2)}, u32[]{:S(2)}) async-start(bf16[32,2,16,512]{3,2,1,0:T(8,128)(2,1)} %bitcast.32), calls=%async_computation.1 | async-start | bytes 2097152 | tf_op jit(solution)/shard_map/all_to_all | solution.py:204
  86.9 30.3 %copy-start = (f32[27,64]{1,0:T(8,128)S(1)}, f32[27,64]{1,0:T(8,128)}, u32[]{:S(2)}) copy-start(f32[27,64]{1,0:T(8,128)} %constant.239.clone) | copy-start | bytes 20740
